TPU v7x, 512 devices: a whole 4x4x16 slice. The times are simulated.
512 devices in a mesh: seq: 32 (over z, core), tensor: 16 (over y, x).
Axes of the slice: x: 4, y: 4, z: 16, core: 2. Of those that a mesh axis runs over, the one named last changes fastest.
Arguments:
- hidden: bfloat16 [4, 64, 5120], P(None, None, 'seq'), may hold values from -400 to 400
- norm_gain: bfloat16 [5120], P('seq'), may hold values from 0.099609375 to 1.8984375
- w_qkv: bfloat16 [5120, 7168], P('seq', 'tensor'), may hold values from -0.078125 to 0.078125
- b_qkv: bfloat16 [7168], P('tensor'), may hold values from -3 to 3
- w_out: bfloat16 [5120, 5120], P('tensor', 'seq'), may hold values from -0.078125 to 0.078125
- prefix_key_cache: bfloat16 [16, 12288, 1024], P('tensor', 'seq'), may hold values from -140 to 140
- prefix_value_cache: bfloat16 [16, 12288, 1024], P('tensor', 'seq'), may hold values from -6 to 6
- suffix_key_cache: bfloat16 [64, 4096, 1024], P('tensor', 'seq'), may hold values from -8 to 8
- suffix_value_cache: bfloat16 [64, 4096, 1024], P('tensor', 'seq'), may hold values from -6 to 6
- prefix_lens: int32 [16], P('tensor'), may hold values from 1 to 12288, as said below
- suffix_lens: int32 [64], P('tensor'), may hold values from 0 to 4096, as said below
Outputs:
- attn_out: float32 [4, 64, 5120], P(None, 'tensor', 'seq')
- new_keys: float32 [64, 4, 1024], P('tensor')
- new_values: float32 [64, 4, 1024], P('tensor')
Inputs may be any that keep to these rules, and one draw needn't show every extreme that they name: `prefix_lens`: some group has exactly 12288 live slots and some exactly one. `suffix_lens`: some request has exactly 4096 live slots and some none.
All inputs are finite; a program needn't handle non-finite values.
Results may differ from a plain program's by a relative error of at most 0.012.
The roundings to bfloat16 on the way count: a program that leaves them out, or rounds other values in their place, can miss the bound.
Values may be sent and summed in bfloat16 or wider, within the bound.
No kernel may reach another device: no remote copies, remote signals or barrier semaphores. Data moves between devices by JAX's collectives and lax.ppermute only.
A program may use at most 64 MiB of HBM per device.

v0:
```python
import jax
import jax.numpy as jnp
from jax import lax
from jax.sharding import PartitionSpec as P

D = 5120
QUERY_HEADS = 40
KEY_HEADS = 8
HEAD_SIZE = 128
KEY_COLUMNS = 1024


epsilon = 1e-06
masked_fill = -1e30


def apply_rotary(values, token_positions):
    half = values.shape[-1] // 2
    freq = jnp.exp(
        -(jnp.arange(half, dtype=jnp.float32) * (2.0 / values.shape[-1]))
        * jnp.log(jnp.float32(1000000.0))
    )
    angles = token_positions[..., None, None] * freq
    cosine = jnp.cos(angles)
    sine = jnp.sin(angles)
    left = values[..., :half]
    right = values[..., half:]
    return jnp.concatenate([left * cosine - right * sine, right * cosine + left * sine], axis=-1)


def body(
    hidden,
    norm_gain,
    w_qkv,
    b_qkv,
    w_out,
    prefix_key_cache,
    prefix_value_cache,
    suffix_key_cache,
    suffix_value_cache,
    prefix_lens,
    suffix_lens,
):
    decode_step_count = hidden.shape[0]
    request_count = suffix_lens.shape[0]
    prefix_count = prefix_key_cache.shape[1]
    suffix_count = suffix_key_cache.shape[1]
    query_group_width = QUERY_HEADS // KEY_HEADS
    query_width = QUERY_HEADS * HEAD_SIZE
    query_rows = decode_step_count * query_group_width
    scale = float(HEAD_SIZE) ** (-0.5)
    seq_index = lax.axis_index("seq")
    xf = hidden.astype(jnp.float32)
    squares = lax.psum(jnp.sum(xf * xf, axis=2), "seq")
    normed = (
        xf * lax.rsqrt(squares / D + epsilon)[..., None] * norm_gain.astype(jnp.float32)
    ).astype(jnp.bfloat16)
    partial_value = jnp.einsum("sbd,dc->sbc", normed, w_qkv, preferred_element_type=jnp.float32)
    bias = b_qkv.astype(jnp.float32)
    summed_cols = lax.psum(partial_value, "seq") + bias
    combined_output = lax.all_to_all(summed_cols, "tensor", split_axis=1, concat_axis=2, tiled=True)
    token_positions = (
        (prefix_lens[0] + suffix_lens)[None, :]
        + jnp.arange(decode_step_count, dtype=jnp.int32)[:, None]
    ).astype(jnp.float32)
    query_matrix = apply_rotary(
        combined_output[..., :query_width].reshape(
            decode_step_count, request_count, QUERY_HEADS, HEAD_SIZE
        ),
        token_positions,
    ).astype(jnp.bfloat16)
    keys_float = apply_rotary(
        combined_output[..., query_width : query_width + KEY_COLUMNS].reshape(
            decode_step_count, request_count, KEY_HEADS, HEAD_SIZE
        ),
        token_positions,
    )
    values_float = combined_output[..., query_width + KEY_COLUMNS :].reshape(
        decode_step_count, request_count, KEY_HEADS, HEAD_SIZE
    )
    current_keys = keys_float.astype(jnp.bfloat16)
    current_values = values_float.astype(jnp.bfloat16)
    new_keys = keys_float.reshape(decode_step_count, request_count, KEY_COLUMNS).transpose(1, 0, 2)
    new_values = values_float.reshape(decode_step_count, request_count, KEY_COLUMNS).transpose(
        1, 0, 2
    )
    query_by_group = (
        query_matrix.reshape(
            decode_step_count, request_count, KEY_HEADS, query_group_width, HEAD_SIZE
        )
        .transpose(1, 2, 0, 3, 4)
        .reshape(request_count, KEY_HEADS, query_rows, HEAD_SIZE)
    )
    prefix_key_block = prefix_key_cache[0].reshape(prefix_count, KEY_HEADS, HEAD_SIZE)
    prefix_value_block = prefix_value_cache[0].reshape(prefix_count, KEY_HEADS, HEAD_SIZE)
    suffix_key_block = suffix_key_cache.reshape(request_count, suffix_count, KEY_HEADS, HEAD_SIZE)
    suffix_value_block = suffix_value_cache.reshape(
        request_count, suffix_count, KEY_HEADS, HEAD_SIZE
    )
    score_pre = (
        jnp.einsum(
            "rhqd,phd->rhqp", query_by_group, prefix_key_block, preferred_element_type=jnp.float32
        )
        * scale
    )
    score_suf = (
        jnp.einsum(
            "rhqd,rshd->rhqs", query_by_group, suffix_key_block, preferred_element_type=jnp.float32
        )
        * scale
    )
    pre_mask = (
        seq_index * prefix_count + jnp.arange(prefix_count, dtype=jnp.int32) < prefix_lens[0]
    )[None, None, None, :]
    suf_mask = (
        (seq_index * suffix_count + jnp.arange(suffix_count, dtype=jnp.int32))[None, :]
        < suffix_lens[:, None]
    )[:, None, None, :]
    fill_pre = jnp.where(pre_mask, score_pre, masked_fill)
    fill_suf = jnp.where(suf_mask, score_suf, masked_fill)
    local_max = jnp.maximum(jnp.max(fill_pre, axis=3), jnp.max(fill_suf, axis=3))
    prob_pre = jnp.where(pre_mask, jnp.exp(fill_pre - local_max[..., None]), 0.0)
    prob_suf = jnp.where(suf_mask, jnp.exp(fill_suf - local_max[..., None]), 0.0)
    local_weight = jnp.sum(prob_pre, axis=3) + jnp.sum(prob_suf, axis=3)
    local_acc = jnp.einsum(
        "rhqp,phd->rhqd",
        prob_pre.astype(jnp.bfloat16),
        prefix_value_block,
        preferred_element_type=jnp.float32,
    )
    local_acc = local_acc + jnp.einsum(
        "rhqs,rshd->rhqd",
        prob_suf.astype(jnp.bfloat16),
        suffix_value_block,
        preferred_element_type=jnp.float32,
    )
    global_max = lax.pmax(local_max, "seq")
    factor = jnp.exp(local_max - global_max)
    global_weight, global_acc = lax.psum(
        (local_weight * factor, local_acc * factor[..., None]), "seq"
    )
    fresh_k = current_keys.transpose(1, 2, 0, 3)
    fresh_v = current_values.transpose(1, 2, 0, 3)
    score_new = (
        jnp.einsum("rhqd,rhid->rhqi", query_by_group, fresh_k, preferred_element_type=jnp.float32)
        * scale
    )
    new_mask = (
        (jnp.arange(query_rows, dtype=jnp.int32) // query_group_width)[:, None]
        >= jnp.arange(decode_step_count, dtype=jnp.int32)[None, :]
    )[None, None]
    fill_new = jnp.where(new_mask, score_new, masked_fill)
    new_max = jnp.max(fill_new, axis=3)
    prob_new = jnp.where(new_mask, jnp.exp(fill_new - new_max[..., None]), 0.0)
    top = jnp.maximum(global_max, new_max)
    factor_old = jnp.exp(global_max - top)
    factor_new = jnp.exp(new_max - top)
    total = global_weight * factor_old + jnp.sum(prob_new, axis=3) * factor_new
    new_acc = jnp.einsum(
        "rhqi,rhid->rhqd",
        prob_new.astype(jnp.bfloat16),
        fresh_v,
        preferred_element_type=jnp.float32,
    )
    summed = global_acc * factor_old[..., None] + new_acc * factor_new[..., None]
    attention_output = (summed / total[..., None]).astype(jnp.bfloat16)
    heads_local = (
        attention_output.reshape(
            request_count, KEY_HEADS, decode_step_count, query_group_width, HEAD_SIZE
        )
        .transpose(2, 0, 1, 3, 4)
        .reshape(decode_step_count, request_count, query_width)
    )
    by_heads = lax.all_to_all(heads_local, "tensor", split_axis=2, concat_axis=1, tiled=True)
    projected = jnp.einsum("sbc,cd->sbd", by_heads, w_out, preferred_element_type=jnp.float32)
    owned = lax.psum_scatter(projected, "tensor", scatter_dimension=1, tiled=True)
    return (owned, new_keys, new_values)


def solution(mesh):
    placed = (
        P(None, None, "seq"),
        P("seq"),
        P("seq", "tensor"),
        P("tensor"),
        P("tensor", "seq"),
        P("tensor", "seq", None),
        P("tensor", "seq", None),
        P("tensor", "seq", None),
        P("tensor", "seq", None),
        P("tensor"),
        P("tensor"),
    )
    return jax.shard_map(
        body,
        mesh=mesh,
        in_specs=placed,
        out_specs=(P(None, "tensor", "seq"), P("tensor", None, None), P("tensor", None, None)),
        check_vma=False,
    )
```

profile of v0, /device:TPU:1, one launch (start us, length us, event | category | flops | bytes accessed | tf_op | source)
XLA Modules:
  0.0 849.9 jit_solution(4505224170774639408)
XLA Ops:
  7.3 0.8 convert_element_type.43
  8.0 1.0 fusion.22
  9.1 53.3 %psum.28 = f32[4,64]{1,0:T(4,128)S(1)} all-reduce(f32[4,64]{1,0:T(4,128)S(1)} %fusion.22), channel_id=1, replica_groups=mesh['seq'=32,'tensor'=16] {'seq'}, use_global_device_ids=true, to_apply=%region_1.0 | all-reduce | flops 256 | bytes 2048 | tf_op jit(solution)/shard_map/psum | solution.py:54
  62.4 2.1 fusion.29
  65.2 0.1 add_convert_fusion.1
  65.2 0.1 multiply_cosine_fusion
  65.5 0.2 copy.148
  65.7 2.2 copy.149
  67.9 202.5 %all-reduce.5.cloned.1.call-done = f32[4,64,448]{2,1,0:T(8,128)} async-done(((f32[4,64,448]{2,1,0:T(8,128)}), f32[4,64,448]{2,1,0:T(8,128)}) %all-reduce.5.cloned.1.call-update) | async-done | bytes 458768 | tf_op jit(solution)/shard_map/psum | solution.py:60
  270.4 1.1 broadcast_add_fusion
  271.5 1.1 copy.98
  272.6 6.5 all-to-all-start
  279.2 0.5 iota_compare_fusion
  279.8 0.1 broadcast_compare_fusion
  279.8 10.0 %all-to-all-done = f32[4,64,448]{2,0,1:T(4,128)S(1)} async-done(((f32[4,64,448]{2,0,1:T(4,128)}), f32[4,64,448]{2,0,1:T(4,128)S(1)}, u32[]{:S(2)}, u32[]{:S(2)}) %all-to-all-start) | async-done | bytes 458784 | tf_op jit(solution)/shard_map/all_to_all | solution.py:61
  289.9 0.3 copy.99
  290.2 0.3 all_to_all.29
  290.5 0.6 slice_bitcast_fusion.1
  291.2 0.1 reshape.150
  291.4 0.2 fusion.51
  291.5 0.4 subtract_convert_fusion
  292.0 0.2 maximum_bitcast_fusion
  292.3 1.4 fusion.52
  293.7 0.7 fusion.53
  294.4 89.4 %pmax.7 = f32[4,8,20]{2,1,0:T(8,128)} all-reduce(f32[4,8,20]{2,1,0:T(8,128)S(1)} %copy_maximum_fusion), channel_id=1, replica_groups=mesh['seq'=32,'tensor'=16] {'seq'}, use_global_device_ids=true, to_apply=%region_5.6 | all-reduce | flops 640 | bytes 5120 | tf_op jit(solution)/shard_map/pmax | solution.py:137
  383.8 1.5 multiply_subtract_fusion
  385.3 1.9 fusion.20
  387.1 1.1 fusion.12
  388.2 90.0 %psum.31 = f32[4,8,20]{2,1,0:T(8,128)S(1)} all-reduce(f32[4,8,20]{2,1,0:T(8,128)S(1)} %get-tuple-element.6), channel_id=1, replica_groups=mesh['seq'=32,'tensor'=16] {'seq'}, use_global_device_ids=true, to_apply=%region_10.11 | all-reduce | flops 640 | bytes 5120 | tf_op jit(solution)/shard_map/psum | solution.py:139
  478.3 1.3 convolution_bitcast_fusion
  479.6 1.2 fusion.4
  480.9 0.3 fusion.54
  481.2 0.1 fusion.37
  481.4 199.4 %all-reduce.7.cloned.1.call-done = f32[4,8,20,128]{3,2,0,1:T(8,128)} async-done(((f32[4,8,20,128]{3,2,0,1:T(8,128)}), f32[4,8,20,128]{3,2,0,1:T(8,128)}) %all-reduce.7.cloned.1.call-update) | async-done | bytes 327696 | tf_op jit(solution)/shard_map/psum | solution.py:139
  680.7 1.5 fusion.6
  682.2 0.1 copy.121
  682.3 4.5 copy.139
  686.8 11.0 %reshape.165 = bf16[16,2,2560]{2,1,0:T(2,128)(2,1)S(1)} reshape(bf16[5120,4,4]{2,1,0:T(4,128)(2,1)} %bitcast.84) | data formatting | bytes 327680
  697.8 13.3 %all_to_all.36 = bf16[16,2,2560]{2,1,0:T(2,128)(2,1)S(1)} all-to-all(bf16[16,2,2560]{2,1,0:T(2,128)(2,1)S(1)} %reshape.165), channel_id=1, replica_groups=mesh['seq'=32,'tensor'=16] {'tensor'}, dimensions={0} | all-to-all | bytes 327680 | tf_op jit(solution)/shard_map/all_to_all | solution.py:174
  711.1 12.3 %reshape.166 = bf16[5120,4,4]{2,1,0:T(4,128)(2,1)} reshape(bf16[16,2,2560]{2,1,0:T(2,128)(2,1)S(1)} %all_to_all.36) | data formatting | bytes 327680
  723.4 6.4 copy.140
  729.9 0.1 copy.125
  730.0 0.1 all_to_all.33
  730.1 0.9 fusion.34
  731.0 1.3 dynamic-slice
  733.0 0.7 fusion.46
  733.7 108.3 %all-reduce.9.cloned.1.call-done = f32[4,64,160]{2,1,0:T(8,128)} async-done(((f32[4,64,160]{2,1,0:T(8,128)}), f32[4,64,160]{2,1,0:T(8,128)}) %all-reduce.9.cloned.1.call-update) | async-done | bytes 163856
  842.0 1.4 constant_dynamic-slice_fusion
  (65 shorter events, 0.4 us)
Async XLA Ops:
  7.2 285.1 %copy-start = (bf16[4,128,1024]{2,1,0:T(8,128)(2,1)S(1)}, bf16[4,128,1024]{2,1,0:T(8,128)(2,1)}, u32[]{:S(2)}) copy-start(bf16[4,128,1024]{2,1,0:T(8,128)(2,1)} %param.18) | copy-start | bytes 3145732
  7.2 58.0 %copy-start.19 = (s32[4]{0:T(128)S(1)}, s32[4]{0:T(128)}, u32[]{:S(2)}) copy-start(s32[4]{0:T(128)} %param.21) | copy-start | bytes 52
  7.2 58.2 %copy-start.16 = (bf16[448]{0:T(512)(128)(2,1)S(1)}, bf16[448]{0:T(512)(128)(2,1)}, u32[]{:S(2)}) copy-start(bf16[448]{0:T(512)(128)(2,1)} %param.14) | copy-start | bytes 2692
  7.2 58.3 %copy-start.4 = (bf16[1,384,1024]{2,1,0:T(8,128)(2,1)S(1)}, bf16[1,384,1024]{2,1,0:T(8,128)(2,1)}, u32[]{:S(2)}) copy-start(bf16[1,384,1024]{2,1,0:T(8,128)(2,1)} %param.16) | copy-start | bytes 2359300
  7.2 263.2 %all-reduce.5.cloned.1.call-start = ((), (), s32[]{:S(2)}) async-start(), calls=%async_computation.2 | async-start | bytes 1048576 | tf_op jit(solution)/shard_map/psum | solution.py:60
  65.4 2.5 copy-start.12
  65.4 2.5 copy-start.13
  67.9 225.8 %copy-start.15 = (pred[384]{0:T(512)(128)(4,1)}, pred[384]{0:T(512)(128)(4,1)S(1)}, u32[]{:S(2)}) copy-start(pred[384]{0:T(512)(128)(4,1)S(1)} %add_compare_fusion) | copy-start | bytes 1156
  272.6 17.2 %all-to-all-start = ((f32[4,64,448]{2,0,1:T(4,128)}), f32[4,64,448]{2,0,1:T(4,128)S(1)}, u32[]{:S(2)}, u32[]{:S(2)}) async-start(f32[4,64,448]{2,0,1:T(4,128)} %copy.98), calls=%async_computation | async-start | bytes 1048576 | tf_op jit(solution)/shard_map/all_to_all | solution.py:61
  279.2 401.5 %all-reduce.7.cloned.1.call-start = ((), (), s32[]{:S(2)}) async-start(), calls=%async_computation.3 | async-start | bytes 786432 | tf_op jit(solution)/shard_map/psum | solution.py:139
  279.8 12.4 %copy-start.18 = (pred[4,128]{1,0:T(4,128)(4,1)}, pred[4,128]{1,0:T(4,128)(4,1)S(1)}, u32[]{:S(2)}) copy-start(pred[4,128]{1,0:T(4,128)(4,1)S(1)} %broadcast_compare_fusion) | copy-start | bytes 1540
  292.2 2.1 copy-start.2
  294.4 183.9 %copy-start.5 = (bf16[48,8,8,128]{3,2,1,0:T(8,128)(2,1)S(1)}, bf16[48,8,8,128]{3,2,1,0:T(8,128)(2,1)}, u32[]{:S(2)}) copy-start(bf16[48,8,8,128]{3,2,1,0:T(8,128)(2,1)} %copy.149) | copy-start | bytes 2359300
  383.8 4.4 copy-start.9
  383.8 4.4 copy-start.14
  478.3 1.3 copy-start.1
  478.3 1.3 copy-start.6
  479.6 1.3 copy-start.3
  479.6 1.3 copy-start.7
  479.6 1.3 copy-start.8
  479.6 1.3 copy-start.17
  479.6 1.7 copy-start.10
  480.8 361.2 %all-reduce.9.cloned.1.call-start = ((), (), s32[]{:S(2)}) async-start(), calls=%async_computation.4 | async-start | bytes 524288
  723.4 6.6 copy-start.11
Sparse Core Ops, SparseCore 0:
  64.6 205.7 all-reduce.4
  481.0 199.7 all-reduce.6
  731.2 110.8 all-reduce.8
where the time goes:
time: 851 us; the launch traced here: 850 us
  waiting for transfers between devices  520 us (61%)
  blocking collectives  246 us (29%)
  local copies, waits for them, and re-layouts  42.4 us (5%)
  between operations  15.6 us (2%)
  other arithmetic  9.67 us (1%)
  matrix products  9.33 us (1%)
    psum x1, waiting for transfers between devices, body(): summed_cols = lax.psum(partial_value, 'seq') + bias  202 us
    psum x1, waiting for transfers between devices, body(): lax.psum((local_weight * factor, local_acc * factor[..., None]), 'seq')  199 us
    unnamed x4, waiting for transfers between devices  108 us
    psum x1, blocking collectives, body(): lax.psum((local_weight * factor, local_acc * factor[..., None]), 'seq')  90 us
    pmax x1, blocking collectives, body(): global_max = lax.pmax(local_max, 'seq')  89.4 us
    psum x1, blocking collectives, body(): squares = lax.psum(jnp.sum(xf * xf, axis=2), 'seq')  53.3 us
    unnamed x46, local copies, waits for them, and re-layouts  28.4 us
  transfers between devices with their start and end apart: 4, of which 4 were waited for; matrix products, arithmetic and copies ran while one was open for 1% of the time, Pallas kernels for 0%

commit v1 on v0

--- a/solution.py
+++ b/solution.py
@@ -41,62 +41,88 @@
     prefix_lens,
     suffix_lens,
 ):
-    decode_step_count = hidden.shape[0]
-    request_count = suffix_lens.shape[0]
+    seq_count = lax.axis_size("seq")
+    tensor_count = lax.axis_size("tensor")
+    steps = hidden.shape[0]
+    request_total = hidden.shape[1]
+    requests = suffix_lens.shape[0]
+    columns = w_qkv.shape[1]
     prefix_count = prefix_key_cache.shape[1]
     suffix_count = suffix_key_cache.shape[1]
     query_group_width = QUERY_HEADS // KEY_HEADS
     query_width = QUERY_HEADS * HEAD_SIZE
-    query_rows = decode_step_count * query_group_width
+    query_rows = steps * query_group_width
     scale = float(HEAD_SIZE) ** (-0.5)
     seq_index = lax.axis_index("seq")
+
+    w_out_cols = lax.all_gather(w_out, "tensor", axis=0, tiled=True)
+
     xf = hidden.astype(jnp.float32)
-    squares = lax.psum(jnp.sum(xf * xf, axis=2), "seq")
+    local_squares = jnp.sum(xf * xf, axis=2)
+    squares = jnp.sum(
+        lax.all_to_all(
+            jnp.broadcast_to(local_squares[None], (seq_count,) + local_squares.shape),
+            "seq", 0, 0, tiled=True,
+        ),
+        axis=0,
+    )
     normed = (
         xf * lax.rsqrt(squares / D + epsilon)[..., None] * norm_gain.astype(jnp.float32)
     ).astype(jnp.bfloat16)
     partial_value = jnp.einsum("sbd,dc->sbc", normed, w_qkv, preferred_element_type=jnp.float32)
-    bias = b_qkv.astype(jnp.float32)
-    summed_cols = lax.psum(partial_value, "seq") + bias
-    combined_output = lax.all_to_all(summed_cols, "tensor", split_axis=1, concat_axis=2, tiled=True)
+
+    halves = seq_count // (steps * requests)
+    half_width = columns // halves
+    groups = request_total // requests
+    chunks = (
+        partial_value.reshape(steps, groups, requests, halves, half_width)
+        .transpose(0, 2, 3, 1, 4)
+        .reshape(seq_count, groups, half_width)
+    )
+    reduced = jnp.sum(lax.all_to_all(chunks, "seq", 0, 0, tiled=True), axis=0)
+    bias = lax.dynamic_slice_in_dim(
+        b_qkv.astype(jnp.float32), (seq_index % halves) * half_width, half_width
+    )
+    reduced = reduced + bias[None, :]
+    owned_rows = lax.all_to_all(reduced, "tensor", 0, 0, tiled=True)
+    gathered = lax.all_gather(owned_rows, "seq", axis=0, tiled=False)
+    combined_output = (
+        gathered.reshape(steps, requests, halves, tensor_count, half_width)
+        .transpose(0, 1, 3, 2, 4)
+        .reshape(steps, requests, tensor_count * columns)
+    )
+
     token_positions = (
         (prefix_lens[0] + suffix_lens)[None, :]
-        + jnp.arange(decode_step_count, dtype=jnp.int32)[:, None]
+        + jnp.arange(steps, dtype=jnp.int32)[:, None]
     ).astype(jnp.float32)
     query_matrix = apply_rotary(
-        combined_output[..., :query_width].reshape(
-            decode_step_count, request_count, QUERY_HEADS, HEAD_SIZE
-        ),
+        combined_output[..., :query_width].reshape(steps, requests, QUERY_HEADS, HEAD_SIZE),
         token_positions,
     ).astype(jnp.bfloat16)
     keys_float = apply_rotary(
         combined_output[..., query_width : query_width + KEY_COLUMNS].reshape(
-            decode_step_count, request_count, KEY_HEADS, HEAD_SIZE
+            steps, requests, KEY_HEADS, HEAD_SIZE
         ),
         token_positions,
     )
     values_float = combined_output[..., query_width + KEY_COLUMNS :].reshape(
-        decode_step_count, request_count, KEY_HEADS, HEAD_SIZE
+        steps, requests, KEY_HEADS, HEAD_SIZE
     )
     current_keys = keys_float.astype(jnp.bfloat16)
     current_values = values_float.astype(jnp.bfloat16)
-    new_keys = keys_float.reshape(decode_step_count, request_count, KEY_COLUMNS).transpose(1, 0, 2)
-    new_values = values_float.reshape(decode_step_count, request_count, KEY_COLUMNS).transpose(
-        1, 0, 2
-    )
+    new_keys = keys_float.reshape(steps, requests, KEY_COLUMNS).transpose(1, 0, 2)
+    new_values = values_float.reshape(steps, requests, KEY_COLUMNS).transpose(1, 0, 2)
     query_by_group = (
-        query_matrix.reshape(
-            decode_step_count, request_count, KEY_HEADS, query_group_width, HEAD_SIZE
-        )
+        query_matrix.reshape(steps, requests, KEY_HEADS, query_group_width, HEAD_SIZE)
         .transpose(1, 2, 0, 3, 4)
-        .reshape(request_count, KEY_HEADS, query_rows, HEAD_SIZE)
-    )
+        .reshape(requests, KEY_HEADS, query_rows, HEAD_SIZE)
+    )
+
     prefix_key_block = prefix_key_cache[0].reshape(prefix_count, KEY_HEADS, HEAD_SIZE)
     prefix_value_block = prefix_value_cache[0].reshape(prefix_count, KEY_HEADS, HEAD_SIZE)
-    suffix_key_block = suffix_key_cache.reshape(request_count, suffix_count, KEY_HEADS, HEAD_SIZE)
-    suffix_value_block = suffix_value_cache.reshape(
-        request_count, suffix_count, KEY_HEADS, HEAD_SIZE
-    )
+    suffix_key_block = suffix_key_cache.reshape(requests, suffix_count, KEY_HEADS, HEAD_SIZE)
+    suffix_value_block = suffix_value_cache.reshape(requests, suffix_count, KEY_HEADS, HEAD_SIZE)
     score_pre = (
         jnp.einsum(
             "rhqd,phd->rhqp", query_by_group, prefix_key_block, preferred_element_type=jnp.float32
@@ -134,11 +160,7 @@
         suffix_value_block,
         preferred_element_type=jnp.float32,
     )
-    global_max = lax.pmax(local_max, "seq")
-    factor = jnp.exp(local_max - global_max)
-    global_weight, global_acc = lax.psum(
-        (local_weight * factor, local_acc * factor[..., None]), "seq"
-    )
+
     fresh_k = current_keys.transpose(1, 2, 0, 3)
     fresh_v = current_values.transpose(1, 2, 0, 3)
     score_new = (
@@ -147,33 +169,50 @@
     )
     new_mask = (
         (jnp.arange(query_rows, dtype=jnp.int32) // query_group_width)[:, None]
-        >= jnp.arange(decode_step_count, dtype=jnp.int32)[None, :]
+        >= jnp.arange(steps, dtype=jnp.int32)[None, :]
     )[None, None]
     fill_new = jnp.where(new_mask, score_new, masked_fill)
     new_max = jnp.max(fill_new, axis=3)
     prob_new = jnp.where(new_mask, jnp.exp(fill_new - new_max[..., None]), 0.0)
-    top = jnp.maximum(global_max, new_max)
-    factor_old = jnp.exp(global_max - top)
-    factor_new = jnp.exp(new_max - top)
-    total = global_weight * factor_old + jnp.sum(prob_new, axis=3) * factor_new
+    new_weight = jnp.sum(prob_new, axis=3)
     new_acc = jnp.einsum(
         "rhqi,rhid->rhqd",
         prob_new.astype(jnp.bfloat16),
         fresh_v,
         preferred_element_type=jnp.float32,
     )
-    summed = global_acc * factor_old[..., None] + new_acc * factor_new[..., None]
-    attention_output = (summed / total[..., None]).astype(jnp.bfloat16)
+
+    packed = jnp.concatenate(
+        [local_acc, local_max[..., None], local_weight[..., None]], axis=-1
+    ).reshape(seq_count, query_rows, HEAD_SIZE + 2)
+    arrived = lax.all_to_all(packed, "seq", 0, 0, tiled=True)
+    part_acc = arrived[..., :HEAD_SIZE]
+    part_max = arrived[..., HEAD_SIZE]
+    part_weight = arrived[..., HEAD_SIZE + 1]
+    global_max = jnp.max(part_max, axis=0)
+    factor = jnp.exp(part_max - global_max[None])
+    global_weight = jnp.sum(part_weight * factor, axis=0)
+    global_acc = jnp.sum(part_acc * factor[..., None], axis=0)
+
+    mine_r = seq_index // KEY_HEADS
+    mine_h = seq_index % KEY_HEADS
+    own_new_max = new_max[mine_r, mine_h]
+    own_new_weight = new_weight[mine_r, mine_h]
+    own_new_acc = new_acc[mine_r, mine_h]
+    top = jnp.maximum(global_max, own_new_max)
+    factor_old = jnp.exp(global_max - top)
+    factor_new = jnp.exp(own_new_max - top)
+    total = global_weight * factor_old + own_new_weight * factor_new
+    summed = global_acc * factor_old[..., None] + own_new_acc * factor_new[..., None]
+    attention_slice = (summed / total[..., None]).astype(jnp.bfloat16)
+
+    attention_all = lax.all_gather(attention_slice, "seq", axis=0, tiled=False)
     heads_local = (
-        attention_output.reshape(
-            request_count, KEY_HEADS, decode_step_count, query_group_width, HEAD_SIZE
-        )
+        attention_all.reshape(requests, KEY_HEADS, steps, query_group_width, HEAD_SIZE)
         .transpose(2, 0, 1, 3, 4)
-        .reshape(decode_step_count, request_count, query_width)
-    )
-    by_heads = lax.all_to_all(heads_local, "tensor", split_axis=2, concat_axis=1, tiled=True)
-    projected = jnp.einsum("sbc,cd->sbd", by_heads, w_out, preferred_element_type=jnp.float32)
-    owned = lax.psum_scatter(projected, "tensor", scatter_dimension=1, tiled=True)
+        .reshape(steps, requests, query_width)
+    )
+    owned = jnp.einsum("sbc,cd->sbd", heads_local, w_out_cols, preferred_element_type=jnp.float32)
     return (owned, new_keys, new_values)
 
 

time: 851 us -> 209 us (0.25)
  waiting for transfers between devices: 520 us -> 65.9 us
  blocking collectives: 246 us -> 57.9 us
  starting transfers between devices: 6.65 us -> 33.3 us
  local copies, waits for them, and re-layouts: 42.4 us -> 19.4 us
    psum x2 -> x0, waiting for transfers between devices: 402 us -> none  [the longest x1 202 us: body(): summed_cols = lax.psum(partial_value, 'seq') + bias]
    psum x2 -> x0, blocking collectives: 143 us -> none  [the longest x1 90 us: body(): lax.psum((local_weight * factor, local_acc * factor[..., None]), 'seq')]
    unnamed x4 -> x1, waiting for transfers between devices: 108 us -> 0.68 us
    pmax x1 -> x0, blocking collectives: 89.4 us -> none  [body(): global_max = lax.pmax(local_max, 'seq')]
    all_gather x0 -> x2, blocking collectives: none -> 57.9 us  [the longest x1 30.3 us: body(): gathered = lax.all_gather(owned_rows, 'seq', axis=0, tiled=False)]
    all_to_all x1 -> x4, waiting for transfers between devices: 10 us -> 65.2 us  [the longest x1 31.7 us: body(): reduced = jnp.sum(lax.all_to_all(chunks, 'seq', 0, 0, tiled=True), axis=0)]
    all_to_all x1 -> x4, starting transfers between devices: 6.53 us -> 33.2 us  [the longest x1 16.7 us: body(): lax.all_to_all(jnp.broadcast_to(local_squares[None], (seq_count,) + local...]
    unnamed x46 -> x30, local copies, waits for them, and re-layouts: 28.4 us -> 10.7 us
  transfers between devices with their start and end apart: 4 -> 5, of which waited for: 4 -> 4; matrix products, arithmetic and copies ran while one was open for 1% -> 11% of each run, Pallas kernels for 0% -> 0%
where the time goes in v1:
time: 209 us
  waiting for transfers between devices  65.9 us (32%)
  blocking collectives  57.9 us (28%)
  starting transfers between devices  33.3 us (16%)
  local copies, waits for them, and re-layouts  19.4 us (9%)
  between operations  15.2 us (7%)
  other arithmetic  10.3 us (5%)
  matrix products  6.65 us (3%)
    all_to_all x1, waiting for transfers between devices, body(): reduced = jnp.sum(lax.all_to_all(chunks, 'seq', 0, 0, tiled=True), axis=0)  31.7 us
    all_gather x1, blocking collectives, body(): gathered = lax.all_gather(owned_rows, 'seq', axis=0, tiled=False)  30.3 us
    all_gather x1, blocking collectives, body(): attention_all = lax.all_gather(attention_slice, 'seq', axis=0, tiled=False)  27.7 us
    all_to_all x1, waiting for transfers between devices, body(): arrived = lax.all_to_all(packed, 'seq', 0, 0, tiled=True)  18.1 us
    all_to_all x1, starting transfers between devices, body(): lax.all_to_all(jnp.broadcast_to(local_squares[None], (seq_count,) + local...  16.7 us
    all_to_all x1, waiting for transfers between devices, body(): lax.all_to_all(jnp.broadcast_to(local_squares[None], (seq_count,) + local...  11.5 us
    unnamed x30, local copies, waits for them, and re-layouts  10.7 us
    all_to_all x1, starting transfers between devices, body(): owned_rows = lax.all_to_all(reduced, 'tensor', 0, 0, tiled=True)  6.75 us
  transfers between devices with their start and end apart: 5, of which 4 were waited for; matrix products, arithmetic and copies ran while one was open for 11% of the time, Pallas kernels for 0%

profile of v1, /device:TPU:1, one launch (start us, length us, event | category | flops | bytes accessed | tf_op | source)
XLA Modules:
  0.0 208.5 jit_solution(6557745466095556476)
XLA Ops:
  7.2 1.1 fusion.21
  8.3 0.7 reshape.377
  9.0 16.7 %all-to-all-start = ((f32[32,1,256]{2,1,0:T(1,128)}), f32[32,1,256]{2,1,0:T(1,128)S(1)}, u32[]{:S(2)}, u32[]{:S(2)}) async-start(f32[32,1,256]{2,1,0:T(1,128)} %reshape.377), calls=%async_computation | async-start | bytes 65536 | tf_op jit(solution)/shard_map/all_to_all | solution.py:63
  25.8 0.7 convert_element_type.50
  26.4 11.5 %all-to-all-done = f32[32,1,256]{2,1,0:T(1,128)S(1)} async-done(((f32[32,1,256]{2,1,0:T(1,128)}), f32[32,1,256]{2,1,0:T(1,128)S(1)}, u32[]{:S(2)}, u32[]{:S(2)}) %all-to-all-start) | async-done | bytes 32800 | tf_op jit(solution)/shard_map/all_to_all | solution.py:63
  37.9 0.5 broadcast.191
  38.4 0.6 reduce.1
  39.2 1.2 fusion.31
  40.4 0.5 reshape.356
  40.9 1.0 copy.235
  41.9 4.8 %all-to-all-start.1 = ((f32[32,16,224]{2,1,0:T(8,128)}), f32[32,16,224]{2,1,0:T(8,128)S(1)}, u32[]{:S(2)}, u32[]{:S(2)}) async-start(f32[32,16,224]{2,1,0:T(8,128)} %bitcast.3), calls=%async_computation.1 | async-start | bytes 1048576 | tf_op jit(solution)/shard_map/all_to_all | solution.py:82
  46.7 0.7 all-gather.4.cloned.1.call-update
  48.5 31.7 %all-to-all-done.1 = f32[32,16,224]{2,1,0:T(8,128)S(1)} async-done(((f32[32,16,224]{2,1,0:T(8,128)}), f32[32,16,224]{2,1,0:T(8,128)S(1)}, u32[]{:S(2)}, u32[]{:S(2)}) %all-to-all-start.1) | async-done | bytes 458784 | tf_op jit(solution)/shard_map/all_to_all | solution.py:82
  80.3 0.6 reshape_add_fusion
  80.9 6.8 %all-to-all-start.2 = ((f32[16,1,224]{2,1,0:T(1,128)}), f32[16,1,224]{2,1,0:T(1,128)S(1)}, u32[]{:S(2)}, u32[]{:S(2)}) async-start(f32[16,1,224]{2,1,0:T(1,128)} %reshape_add_fusion), calls=%async_computation.2 | async-start | bytes 32768 | tf_op jit(solution)/shard_map/all_to_all | solution.py:87
  87.9 2.2 %copy.285 = bf16[48,8,8,128]{3,2,1,0:T(8,128)(2,1)} copy(bf16[48,8,8,128]{3,1,2,0:T(8,128)(2,1)} %bitcast.110) | data formatting | bytes 1572864
  90.1 4.0 %all-to-all-done.2 = f32[16,1,224]{2,1,0:T(1,128)S(1)} async-done(((f32[16,1,224]{2,1,0:T(1,128)}), f32[16,1,224]{2,1,0:T(1,128)S(1)}, u32[]{:S(2)}, u32[]{:S(2)}) %all-to-all-start.2) | async-done | bytes 14368 | tf_op jit(solution)/shard_map/all_to_all | solution.py:87
  94.1 30.3 %all-gather = f32[512,1,224]{2,0,1:T(8,128)S(1)} all-gather(f32[16,1,224]{2,0,1:T(8,128)S(1)} %copy.236), channel_id=2, replica_groups=mesh['seq'=32,'tensor'=16] {'seq'}, dimensions={0}, use_global_device_ids=true | all-gather | bytes 473088 | tf_op jit(solution)/shard_map/all_gather | solution.py:88
  124.3 0.4 copy.237
  124.8 0.8 reshape.359
  125.6 0.3 subtract_convert_fusion
  126.2 0.7 fusion.68
  126.8 0.7 fusion.67
  127.6 0.3 fusion.19
  127.9 0.4 fusion.9
  128.4 1.1 copy.256
  129.5 1.1 copy.255
  130.6 1.7 fusion.4
  132.4 0.5 fusion.11
  133.2 0.7 copy-done.2
  134.1 0.4 copy.257
  134.5 1.5 reshape.379
  136.0 4.9 %all-to-all-start.3 = ((f32[32,1,2600]{2,1,0:T(1,128)}), f32[32,1,2600]{2,1,0:T(1,128)S(1)}, u32[]{:S(2)}, u32[]{:S(2)}) async-start(f32[32,1,2600]{2,1,0:T(1,128)} %reshape.379), calls=%async_computation.3 | async-start | bytes 688128 | tf_op jit(solution)/shard_map/all_to_all | solution.py:188
  141.1 0.7 copy.269
  141.9 0.3 fusion.66
  142.2 0.3 fusion.38
  142.6 0.7 fusion.51
  143.3 0.7 fusion.36
  144.0 2.2 %copy.268 = bf16[16,320,160]{1,0,2:T(8,128)(2,1)S(1)} copy(bf16[16,320,160]{1,2,0:T(8,128)(2,1)} %all-gather.4.cloned.1.call-done) | data formatting | bytes 3276800 | tf_op jit(solution)/shard_map/all_gather | solution.py:58
  146.2 2.5 %reshape.375 = bf16[5120,160,1]{0,1,2:T(8,128)(2,1)} reshape(bf16[16,320,160]{1,0,2:T(8,128)(2,1)S(1)} %copy.268) | data formatting | bytes 3276800
  148.7 18.1 %all-to-all-done.3 = f32[32,1,2600]{2,1,0:T(1,128)S(1)} async-done(((f32[32,1,2600]{2,1,0:T(1,128)}), f32[32,1,2600]{2,1,0:T(1,128)S(1)}, u32[]{:S(2)}, u32[]{:S(2)}) %all-to-all-start.3) | async-done | bytes 332832 | tf_op jit(solution)/shard_map/all_to_all | solution.py:188
  166.8 1.4 reduce.2
  168.2 0.4 reshape.380
  168.6 1.0 fusion.64
  169.9 1.3 copy.280
  171.7 0.7 fusion.57
  172.6 27.7 %all_gather.15 = bf16[32,20,128]{2,1,0:T(8,128)(2,1)S(1)} all-gather(bf16[1,20,128]{2,1,0:T(8,128)(2,1)S(1)} %copy.265), channel_id=1, replica_groups=mesh['seq'=32,'tensor'=16] {'seq'}, dimensions={0}, use_global_device_ids=true | all-gather | bytes 168960 | tf_op jit(solution)/shard_map/all_gather | solution.py:209
  200.5 1.2 fusion.69
  (65 shorter events, 3.0 us)
Async XLA Ops:
  7.2 119.7 %copy-start = (bf16[4,128,1024]{2,1,0:T(8,128)(2,1)S(1)}, bf16[4,128,1024]{2,1,0:T(8,128)(2,1)}, u32[]{:S(2)}) copy-start(bf16[4,128,1024]{2,1,0:T(8,128)(2,1)} %param.18) | copy-start | bytes 3145732
  9.0 28.9 %all-to-all-start = ((f32[32,1,256]{2,1,0:T(1,128)}), f32[32,1,256]{2,1,0:T(1,128)S(1)}, u32[]{:S(2)}, u32[]{:S(2)}) async-start(f32[32,1,256]{2,1,0:T(1,128)} %reshape.377), calls=%async_computation | async-start | bytes 65536 | tf_op jit(solution)/shard_map/all_to_all | solution.py:63
  40.9 7.2 %copy-start.8 = (bf16[448]{0:T(512)(128)(2,1)S(1)}, bf16[448]{0:T(512)(128)(2,1)}, u32[]{:S(2)}) copy-start(bf16[448]{0:T(512)(128)(2,1)} %param.14) | copy-start | bytes 2692
  40.9 7.3 %copy-start.9 = (s32[4]{0:T(128)S(1)}, s32[4]{0:T(128)}, u32[]{:S(2)}) copy-start(s32[4]{0:T(128)} %param.21) | copy-start | bytes 52
  41.9 45.8 %copy-start.6 = (bf16[1,384,1024]{2,1,0:T(8,128)(2,1)S(1)}, bf16[1,384,1024]{2,1,0:T(8,128)(2,1)}, u32[]{:S(2)}) copy-start(bf16[1,384,1024]{2,1,0:T(8,128)(2,1)} %param.16) | copy-start | bytes 2359300
  41.9 38.4 %all-to-all-start.1 = ((f32[32,16,224]{2,1,0:T(8,128)}), f32[32,16,224]{2,1,0:T(8,128)S(1)}, u32[]{:S(2)}, u32[]{:S(2)}) async-start(f32[32,16,224]{2,1,0:T(8,128)} %bitcast.3), calls=%async_computation.1 | async-start | bytes 1048576 | tf_op jit(solution)/shard_map/all_to_all | solution.py:82
  46.7 97.3 %all-gather.4.cloned.1.call-start = ((), (), s32[]{:S(2)}) async-start(), calls=%async_computation.4 | async-start | bytes 2088960 | tf_op jit(solution)/shard_map/all_gather | solution.py:58
  80.9 13.2 %all-to-all-start.2 = ((f32[16,1,224]{2,1,0:T(1,128)}), f32[16,1,224]{2,1,0:T(1,128)S(1)}, u32[]{:S(2)}, u32[]{:S(2)}) async-start(f32[16,1,224]{2,1,0:T(1,128)} %reshape_add_fusion), calls=%async_computation.2 | async-start | bytes 32768 | tf_op jit(solution)/shard_map/all_to_all | solution.py:87
  126.1 1.4 copy-start.4
  130.6 1.8 copy-start.7
  132.9 1.0 copy-start.2
  132.9 1.1 copy-start.3
  136.0 5.9 %copy-start.5 = (bf16[4,8,4,5,128]{4,1,3,2,0:T(8,128)(2,1)S(1)}, bf16[4,8,4,5,128]{4,1,3,2,0:T(8,128)(2,1)}, u32[]{:S(2)}) copy-start(bf16[4,8,4,5,128]{4,1,3,2,0:T(8,128)(2,1)} %copy-done.4) | copy-start | bytes 491524
  136.0 30.8 %all-to-all-start.3 = ((f32[32,1,2600]{2,1,0:T(1,128)}), f32[32,1,2600]{2,1,0:T(1,128)S(1)}, u32[]{:S(2)}, u32[]{:S(2)}) async-start(f32[32,1,2600]{2,1,0:T(1,128)} %reshape.379), calls=%async_computation.3 | async-start | bytes 688128 | tf_op jit(solution)/shard_map/all_to_all | solution.py:188
  169.9 30.7 %copy-start.1 = (bf16[5120,160,1]{0,1,2:T(8,128)(2,1)S(1)}, bf16[5120,160,1]{0,1,2:T(8,128)(2,1)}, u32[]{:S(2)}) copy-start(bf16[5120,160,1]{0,1,2:T(8,128)(2,1)} %reshape.375) | copy-start | bytes 4915204
Sparse Core Ops, SparseCore 0:
  50.5 59.9 all-gather.3

commit v2 on v1

--- a/solution.py
+++ b/solution.py
@@ -26,6 +26,13 @@
     left = values[..., :half]
     right = values[..., half:]
     return jnp.concatenate([left * cosine - right * sine, right * cosine + left * sine], axis=-1)
+
+
+def broadcast_gather(block, axis):
+    count = lax.axis_size(axis)
+    return lax.all_to_all(
+        jnp.broadcast_to(block[None], (count,) + block.shape), axis, 0, 0, tiled=True
+    )
 
 
 def body(
@@ -55,7 +62,7 @@
     scale = float(HEAD_SIZE) ** (-0.5)
     seq_index = lax.axis_index("seq")
 
-    w_out_cols = lax.all_gather(w_out, "tensor", axis=0, tiled=True)
+    w_out_cols = broadcast_gather(w_out, "tensor").reshape(-1, w_out.shape[1])
 
     xf = hidden.astype(jnp.float32)
     local_squares = jnp.sum(xf * xf, axis=2)
@@ -85,7 +92,7 @@
     )
     reduced = reduced + bias[None, :]
     owned_rows = lax.all_to_all(reduced, "tensor", 0, 0, tiled=True)
-    gathered = lax.all_gather(owned_rows, "seq", axis=0, tiled=False)
+    gathered = broadcast_gather(owned_rows, "seq")
     combined_output = (
         gathered.reshape(steps, requests, halves, tensor_count, half_width)
         .transpose(0, 1, 3, 2, 4)
@@ -206,7 +213,7 @@
     summed = global_acc * factor_old[..., None] + own_new_acc * factor_new[..., None]
     attention_slice = (summed / total[..., None]).astype(jnp.bfloat16)
 
-    attention_all = lax.all_gather(attention_slice, "seq", axis=0, tiled=False)
+    attention_all = broadcast_gather(attention_slice, "seq")
     heads_local = (
         attention_all.reshape(requests, KEY_HEADS, steps, query_group_width, HEAD_SIZE)
         .transpose(2, 0, 1, 3, 4)

time: 209 us -> 234 us (1.12)
  waiting for transfers between devices: 65.9 us -> 124 us
  blocking collectives: 57.9 us -> 13 us
  between operations: 15.2 us -> 1.77 us
  starting transfers between devices: 33.3 us -> 41.1 us
  local copies, waits for them, and re-layouts: 19.4 us -> 26.1 us
  other arithmetic: 10.3 us -> 16.2 us
  matrix products: 6.65 us -> 11.1 us
    all_gather x2 -> x0, blocking collectives: 57.9 us -> none  [the longest x1 30.3 us: body(): gathered = lax.all_gather(owned_rows, 'seq', axis=0, tiled=False)]
    all_to_all x1 -> x3, waiting for transfers between devices: 3.98 us -> 54.8 us  [broadcast_gather(): lax.all_to_all(jnp.broadcast_to(block[None], (count,) + block.shape), axi...]
    all_to_all x0 -> x1, blocking collectives: none -> 13 us  [body(): owned_rows = lax.all_to_all(reduced, 'tensor', 0, 0, tiled=True)]
    all_to_all x1 -> x3, starting transfers between devices: 6.75 us -> 15.4 us  [broadcast_gather(): lax.all_to_all(jnp.broadcast_to(block[None], (count,) + block.shape), axi...]
    all_to_all x1, waiting for transfers between devices: 18.1 us -> 23.9 us  [body(): arrived = lax.all_to_all(packed, 'seq', 0, 0, tiled=True)]
    all_to_all x1 -> x2, local copies, waits for them, and re-layouts: 0.01 us -> 3.19 us  [broadcast_gather(): lax.all_to_all(jnp.broadcast_to(block[None], (count,) + block.shape), axi...]
    broadcast_in_dim x0 -> x3, local copies, waits for them, and re-layouts: none -> 3.08 us  [broadcast_gather(): jnp.broadcast_to(block[None], (count,) + block.shape)]
    reshape x0 -> x1, local copies, waits for them, and re-layouts: none -> 2.53 us  [body(): w_out_cols = broadcast_gather(w_out, 'tensor').reshape(-1, w_out.shape[1])]
  transfers between devices with their start and end apart: 5 -> 6, of which waited for: 4 -> 6; matrix products, arithmetic and copies ran while one was open for 11% -> 13% of each run, Pallas kernels for 0% -> 0%
where the time goes in v2:
time: 234 us; the launch traced here: 233 us
  waiting for transfers between devices  124 us (53%)
  starting transfers between devices  41.1 us (18%)
  local copies, waits for them, and re-layouts  26.1 us (11%)
  other arithmetic  16.2 us (7%)
  blocking collectives  13 us (6%)
  matrix products  11.1 us (5%)
    all_to_all x3, waiting for transfers between devices, broadcast_gather(): lax.all_to_all(jnp.broadcast_to(block[None], (count,) + block.shape), axi...  54.8 us
    all_to_all x1, waiting for transfers between devices, body(): reduced = jnp.sum(lax.all_to_all(chunks, 'seq', 0, 0, tiled=True), axis=0)  33.4 us
    all_to_all x1, waiting for transfers between devices, body(): arrived = lax.all_to_all(packed, 'seq', 0, 0, tiled=True)  23.9 us
    all_to_all x1, starting transfers between devices, body(): lax.all_to_all(jnp.broadcast_to(local_squares[None], (seq_count,) + local...  16.7 us
    all_to_all x3, starting transfers between devices, broadcast_gather(): lax.all_to_all(jnp.broadcast_to(block[None], (count,) + block.shape), axi...  15.4 us
    all_to_all x1, blocking collectives, body(): owned_rows = lax.all_to_all(reduced, 'tensor', 0, 0, tiled=True)  13 us
    all_to_all x1, waiting for transfers between devices, body(): lax.all_to_all(jnp.broadcast_to(local_squares[None], (seq_count,) + local...  11.5 us
    unnamed x42, local copies, waits for them, and re-layouts  9.65 us
  transfers between devices with their start and end apart: 6, of which 6 were waited for; matrix products, arithmetic and copies ran while one was open for 13% of the time, Pallas kernels for 0%

profile of v2, /device:TPU:1, one launch (start us, length us, event | category | flops | bytes accessed | tf_op | source)
XLA Modules:
  0.0 232.7 jit_solution(14618126303984083541)
XLA Ops:
  0.6 1.1 fusion.21
  1.8 0.7 reshape.343
  2.5 16.7 %all-to-all-start = ((f32[32,1,256]{2,1,0:T(1,128)}), f32[32,1,256]{2,1,0:T(1,128)S(1)}, u32[]{:S(2)}, u32[]{:S(2)}) async-start(f32[32,1,256]{2,1,0:T(1,128)} %reshape.343), calls=%async_computation | async-start | bytes 65536 | tf_op jit(solution)/shard_map/all_to_all | solution.py:70
  19.3 0.7 convert_element_type.47
  19.9 11.5 %all-to-all-done = f32[32,1,256]{2,1,0:T(1,128)S(1)} async-done(((f32[32,1,256]{2,1,0:T(1,128)}), f32[32,1,256]{2,1,0:T(1,128)S(1)}, u32[]{:S(2)}, u32[]{:S(2)}) %all-to-all-start) | async-done | bytes 32800 | tf_op jit(solution)/shard_map/all_to_all | solution.py:70
  31.9 0.7 reduce.1
  32.8 1.2 fusion.31
  34.5 1.0 copy.223
  35.4 4.7 %all-to-all-start.1 = ((f32[32,16,224]{2,1,0:T(8,128)}), f32[32,16,224]{2,1,0:T(8,128)S(1)}, u32[]{:S(2)}, u32[]{:S(2)}) async-start(f32[32,16,224]{2,1,0:T(8,128)} %bitcast.3), calls=%async_computation.1 | async-start | bytes 1048576 | tf_op jit(solution)/shard_map/all_to_all | solution.py:89
  40.2 33.4 %all-to-all-done.1 = f32[32,16,224]{2,1,0:T(8,128)S(1)} async-done(((f32[32,16,224]{2,1,0:T(8,128)}), f32[32,16,224]{2,1,0:T(8,128)S(1)}, u32[]{:S(2)}, u32[]{:S(2)}) %all-to-all-start.1) | async-done | bytes 458784 | tf_op jit(solution)/shard_map/all_to_all | solution.py:89
  73.7 13.0 %all_to_all.36 = f32[16,1,224]{2,1,0:T(1,128)S(1)} all-to-all(f32[16,1,224]{2,1,0:T(1,128)S(1)} %reshape_add_fusion), channel_id=1, replica_groups=mesh['seq'=32,'tensor'=16] {'tensor'}, dimensions={0} | all-to-all | bytes 28672 | tf_op jit(solution)/shard_map/all_to_all | solution.py:94
  86.7 0.9 broadcast_in_dim.114
  87.6 5.8 %all-to-all-start.3 = ((f32[32,16,224]{2,1,0:T(8,128)}), f32[32,16,224]{2,1,0:T(8,128)S(1)}, u32[]{:S(2)}, u32[]{:S(2)}) async-start(f32[32,16,224]{2,1,0:T(8,128)} %broadcast_in_dim.114), calls=%async_computation.3 | async-start | bytes 1048576 | tf_op jit(solution)/shard_map/all_to_all | solution.py:33
  94.5 2.2 copy.272
  97.3 29.6 %all-to-all-done.3 = f32[32,16,224]{2,1,0:T(8,128)S(1)} async-done(((f32[32,16,224]{2,1,0:T(8,128)}), f32[32,16,224]{2,1,0:T(8,128)S(1)}, u32[]{:S(2)}, u32[]{:S(2)}) %all-to-all-start.3) | async-done | bytes 458784 | tf_op jit(solution)/shard_map/all_to_all | solution.py:33
  127.3 0.8 reshape.328
  128.8 0.7 fusion.70
  129.5 0.7 fusion.71
  132.1 1.1 copy.242
  133.2 1.6 fusion.11
  135.1 0.7 copy-done.3
  136.3 1.5 reshape.345
  137.8 4.3 %all-to-all-start.4 = ((f32[32,1,2600]{2,1,0:T(1,128)}), f32[32,1,2600]{2,1,0:T(1,128)S(1)}, u32[]{:S(2)}, u32[]{:S(2)}) async-start(f32[32,1,2600]{2,1,0:T(1,128)} %reshape.345), calls=%async_computation.4 | async-start | bytes 688128 | tf_op jit(solution)/shard_map/all_to_all | solution.py:195
  143.5 0.7 multiply_subtract_fusion
  144.2 23.9 %all-to-all-done.4 = f32[32,1,2600]{2,1,0:T(1,128)S(1)} async-done(((f32[32,1,2600]{2,1,0:T(1,128)}), f32[32,1,2600]{2,1,0:T(1,128)S(1)}, u32[]{:S(2)}, u32[]{:S(2)}) %all-to-all-start.4) | async-done | bytes 332832 | tf_op jit(solution)/shard_map/all_to_all | solution.py:195
  168.1 1.5 broadcast_in_dim.124
  169.6 3.9 %all-to-all-start.6 = ((bf16[16,320,160]{1,2,0:T(8,128)(2,1)}), bf16[16,320,160]{1,2,0:T(8,128)(2,1)S(1)}, u32[]{:S(2)}, u32[]{:S(2)}) async-start(bf16[16,320,160]{1,2,0:T(8,128)(2,1)} %broadcast_in_dim.124), calls=%async_computation.6 | async-start | bytes 3932160 | tf_op jit(solution)/shard_map/all_to_all | solution.py:33
  173.5 1.8 fusion.69
  175.9 0.8 convert_element_type.56
  176.7 1.5 fusion.36
  178.2 1.9 fusion.38
  180.1 2.4 %reduce.2 = f32[32,2600]{1,0:T(8,128)S(1)} reduce(f32[32,1,2600]{2,1,0:T(1,128)} %copy-done.2, f32[]{:T(128)} %broadcast.168), dimensions={1}, to_apply=%all_to_all.26.reduce_sub_computation | reduce | bytes 665604 | tf_op jit(solution)/shard_map/all_to_all | solution.py:195
  182.6 1.3 reshape.346
  183.9 2.2 fusion.67
  186.1 1.2 copy.267
  187.9 1.2 fusion.18
  189.1 0.7 fusion.60
  189.8 0.8 fusion.53
  190.6 12.4 %all-to-all-done.6 = bf16[16,320,160]{1,2,0:T(8,128)(2,1)S(1)} async-done(((bf16[16,320,160]{1,2,0:T(8,128)(2,1)}), bf16[16,320,160]{1,2,0:T(8,128)(2,1)S(1)}, u32[]{:S(2)}, u32[]{:S(2)}) %all-to-all-start.6) | async-done | bytes 1638432 | tf_op jit(solution)/shard_map/all_to_all | solution.py:33
  203.0 0.8 broadcast_in_dim.123
  204.4 5.7 %all-to-all-start.5 = ((bf16[32,20,128]{2,1,0:T(8,128)(2,1)}), bf16[32,20,128]{2,1,0:T(8,128)(2,1)}, u32[]{:S(2)}, u32[]{:S(2)}) async-start(bf16[32,20,128]{2,1,0:T(8,128)(2,1)} %broadcast_in_dim.123), calls=%async_computation.5 | async-start | bytes 393216 | tf_op jit(solution)/shard_map/all_to_all | solution.py:33
  210.1 2.2 copy.254
  212.3 2.5 %reshape.341 = bf16[5120,160,1]{0,1,2:T(8,128)(2,1)} reshape(bf16[16,320,160]{1,0,2:T(8,128)(2,1)S(1)} %copy.254) | data formatting | bytes 3276800 | tf_op jit(solution)/shard_map/reshape | solution.py:65
  214.9 0.7 copy.255
  215.5 0.7 fusion.54
  216.3 12.7 %all-to-all-done.5 = bf16[32,20,128]{2,1,0:T(8,128)(2,1)} async-done(((bf16[32,20,128]{2,1,0:T(8,128)(2,1)}), bf16[32,20,128]{2,1,0:T(8,128)(2,1)}, u32[]{:S(2)}, u32[]{:S(2)}) %all-to-all-start.5) | async-done | bytes 163872 | tf_op jit(solution)/shard_map/all_to_all | solution.py:33
  229.0 0.9 copy.252
  230.1 2.6 %fusion.72 = f32[4,4,160]{2,1,0:T(4,128)} fusion(bf16[4,4,5120]{2,1,0:T(4,128)(2,1)S(1)} %reshape.335, bf16[5120,160,1]{0,1,2:T(8,128)(2,1)} %reshape.341), kind=kOutput, calls=%fused_computation.113 | convolution fusion | flops 26214400 | bytes 1812480 | tf_op jit(solution)/shard_map/sbc,cd->sbd/dot_general | solution.py:222
  (78 shorter events, 9.2 us)
Async XLA Ops:
  0.6 128.1 %copy-start = (bf16[4,128,1024]{2,1,0:T(8,128)(2,1)S(1)}, bf16[4,128,1024]{2,1,0:T(8,128)(2,1)}, u32[]{:S(2)}) copy-start(bf16[4,128,1024]{2,1,0:T(8,128)(2,1)} %param.18) | copy-start | bytes 3145732
  2.5 28.9 %all-to-all-start = ((f32[32,1,256]{2,1,0:T(1,128)}), f32[32,1,256]{2,1,0:T(1,128)S(1)}, u32[]{:S(2)}, u32[]{:S(2)}) async-start(f32[32,1,256]{2,1,0:T(1,128)} %reshape.343), calls=%async_computation | async-start | bytes 65536 | tf_op jit(solution)/shard_map/all_to_all | solution.py:70
  34.5 5.7 %copy-start.14 = (bf16[448]{0:T(512)(128)(2,1)S(1)}, bf16[448]{0:T(512)(128)(2,1)}, u32[]{:S(2)}) copy-start(bf16[448]{0:T(512)(128)(2,1)} %param.14) | copy-start | bytes 2692
  35.4 38.2 %all-to-all-start.1 = ((f32[32,16,224]{2,1,0:T(8,128)}), f32[32,16,224]{2,1,0:T(8,128)S(1)}, u32[]{:S(2)}, u32[]{:S(2)}) async-start(f32[32,16,224]{2,1,0:T(8,128)} %bitcast.3), calls=%async_computation.1 | async-start | bytes 1048576 | tf_op jit(solution)/shard_map/all_to_all | solution.py:89
  40.1 53.9 %copy-start.15 = (s32[4]{0:T(128)S(1)}, s32[4]{0:T(128)}, u32[]{:S(2)}) copy-start(s32[4]{0:T(128)} %param.21) | copy-start | bytes 52
  40.1 54.2 %copy-start.6 = (bf16[1,384,1024]{2,1,0:T(8,128)(2,1)S(1)}, bf16[1,384,1024]{2,1,0:T(8,128)(2,1)}, u32[]{:S(2)}) copy-start(bf16[1,384,1024]{2,1,0:T(8,128)(2,1)} %param.16) | copy-start | bytes 2359300
  87.6 39.3 %all-to-all-start.3 = ((f32[32,16,224]{2,1,0:T(8,128)}), f32[32,16,224]{2,1,0:T(8,128)S(1)}, u32[]{:S(2)}, u32[]{:S(2)}) async-start(f32[32,16,224]{2,1,0:T(8,128)} %broadcast_in_dim.114), calls=%async_computation.3 | async-start | bytes 1048576 | tf_op jit(solution)/shard_map/all_to_all | solution.py:33
  97.3 31.5 %copy-start.12 = (pred[4,128]{1,0:T(4,128)(4,1)}, pred[4,128]{1,0:T(4,128)(4,1)S(1)}, u32[]{:S(2)}) copy-start(pred[4,128]{1,0:T(4,128)(4,1)S(1)} %broadcast_compare_fusion) | copy-start | bytes 1540
  128.5 1.1 copy-start.10
  128.7 1.5 copy-start.5
  129.5 0.7 copy-start.13
  129.5 1.2 copy-start.4
  131.2 2.0 copy-start.11
  134.8 1.0 copy-start.3
  136.3 31.8 %copy-start.9 = (bf16[320,160]{0,1:T(8,128)(2,1)S(1)}, bf16[320,160]{0,1:T(8,128)(2,1)}, u32[]{:S(2)}) copy-start(bf16[320,160]{0,1:T(8,128)(2,1)} %param.15) | copy-start | bytes 307204
  137.8 30.3 %all-to-all-start.4 = ((f32[32,1,2600]{2,1,0:T(1,128)}), f32[32,1,2600]{2,1,0:T(1,128)S(1)}, u32[]{:S(2)}, u32[]{:S(2)}) async-start(f32[32,1,2600]{2,1,0:T(1,128)} %reshape.345), calls=%async_computation.4 | async-start | bytes 688128 | tf_op jit(solution)/shard_map/all_to_all | solution.py:195
  168.1 1.5 copy-start.2
  169.6 33.4 %all-to-all-start.6 = ((bf16[16,320,160]{1,2,0:T(8,128)(2,1)}), bf16[16,320,160]{1,2,0:T(8,128)(2,1)S(1)}, u32[]{:S(2)}, u32[]{:S(2)}) async-start(bf16[16,320,160]{1,2,0:T(8,128)(2,1)} %broadcast_in_dim.124), calls=%async_computation.6 | async-start | bytes 3932160 | tf_op jit(solution)/shard_map/all_to_all | solution.py:33
  203.0 1.4 copy-start.1
  204.4 24.6 %all-to-all-start.5 = ((bf16[32,20,128]{2,1,0:T(8,128)(2,1)}), bf16[32,20,128]{2,1,0:T(8,128)(2,1)}, u32[]{:S(2)}, u32[]{:S(2)}) async-start(bf16[32,20,128]{2,1,0:T(8,128)(2,1)} %broadcast_in_dim.123), calls=%async_computation.5 | async-start | bytes 393216 | tf_op jit(solution)/shard_map/all_to_all | solution.py:33
  212.3 2.6 %copy-start.8 = (f32[4,4,1024]{2,0,1:T(4,128)S(1)}, f32[4,4,1024]{2,0,1:T(4,128)}, u32[]{:S(2)}) copy-start(f32[4,4,1024]{2,0,1:T(4,128)} %get-tuple-element.30) | copy-start | bytes 196612
  212.3 3.2 %copy-start.7 = (f32[4,4,8,64]{3,0,2,1:T(4,128)S(1)}, f32[4,4,8,64]{3,0,2,1:T(4,128)}, u32[]{:S(2)}) copy-start(f32[4,4,8,64]{3,0,2,1:T(4,128)} %get-tuple-element.35) | copy-start | bytes 98308

commit v3 on v1

--- a/solution.py
+++ b/solution.py
@@ -10,6 +10,7 @@
 KEY_COLUMNS = 1024
 
 
+SEQ = ("z", "core")
 epsilon = 1e-06
 masked_fill = -1e30
 
@@ -41,7 +42,7 @@
     prefix_lens,
     suffix_lens,
 ):
-    seq_count = lax.axis_size("seq")
+    seq_count = lax.axis_size(SEQ)
     tensor_count = lax.axis_size("tensor")
     steps = hidden.shape[0]
     request_total = hidden.shape[1]
@@ -53,7 +54,7 @@
     query_width = QUERY_HEADS * HEAD_SIZE
     query_rows = steps * query_group_width
     scale = float(HEAD_SIZE) ** (-0.5)
-    seq_index = lax.axis_index("seq")
+    seq_index = lax.axis_index(SEQ)
 
     w_out_cols = lax.all_gather(w_out, "tensor", axis=0, tiled=True)
 
@@ -62,7 +63,7 @@
     squares = jnp.sum(
         lax.all_to_all(
             jnp.broadcast_to(local_squares[None], (seq_count,) + local_squares.shape),
-            "seq", 0, 0, tiled=True,
+            SEQ, 0, 0, tiled=True,
         ),
         axis=0,
     )
@@ -74,18 +75,20 @@
     halves = seq_count // (steps * requests)
     half_width = columns // halves
     groups = request_total // requests
-    chunks = (
-        partial_value.reshape(steps, groups, requests, halves, half_width)
-        .transpose(0, 2, 3, 1, 4)
-        .reshape(seq_count, groups, half_width)
-    )
-    reduced = jnp.sum(lax.all_to_all(chunks, "seq", 0, 0, tiled=True), axis=0)
+    core = lax.axis_index("core")
+    plane_count = seq_count // halves
+    by_half = partial_value.reshape(steps, groups, requests, halves, half_width)
+    keep = lax.dynamic_index_in_dim(by_half, core, axis=3, keepdims=False)
+    send = lax.dynamic_index_in_dim(by_half, 1 - core, axis=3, keepdims=False)
+    pair_sum = keep + lax.ppermute(send, "core", [(0, 1), (1, 0)])
+    chunks = pair_sum.transpose(0, 2, 1, 3).reshape(plane_count, groups, half_width)
+    reduced = jnp.sum(lax.all_to_all(chunks, "z", 0, 0, tiled=True), axis=0)
     bias = lax.dynamic_slice_in_dim(
         b_qkv.astype(jnp.float32), (seq_index % halves) * half_width, half_width
     )
     reduced = reduced + bias[None, :]
     owned_rows = lax.all_to_all(reduced, "tensor", 0, 0, tiled=True)
-    gathered = lax.all_gather(owned_rows, "seq", axis=0, tiled=False)
+    gathered = lax.all_gather(owned_rows, SEQ, axis=0, tiled=False)
     combined_output = (
         gathered.reshape(steps, requests, halves, tensor_count, half_width)
         .transpose(0, 1, 3, 2, 4)
@@ -184,8 +187,20 @@
 
     packed = jnp.concatenate(
         [local_acc, local_max[..., None], local_weight[..., None]], axis=-1
-    ).reshape(seq_count, query_rows, HEAD_SIZE + 2)
-    arrived = lax.all_to_all(packed, "seq", 0, 0, tiled=True)
+    ).reshape(requests, KEY_HEADS // 2, 2, query_rows, HEAD_SIZE + 2)
+    keep = lax.dynamic_index_in_dim(packed, core, axis=2, keepdims=False)
+    came = lax.ppermute(
+        lax.dynamic_index_in_dim(packed, 1 - core, axis=2, keepdims=False), "core", [(0, 1), (1, 0)]
+    )
+    pair_max = jnp.maximum(keep[..., HEAD_SIZE], came[..., HEAD_SIZE])
+    keep_factor = jnp.exp(keep[..., HEAD_SIZE] - pair_max)
+    came_factor = jnp.exp(came[..., HEAD_SIZE] - pair_max)
+    pair_weight = keep[..., HEAD_SIZE + 1] * keep_factor + came[..., HEAD_SIZE + 1] * came_factor
+    pair_acc = keep[..., :HEAD_SIZE] * keep_factor[..., None] + came[..., :HEAD_SIZE] * came_factor[..., None]
+    pair_packed = jnp.concatenate(
+        [pair_acc, pair_max[..., None], pair_weight[..., None]], axis=-1
+    ).reshape(seq_count // 2, query_rows, HEAD_SIZE + 2)
+    arrived = lax.all_to_all(pair_packed, "z", 0, 0, tiled=True)
     part_acc = arrived[..., :HEAD_SIZE]
     part_max = arrived[..., HEAD_SIZE]
     part_weight = arrived[..., HEAD_SIZE + 1]
@@ -206,7 +221,7 @@
     summed = global_acc * factor_old[..., None] + own_new_acc * factor_new[..., None]
     attention_slice = (summed / total[..., None]).astype(jnp.bfloat16)
 
-    attention_all = lax.all_gather(attention_slice, "seq", axis=0, tiled=False)
+    attention_all = lax.all_gather(attention_slice, SEQ, axis=0, tiled=False)
     heads_local = (
         attention_all.reshape(requests, KEY_HEADS, steps, query_group_width, HEAD_SIZE)
         .transpose(2, 0, 1, 3, 4)
@@ -218,22 +233,25 @@
 
 def solution(mesh):
     placed = (
-        P(None, None, "seq"),
-        P("seq"),
-        P("seq", "tensor"),
+        P(None, None, SEQ),
+        P(SEQ),
+        P(SEQ, "tensor"),
         P("tensor"),
-        P("tensor", "seq"),
-        P("tensor", "seq", None),
-        P("tensor", "seq", None),
-        P("tensor", "seq", None),
-        P("tensor", "seq", None),
+        P("tensor", SEQ),
+        P("tensor", SEQ, None),
+        P("tensor", SEQ, None),
+        P("tensor", SEQ, None),
+        P("tensor", SEQ, None),
         P("tensor"),
         P("tensor"),
     )
+    planes = jax.sharding.Mesh(
+        mesh.devices.reshape(-1, 2, mesh.devices.shape[1]), ("z", "core", "tensor")
+    )
     return jax.shard_map(
         body,
-        mesh=mesh,
+        mesh=planes,
         in_specs=placed,
-        out_specs=(P(None, "tensor", "seq"), P("tensor", None, None), P("tensor", None, None)),
+        out_specs=(P(None, "tensor", ("z", "core")), P("tensor", None, None), P("tensor", None, None)),
         check_vma=False,
     )

time: 209 us -> 205 us (0.981)
  waiting for transfers between devices: 65.9 us -> 41.2 us
  blocking collectives: 57.9 us -> 72.1 us
  starting transfers between devices: 33.3 us -> 36.7 us
  other arithmetic: 10.3 us -> 12.6 us
    all_to_all x2, waiting for transfers between devices: 49.8 us -> 24.1 us  [the longest x1 14.2 us: body(): reduced = jnp.sum(lax.all_to_all(chunks, 'z', 0, 0, tiled=True), axis=0)]
    all_gather x2, blocking collectives: 57.9 us -> 72.1 us  [the longest x1 38.1 us: body(): gathered = lax.all_gather(owned_rows, SEQ, axis=0, tiled=False)]
    ppermute x0 -> x2, starting transfers between devices: none -> 5.24 us  [the longest x1 3.16 us: body(): pair_sum = keep + lax.ppermute(send, 'core', [(0, 1), (1, 0)])]
    unnamed x30 -> x41, local copies, waits for them, and re-layouts: 10.7 us -> 7.92 us
    add x0 -> x2, other arithmetic: none -> 2.72 us  [the longest x1 1.95 us: body(): keep[..., :HEAD_SIZE] * keep_factor[..., None]]
  transfers between devices with their start and end apart: 5 -> 7, of which waited for: 4 -> 5; matrix products, arithmetic and copies ran while one was open for 11% -> 14% of each run, Pallas kernels for 0% -> 0%
where the time goes in v3:
time: 205 us; the launch traced here: 204 us
  blocking collectives  72.1 us (35%)
  waiting for transfers between devices  41.2 us (20%)
  starting transfers between devices  36.7 us (18%)
  local copies, waits for them, and re-layouts  19.4 us (9%)
  between operations  15.3 us (7%)
  other arithmetic  12.6 us (6%)
  matrix products  6.72 us (3%)
    all_gather x1, blocking collectives, body(): gathered = lax.all_gather(owned_rows, SEQ, axis=0, tiled=False)  38.1 us
    all_gather x1, blocking collectives, body(): attention_all = lax.all_gather(attention_slice, SEQ, axis=0, tiled=False)  33.9 us
    all_to_all x1, starting transfers between devices, body(): lax.all_to_all(jnp.broadcast_to(local_squares[None], (seq_count,) + local...  16.7 us
    all_to_all x1, waiting for transfers between devices, body(): reduced = jnp.sum(lax.all_to_all(chunks, 'z', 0, 0, tiled=True), axis=0)  14.2 us
    all_to_all x1, waiting for transfers between devices, body(): lax.all_to_all(jnp.broadcast_to(local_squares[None], (seq_count,) + local...  10.7 us
    all_to_all x1, waiting for transfers between devices, body(): arrived = lax.all_to_all(pair_packed, 'z', 0, 0, tiled=True)  9.89 us
    unnamed x41, local copies, waits for them, and re-layouts  7.92 us
    all_to_all x1, starting transfers between devices, body(): owned_rows = lax.all_to_all(reduced, 'tensor', 0, 0, tiled=True)  6.76 us
  transfers between devices with their start and end apart: 7, of which 5 were waited for; matrix products, arithmetic and copies ran while one was open for 14% of the time, Pallas kernels for 0%

profile of v3, /device:TPU:1, one launch (start us, length us, event | category | flops | bytes accessed | tf_op | source)
XLA Modules:
  0.0 204.0 jit_solution(13018555632621278587)
XLA Ops:
  7.2 1.1 fusion.19
  8.3 0.7 reshape.381
  9.0 16.7 %all-to-all-start = ((f32[32,1,256]{2,1,0:T(1,128)}), f32[32,1,256]{2,1,0:T(1,128)S(1)}, u32[]{:S(2)}, u32[]{:S(2)}) async-start(f32[32,1,256]{2,1,0:T(1,128)} %reshape.381), calls=%async_computation | async-start | bytes 65536 | tf_op jit(solution)/shard_map/all_to_all | solution.py:64
  25.8 0.7 all-gather.4.cloned.1.call-update
  26.5 0.7 convert_element_type.50
  27.2 10.7 %all-to-all-done = f32[32,1,256]{2,1,0:T(1,128)S(1)} async-done(((f32[32,1,256]{2,1,0:T(1,128)}), f32[32,1,256]{2,1,0:T(1,128)S(1)}, u32[]{:S(2)}, u32[]{:S(2)}) %all-to-all-start) | async-done | bytes 32800 | tf_op jit(solution)/shard_map/all_to_all | solution.py:64
  37.9 0.5 broadcast.195
  38.4 0.6 reduce.1
  39.2 1.2 fusion.27
  40.5 0.4 reshape.360
  40.9 0.5 constant_dynamic-slice_fusion.5
  41.5 3.2 %collective-permute-start = (f32[4,16,4,224]{3,1,2,0:T(8,128)S(1)}, f32[4,16,4,224]{3,1,2,0:T(8,128)S(1)}, u32[]{:S(2)}, u32[]{:S(2)}) collective-permute-start(f32[4,16,4,224]{3,1,2,0:T(8,128)S(1)} %bitcast.133), channel_id=1, source_target_pairs={{0,16},{16,0},{1,17},{17,1},{2,18},{18,2},{3,19},{19,3},{4,20},{20... | collective-permute-start | bytes 688136 | tf_op jit(solution)/shard_map/ppermute | solution.py:83
  45.4 0.5 iota_compare_fusion
  45.9 0.8 bitcast_add_fusion
  46.7 3.7 %all-to-all-start.1 = ((f32[16,16,224]{2,1,0:T(8,128)}), f32[16,16,224]{2,1,0:T(8,128)S(1)}, u32[]{:S(2)}, u32[]{:S(2)}) async-start(f32[16,16,224]{2,1,0:T(8,128)} %bitcast.5), calls=%async_computation.1 | async-start | bytes 524288 | tf_op jit(solution)/shard_map/all_to_all | solution.py:85
  50.7 14.2 %all-to-all-done.1 = f32[16,16,224]{2,1,0:T(8,128)S(1)} async-done(((f32[16,16,224]{2,1,0:T(8,128)}), f32[16,16,224]{2,1,0:T(8,128)S(1)}, u32[]{:S(2)}, u32[]{:S(2)}) %all-to-all-start.1) | async-done | bytes 229408 | tf_op jit(solution)/shard_map/all_to_all | solution.py:85
  64.9 0.6 reshape_add_fusion
  65.5 6.8 %all-to-all-start.2 = ((f32[16,1,224]{2,1,0:T(1,128)}), f32[16,1,224]{2,1,0:T(1,128)S(1)}, u32[]{:S(2)}, u32[]{:S(2)}) async-start(f32[16,1,224]{2,1,0:T(1,128)} %reshape_add_fusion), calls=%async_computation.2 | async-start | bytes 32768 | tf_op jit(solution)/shard_map/all_to_all | solution.py:90
  72.5 1.1 copy.404
  73.6 5.1 %all-to-all-done.2 = f32[16,1,224]{2,1,0:T(1,128)S(1)} async-done(((f32[16,1,224]{2,1,0:T(1,128)}), f32[16,1,224]{2,1,0:T(1,128)S(1)}, u32[]{:S(2)}, u32[]{:S(2)}) %all-to-all-start.2) | async-done | bytes 14368 | tf_op jit(solution)/shard_map/all_to_all | solution.py:90
  78.7 38.1 %all-gather = f32[512,1,224]{2,0,1:T(8,128)S(1)} all-gather(f32[16,1,224]{2,0,1:T(8,128)S(1)} %copy.342), channel_id=2, replica_groups=mesh['z'=16,'core'=2,'tensor'=16] {'z','core'}, dimensions={0}, use_global_device_ids=true | all-gather | bytes 473088 | tf_op jit(solution)/shard_map/all_gather | solution.py:91
  116.8 0.4 copy.343
  117.2 0.8 reshape.363
  118.1 0.7 slice_bitcast_fusion.1
  119.4 0.7 fusion.65
  120.1 0.7 fusion.66
  120.8 0.4 fusion.9
  121.3 0.5 convolution_bitcast_fusion
  124.2 0.7 copy.362
  124.9 2.1 %collective-permute-start.1 = (f32[4,4,20,130]{3,1,2,0:T(4,128)S(1)}, f32[4,4,20,130]{3,1,2,0:T(4,128)S(1)}, u32[]{:S(2)}, u32[]{:S(2)}) collective-permute-start(f32[4,4,20,130]{3,1,2,0:T(4,128)S(1)} %get-tuple-element.32), channel_id=1, source_target_pairs={{0,16},{16,0},{1,17},{17,1},{2,18},{18,2},{3,19},{19,3},{4,20},{20... | collective-permute-start | bytes 499208 | tf_op jit(solution)/shard_map/ppermute | solution.py:192
  127.1 0.7 multiply_subtract_fusion
  127.8 0.6 collective-permute-done.1
  129.0 0.6 fusion.49
  129.6 0.6 fusion.48
  130.5 0.4 copy.365
  130.9 1.9 fusion.8
  132.9 1.6 copy.366
  135.3 1.1 reshape.383
  136.3 4.2 %all-to-all-start.3 = ((f32[16,1,2600]{2,1,0:T(1,128)}), f32[16,1,2600]{2,1,0:T(1,128)S(1)}, u32[]{:S(2)}, u32[]{:S(2)}) async-start(f32[16,1,2600]{2,1,0:T(1,128)} %reshape.383), calls=%async_computation.3 | async-start | bytes 344064 | tf_op jit(solution)/shard_map/all_to_all | solution.py:203
  140.9 0.9 slice.106
  141.8 0.7 copy.381
  142.8 0.7 fusion.43
  143.6 9.9 %all-to-all-done.3 = f32[16,1,2600]{2,1,0:T(1,128)S(1)} async-done(((f32[16,1,2600]{2,1,0:T(1,128)}), f32[16,1,2600]{2,1,0:T(1,128)S(1)}, u32[]{:S(2)}, u32[]{:S(2)}) %all-to-all-start.3) | async-done | bytes 166432 | tf_op jit(solution)/shard_map/all_to_all | solution.py:203
  153.5 1.0 reduce.2
  155.6 33.9 %all_gather.15 = bf16[32,20,128]{2,1,0:T(8,128)(2,1)S(1)} all-gather(bf16[1,20,128]{2,1,0:T(8,128)(2,1)S(1)} %copy.377), channel_id=1, replica_groups=mesh['z'=16,'core'=2,'tensor'=16] {'z','core'}, dimensions={0}, use_global_device_ids=true | all-gather | bytes 168960 | tf_op jit(solution)/shard_map/all_gather | solution.py:224
  189.8 2.2 %copy.380 = bf16[16,320,160]{1,0,2:T(8,128)(2,1)S(1)} copy(bf16[16,320,160]{1,2,0:T(8,128)(2,1)} %all-gather.4.cloned.1.call-done) | data formatting | bytes 3276800 | tf_op jit(solution)/shard_map/all_gather | solution.py:59
  192.0 2.5 %reshape.379 = bf16[5120,160,1]{0,1,2:T(8,128)(2,1)} reshape(bf16[16,320,160]{1,0,2:T(8,128)(2,1)S(1)} %copy.380) | data formatting | bytes 3276800
  194.6 2.6 %fusion.67 = f32[4,4,160]{2,1,0:T(4,128)} fusion(bf16[4,4,5120]{2,1,0:T(4,128)(2,1)S(1)} %reshape.370, bf16[5120,160,1]{0,1,2:T(8,128)(2,1)} %reshape.379), kind=kOutput, calls=%fused_computation.122 | convolution fusion | flops 26214400 | bytes 1812480 | tf_op jit(solution)/shard_map/sbc,cd->sbd/dot_general | solution.py:230
  (93 shorter events, 7.5 us)
Async XLA Ops:
  7.2 112.9 %copy-start = (bf16[4,128,1024]{2,1,0:T(8,128)(2,1)S(1)}, bf16[4,128,1024]{2,1,0:T(8,128)(2,1)}, u32[]{:S(2)}) copy-start(bf16[4,128,1024]{2,1,0:T(8,128)(2,1)} %param.18) | copy-start | bytes 3145732
  9.0 28.9 %all-to-all-start = ((f32[32,1,256]{2,1,0:T(1,128)}), f32[32,1,256]{2,1,0:T(1,128)S(1)}, u32[]{:S(2)}, u32[]{:S(2)}) async-start(f32[32,1,256]{2,1,0:T(1,128)} %reshape.381), calls=%async_computation | async-start | bytes 65536 | tf_op jit(solution)/shard_map/all_to_all | solution.py:64
  25.8 164.0 %all-gather.4.cloned.1.call-start = ((), (), s32[]{:S(2)}) async-start(), calls=%async_computation.4 | async-start | bytes 2088960 | tf_op jit(solution)/shard_map/all_gather | solution.py:59
  40.5 4.9 %copy-start.12 = (bf16[448]{0:T(512)(128)(2,1)S(1)}, bf16[448]{0:T(512)(128)(2,1)}, u32[]{:S(2)}) copy-start(bf16[448]{0:T(512)(128)(2,1)} %param.14) | copy-start | bytes 2692
  41.4 9.0 %copy-start.13 = (s32[4]{0:T(128)S(1)}, s32[4]{0:T(128)}, u32[]{:S(2)}) copy-start(s32[4]{0:T(128)} %param.21) | copy-start | bytes 52
  41.4 30.9 %copy-start.3 = (bf16[1,384,1024]{2,1,0:T(8,128)(2,1)S(1)}, bf16[1,384,1024]{2,1,0:T(8,128)(2,1)}, u32[]{:S(2)}) copy-start(bf16[1,384,1024]{2,1,0:T(8,128)(2,1)} %param.16) | copy-start | bytes 2359300
  41.5 4.4 %collective-permute-start = (f32[4,16,4,224]{3,1,2,0:T(8,128)S(1)}, f32[4,16,4,224]{3,1,2,0:T(8,128)S(1)}, u32[]{:S(2)}, u32[]{:S(2)}) collective-permute-start(f32[4,16,4,224]{3,1,2,0:T(8,128)S(1)} %bitcast.133), channel_id=1, source_target_pairs={{0,16},{16,0},{1,17},{17,1},{2,18},{18,2},{3,19},{19,3},{4,20},{20... | collective-permute-start | bytes 688136 | tf_op jit(solution)/shard_map/ppermute | solution.py:83
  46.7 25.8 %copy-start.4 = (bf16[1,384,1024]{2,1,0:T(8,128)(2,1)S(1)}, bf16[1,384,1024]{2,1,0:T(8,128)(2,1)}, u32[]{:S(2)}) copy-start(bf16[1,384,1024]{2,1,0:T(8,128)(2,1)} %param.17) | copy-start | bytes 2359300
  46.7 18.2 %all-to-all-start.1 = ((f32[16,16,224]{2,1,0:T(8,128)}), f32[16,16,224]{2,1,0:T(8,128)S(1)}, u32[]{:S(2)}, u32[]{:S(2)}) async-start(f32[16,16,224]{2,1,0:T(8,128)} %bitcast.5), calls=%async_computation.1 | async-start | bytes 524288 | tf_op jit(solution)/shard_map/all_to_all | solution.py:85
  65.5 13.2 %all-to-all-start.2 = ((f32[16,1,224]{2,1,0:T(1,128)}), f32[16,1,224]{2,1,0:T(1,128)S(1)}, u32[]{:S(2)}, u32[]{:S(2)}) async-start(f32[16,1,224]{2,1,0:T(1,128)} %reshape_add_fusion), calls=%async_computation.2 | async-start | bytes 32768 | tf_op jit(solution)/shard_map/all_to_all | solution.py:90
  118.1 1.3 copy-start.1
  120.0 1.2 copy-start.5
  121.3 1.2 copy-start.2
  124.9 3.5 %collective-permute-start.1 = (f32[4,4,20,130]{3,1,2,0:T(4,128)S(1)}, f32[4,4,20,130]{3,1,2,0:T(4,128)S(1)}, u32[]{:S(2)}, u32[]{:S(2)}) collective-permute-start(f32[4,4,20,130]{3,1,2,0:T(4,128)S(1)} %get-tuple-element.32), channel_id=1, source_target_pairs={{0,16},{16,0},{1,17},{17,1},{2,18},{18,2},{3,19},{19,3},{4,20},{20... | collective-permute-start | bytes 499208 | tf_op jit(solution)/shard_map/ppermute | solution.py:192
  129.6 0.6 copy-start.8
  132.9 1.6 copy-start.10
  132.9 1.8 copy-start.9
  134.9 5.6 %copy-start.6 = (f32[4,4,8,64]{3,0,2,1:T(4,128)S(1)}, f32[4,4,8,64]{3,0,2,1:T(4,128)}, u32[]{:S(2)}) copy-start(f32[4,4,8,64]{3,0,2,1:T(4,128)} %get-tuple-element.48) | copy-start | bytes 98308
  134.9 5.6 %copy-start.11 = (pred[20,4]{0,1:T(4,128)(4,1)S(1)}, pred[20,4]{0,1:T(4,128)(4,1)}, u32[]{:S(2)}) copy-start(pred[20,4]{0,1:T(4,128)(4,1)} %iota_compare_fusion) | copy-start | bytes 244
  135.1 6.7 %copy-start.7 = (f32[4,4,1024]{2,0,1:T(4,128)S(1)}, f32[4,4,1024]{2,0,1:T(4,128)}, u32[]{:S(2)}) copy-start(f32[4,4,1024]{2,0,1:T(4,128)} %get-tuple-element.36) | copy-start | bytes 196612
  136.3 17.1 %all-to-all-start.3 = ((f32[16,1,2600]{2,1,0:T(1,128)}), f32[16,1,2600]{2,1,0:T(1,128)S(1)}, u32[]{:S(2)}, u32[]{:S(2)}) async-start(f32[16,1,2600]{2,1,0:T(1,128)} %reshape.383), calls=%async_computation.3 | async-start | bytes 344064 | tf_op jit(solution)/shard_map/all_to_all | solution.py:203
Sparse Core Ops, SparseCore 0:
  29.6 59.8 all-gather.3

commit v4 on v3

--- a/solution.py
+++ b/solution.py
@@ -121,6 +121,7 @@
         .transpose(1, 2, 0, 3, 4)
         .reshape(requests, KEY_HEADS, query_rows, HEAD_SIZE)
     )
+    w_out_cols, query_by_group = lax.optimization_barrier((w_out_cols, query_by_group))
 
     prefix_key_block = prefix_key_cache[0].reshape(prefix_count, KEY_HEADS, HEAD_SIZE)
     prefix_value_block = prefix_value_cache[0].reshape(prefix_count, KEY_HEADS, HEAD_SIZE)
@@ -185,25 +186,45 @@
         preferred_element_type=jnp.float32,
     )
 
+    lane_pad = ((0, 0), (0, 0), (0, HEAD_SIZE - query_rows))
     packed = jnp.concatenate(
-        [local_acc, local_max[..., None], local_weight[..., None]], axis=-1
-    ).reshape(requests, KEY_HEADS // 2, 2, query_rows, HEAD_SIZE + 2)
+        [
+            local_acc,
+            jnp.pad(local_max, lane_pad)[:, :, None, :],
+            jnp.pad(local_weight, lane_pad)[:, :, None, :],
+        ],
+        axis=2,
+    ).reshape(requests, KEY_HEADS // 2, 2, query_rows + 2, HEAD_SIZE)
     keep = lax.dynamic_index_in_dim(packed, core, axis=2, keepdims=False)
     came = lax.ppermute(
         lax.dynamic_index_in_dim(packed, 1 - core, axis=2, keepdims=False), "core", [(0, 1), (1, 0)]
     )
-    pair_max = jnp.maximum(keep[..., HEAD_SIZE], came[..., HEAD_SIZE])
-    keep_factor = jnp.exp(keep[..., HEAD_SIZE] - pair_max)
-    came_factor = jnp.exp(came[..., HEAD_SIZE] - pair_max)
-    pair_weight = keep[..., HEAD_SIZE + 1] * keep_factor + came[..., HEAD_SIZE + 1] * came_factor
-    pair_acc = keep[..., :HEAD_SIZE] * keep_factor[..., None] + came[..., :HEAD_SIZE] * came_factor[..., None]
+    keep_max = keep[..., query_rows, :query_rows]
+    came_max = came[..., query_rows, :query_rows]
+    pair_max = jnp.maximum(keep_max, came_max)
+    keep_factor = jnp.exp(keep_max - pair_max)
+    came_factor = jnp.exp(came_max - pair_max)
+    pair_weight = (
+        keep[..., query_rows + 1, :query_rows] * keep_factor
+        + came[..., query_rows + 1, :query_rows] * came_factor
+    )
+    pair_acc = (
+        keep[..., :query_rows, :] * keep_factor[..., None]
+        + came[..., :query_rows, :] * came_factor[..., None]
+    )
+    pad_rows = ((0, 0), (0, 0), (0, HEAD_SIZE - query_rows))
     pair_packed = jnp.concatenate(
-        [pair_acc, pair_max[..., None], pair_weight[..., None]], axis=-1
-    ).reshape(seq_count // 2, query_rows, HEAD_SIZE + 2)
+        [
+            pair_acc,
+            jnp.pad(pair_max, pad_rows)[:, :, None, :],
+            jnp.pad(pair_weight, pad_rows)[:, :, None, :],
+        ],
+        axis=2,
+    ).reshape(seq_count // 2, query_rows + 2, HEAD_SIZE)
     arrived = lax.all_to_all(pair_packed, "z", 0, 0, tiled=True)
-    part_acc = arrived[..., :HEAD_SIZE]
-    part_max = arrived[..., HEAD_SIZE]
-    part_weight = arrived[..., HEAD_SIZE + 1]
+    part_acc = arrived[:, :query_rows, :]
+    part_max = arrived[:, query_rows, :query_rows]
+    part_weight = arrived[:, query_rows + 1, :query_rows]
     global_max = jnp.max(part_max, axis=0)
     factor = jnp.exp(part_max - global_max[None])
     global_weight = jnp.sum(part_weight * factor, axis=0)

time: 205 us -> 198 us (0.966)
  other arithmetic: 12.6 us -> 8.59 us
  local copies, waits for them, and re-layouts: 19.4 us -> 16 us
    unnamed x41 -> x37, local copies, waits for them, and re-layouts: 7.92 us -> 5 us
    optimization_barrier x0 -> x1, local copies, waits for them, and re-layouts: none -> 2.54 us  [body(): lax.optimization_barrier((w_out_cols, query_by_group))]
    all_to_all x1, waiting for transfers between devices: 9.89 us -> 12.2 us  [body(): arrived = lax.all_to_all(pair_packed, 'z', 0, 0, tiled=True)]
  transfers between devices with their start and end apart: 7 -> 7, of which waited for: 5 -> 4; matrix products, arithmetic and copies ran while one was open for 14% -> 9% of each run, Pallas kernels for 0% -> 0%
where the time goes in v4:
time: 198 us
  blocking collectives  73.1 us (37%)
  waiting for transfers between devices  41.6 us (21%)
  starting transfers between devices  36.7 us (19%)
  local copies, waits for them, and re-layouts  16 us (8%)
  between operations  15.2 us (8%)
  other arithmetic  8.59 us (4%)
  matrix products  6.3 us (3%)
    all_gather x1, blocking collectives, body(): gathered = lax.all_gather(owned_rows, SEQ, axis=0, tiled=False)  38.1 us
    all_gather x1, blocking collectives, body(): attention_all = lax.all_gather(attention_slice, SEQ, axis=0, tiled=False)  35 us
    all_to_all x1, starting transfers between devices, body(): lax.all_to_all(jnp.broadcast_to(local_squares[None], (seq_count,) + local...  16.7 us
    all_to_all x1, waiting for transfers between devices, body(): reduced = jnp.sum(lax.all_to_all(chunks, 'z', 0, 0, tiled=True), axis=0)  13.6 us
    all_to_all x1, waiting for transfers between devices, body(): arrived = lax.all_to_all(pair_packed, 'z', 0, 0, tiled=True)  12.2 us
    all_to_all x1, waiting for transfers between devices, body(): lax.all_to_all(jnp.broadcast_to(local_squares[None], (seq_count,) + local...  11.4 us
    all_to_all x1, starting transfers between devices, body(): owned_rows = lax.all_to_all(reduced, 'tensor', 0, 0, tiled=True)  6.77 us
    unnamed x37, local copies, waits for them, and re-layouts  5 us
  transfers between devices with their start and end apart: 7, of which 4 were waited for; matrix products, arithmetic and copies ran while one was open for 9% of the time, Pallas kernels for 0%

profile of v4, /device:TPU:1, one launch (start us, length us, event | category | flops | bytes accessed | tf_op | source)
XLA Modules:
  0.0 197.5 jit_solution(17961246166062307471)
XLA Ops:
  7.2 0.7 all-gather.4.cloned.1.call-update
  7.9 1.0 fusion.20
  9.0 0.7 reshape.382
  9.7 16.7 %all-to-all-start = ((f32[32,1,256]{2,1,0:T(1,128)}), f32[32,1,256]{2,1,0:T(1,128)S(1)}, u32[]{:S(2)}, u32[]{:S(2)}) async-start(f32[32,1,256]{2,1,0:T(1,128)} %reshape.382), calls=%async_computation | async-start | bytes 65536 | tf_op jit(solution)/shard_map/all_to_all | solution.py:64
  26.5 0.7 convert_element_type.56
  27.1 11.4 %all-to-all-done = f32[32,1,256]{2,1,0:T(1,128)S(1)} async-done(((f32[32,1,256]{2,1,0:T(1,128)}), f32[32,1,256]{2,1,0:T(1,128)S(1)}, u32[]{:S(2)}, u32[]{:S(2)}) %all-to-all-start) | async-done | bytes 32800 | tf_op jit(solution)/shard_map/all_to_all | solution.py:64
  38.5 0.5 broadcast.207
  39.1 0.7 reduce.1
  39.9 1.3 fusion.29
  41.2 0.4 reshape.362
  41.7 0.5 constant_dynamic-slice_fusion.4
  42.2 3.2 %collective-permute-start = (f32[4,16,4,224]{3,1,2,0:T(8,128)S(1)}, f32[4,16,4,224]{3,1,2,0:T(8,128)S(1)}, u32[]{:S(2)}, u32[]{:S(2)}) collective-permute-start(f32[4,16,4,224]{3,1,2,0:T(8,128)S(1)} %bitcast.150), channel_id=1, source_target_pairs={{0,16},{16,0},{1,17},{17,1},{2,18},{18,2},{3,19},{19,3},{4,20},{20... | collective-permute-start | bytes 688136 | tf_op jit(solution)/shard_map/ppermute | solution.py:83
  46.2 0.5 iota_compare_fusion
  46.7 0.8 bitcast_add_fusion
  47.5 3.7 %all-to-all-start.1 = ((f32[16,16,224]{2,1,0:T(8,128)}), f32[16,16,224]{2,1,0:T(8,128)S(1)}, u32[]{:S(2)}, u32[]{:S(2)}) async-start(f32[16,16,224]{2,1,0:T(8,128)} %bitcast.6), calls=%async_computation.1 | async-start | bytes 524288 | tf_op jit(solution)/shard_map/all_to_all | solution.py:85
  51.2 0.6 broadcast_compare_fusion
  52.0 13.6 %all-to-all-done.1 = f32[16,16,224]{2,1,0:T(8,128)S(1)} async-done(((f32[16,16,224]{2,1,0:T(8,128)}), f32[16,16,224]{2,1,0:T(8,128)S(1)}, u32[]{:S(2)}, u32[]{:S(2)}) %all-to-all-start.1) | async-done | bytes 229408 | tf_op jit(solution)/shard_map/all_to_all | solution.py:85
  65.7 0.6 reshape_add_fusion
  66.3 6.8 %all-to-all-start.2 = ((f32[16,1,224]{2,1,0:T(1,128)}), f32[16,1,224]{2,1,0:T(1,128)S(1)}, u32[]{:S(2)}, u32[]{:S(2)}) async-start(f32[16,1,224]{2,1,0:T(1,128)} %reshape_add_fusion), calls=%async_computation.2 | async-start | bytes 32768 | tf_op jit(solution)/shard_map/all_to_all | solution.py:90
  73.1 0.5 add_compare_fusion
  73.6 1.1 copy.295
  74.7 1.1 copy.296
  75.8 3.7 %all-to-all-done.2 = f32[16,1,224]{2,1,0:T(1,128)S(1)} async-done(((f32[16,1,224]{2,1,0:T(1,128)}), f32[16,1,224]{2,1,0:T(1,128)S(1)}, u32[]{:S(2)}, u32[]{:S(2)}) %all-to-all-start.2) | async-done | bytes 14368 | tf_op jit(solution)/shard_map/all_to_all | solution.py:90
  79.5 38.1 %all-gather = f32[512,1,224]{2,0,1:T(8,128)S(1)} all-gather(f32[16,1,224]{2,0,1:T(8,128)S(1)} %copy.236), channel_id=2, replica_groups=mesh['z'=16,'core'=2,'tensor'=16] {'z','core'}, dimensions={0}, use_global_device_ids=true | all-gather | bytes 473088 | tf_op jit(solution)/shard_map/all_gather | solution.py:91
  117.6 0.4 copy.237
  118.1 0.8 reshape.365
  119.4 0.7 copy.242
  120.1 0.6 slice_bitcast_fusion.1
  120.7 0.7 fusion.63
  121.5 2.2 %copy.232 = bf16[16,320,160]{1,0,2:T(8,128)(2,1)S(1)} copy(bf16[16,320,160]{1,2,0:T(8,128)(2,1)} %all-gather.4.cloned.1.call-done) | data formatting | bytes 3276800 | tf_op jit(solution)/shard_map/all_gather | solution.py:59
  123.7 2.5 %reshape.377 = bf16[5120,160]{0,1:T(8,128)(2,1)} reshape(bf16[16,320,160]{1,0,2:T(8,128)(2,1)S(1)} %copy.232) | data formatting | bytes 3276800 | tf_op jit(solution)/shard_map/optimization_barrier | solution.py:124
  126.3 1.7 fusion.66
  128.0 0.7 fusion.65
  128.7 0.4 fusion.10
  129.4 0.3 fusion.18
  129.8 0.5 convolution_bitcast_fusion
  130.3 0.7 copy-done.3
  131.1 0.4 convolution_add_fusion
  131.8 2.1 %collective-permute-start.1 = (f32[4,4,22,128]{3,1,0,2:T(4,128)S(1)}, f32[4,4,22,128]{3,1,0,2:T(4,128)S(1)}, u32[]{:S(2)}, u32[]{:S(2)}) collective-permute-start(f32[4,4,22,128]{3,1,0,2:T(4,128)S(1)} %copy.260), channel_id=1, source_target_pairs={{0,16},{16,0},{1,17},{17,1},{2,18},{18,2},{3,19},{19,3},{4,20},{20... | collective-permute-start | bytes 540680 | tf_op jit(solution)/shard_map/ppermute | solution.py:199
  134.1 0.7 copy.272
  134.8 0.7 fusion.45
  136.1 0.7 copy.263
  136.8 4.2 %all-to-all-start.3 = ((f32[16,22,128]{2,1,0:T(8,128)}), f32[16,22,128]{2,1,0:T(8,128)S(1)}, u32[]{:S(2)}, u32[]{:S(2)}) async-start(f32[16,22,128]{2,1,0:T(8,128)} %copy.263), calls=%async_computation.3 | async-start | bytes 393216 | tf_op jit(solution)/shard_map/all_to_all | solution.py:224
  141.0 0.3 fusion.64
  141.3 0.3 fusion.36
  141.7 12.2 %all-to-all-done.3 = f32[16,22,128]{2,1,0:T(8,128)S(1)} async-done(((f32[16,22,128]{2,1,0:T(8,128)}), f32[16,22,128]{2,1,0:T(8,128)S(1)}, u32[]{:S(2)}, u32[]{:S(2)}) %all-to-all-start.3) | async-done | bytes 180256 | tf_op jit(solution)/shard_map/all_to_all | solution.py:224
  154.3 35.0 %all_gather.16 = bf16[32,20,128]{2,1,0:T(8,128)(2,1)S(1)} all-gather(bf16[1,20,128]{2,1,0:T(8,128)(2,1)S(1)} %copy.269), channel_id=1, replica_groups=mesh['z'=16,'core'=2,'tensor'=16] {'z','core'}, dimensions={0}, use_global_device_ids=true | all-gather | bytes 168960 | tf_op jit(solution)/shard_map/all_gather | solution.py:245
  189.5 1.2 fusion
  (85 shorter events, 3.2 us)
Async XLA Ops:
  7.2 119.1 %copy-start = (bf16[4,128,1024]{2,1,0:T(8,128)(2,1)S(1)}, bf16[4,128,1024]{2,1,0:T(8,128)(2,1)}, u32[]{:S(2)}) copy-start(bf16[4,128,1024]{2,1,0:T(8,128)(2,1)} %param.18) | copy-start | bytes 3145732
  7.2 114.3 %all-gather.4.cloned.1.call-start = ((), (), s32[]{:S(2)}) async-start(), calls=%async_computation.4 | async-start | bytes 2088960 | tf_op jit(solution)/shard_map/all_gather | solution.py:59
  9.7 28.9 %all-to-all-start = ((f32[32,1,256]{2,1,0:T(1,128)}), f32[32,1,256]{2,1,0:T(1,128)S(1)}, u32[]{:S(2)}, u32[]{:S(2)}) async-start(f32[32,1,256]{2,1,0:T(1,128)} %reshape.382), calls=%async_computation | async-start | bytes 65536 | tf_op jit(solution)/shard_map/all_to_all | solution.py:64
  41.2 4.9 %copy-start.12 = (bf16[448]{0:T(512)(128)(2,1)S(1)}, bf16[448]{0:T(512)(128)(2,1)}, u32[]{:S(2)}) copy-start(bf16[448]{0:T(512)(128)(2,1)} %param.14) | copy-start | bytes 2692
  42.1 9.0 %copy-start.14 = (s32[4]{0:T(128)S(1)}, s32[4]{0:T(128)}, u32[]{:S(2)}) copy-start(s32[4]{0:T(128)} %param.21) | copy-start | bytes 52
  42.2 31.4 %copy-start.5 = (bf16[1,384,1024]{2,1,0:T(8,128)(2,1)S(1)}, bf16[1,384,1024]{2,1,0:T(8,128)(2,1)}, u32[]{:S(2)}) copy-start(bf16[1,384,1024]{2,1,0:T(8,128)(2,1)} %param.16) | copy-start | bytes 2359300
  42.2 4.5 %collective-permute-start = (f32[4,16,4,224]{3,1,2,0:T(8,128)S(1)}, f32[4,16,4,224]{3,1,2,0:T(8,128)S(1)}, u32[]{:S(2)}, u32[]{:S(2)}) collective-permute-start(f32[4,16,4,224]{3,1,2,0:T(8,128)S(1)} %bitcast.150), channel_id=1, source_target_pairs={{0,16},{16,0},{1,17},{17,1},{2,18},{18,2},{3,19},{19,3},{4,20},{20... | collective-permute-start | bytes 688136 | tf_op jit(solution)/shard_map/ppermute | solution.py:83
  47.5 27.2 %copy-start.6 = (bf16[1,384,1024]{2,1,0:T(8,128)(2,1)S(1)}, bf16[1,384,1024]{2,1,0:T(8,128)(2,1)}, u32[]{:S(2)}) copy-start(bf16[1,384,1024]{2,1,0:T(8,128)(2,1)} %param.17) | copy-start | bytes 2359300
  47.5 18.1 %all-to-all-start.1 = ((f32[16,16,224]{2,1,0:T(8,128)}), f32[16,16,224]{2,1,0:T(8,128)S(1)}, u32[]{:S(2)}, u32[]{:S(2)}) async-start(f32[16,16,224]{2,1,0:T(8,128)} %bitcast.6), calls=%async_computation.1 | async-start | bytes 524288 | tf_op jit(solution)/shard_map/all_to_all | solution.py:85
  66.3 13.2 %all-to-all-start.2 = ((f32[16,1,224]{2,1,0:T(1,128)}), f32[16,1,224]{2,1,0:T(1,128)S(1)}, u32[]{:S(2)}, u32[]{:S(2)}) async-start(f32[16,1,224]{2,1,0:T(1,128)} %reshape_add_fusion), calls=%async_computation.2 | async-start | bytes 32768 | tf_op jit(solution)/shard_map/all_to_all | solution.py:90
  126.2 1.8 copy-start.1
  126.2 1.8 copy-start.4
  126.2 1.8 copy-start.11
  128.7 0.7 copy-start.13
  128.7 1.1 copy-start.7
  129.8 1.2 copy-start.3
  131.5 2.4 %copy-start.8 = (f32[4,4,8,64]{3,2,1,0:T(8,128)S(1)}, f32[4,4,8,64]{3,2,1,0:T(8,128)}, u32[]{:S(2)}) copy-start(f32[4,4,8,64]{3,2,1,0:T(8,128)} %get-tuple-element.49) | copy-start | bytes 98308
  131.5 2.6 %copy-start.9 = (f32[4,4,1024]{2,0,1:T(4,128)S(1)}, f32[4,4,1024]{2,0,1:T(4,128)}, u32[]{:S(2)}) copy-start(f32[4,4,1024]{2,0,1:T(4,128)} %get-tuple-element.36) | copy-start | bytes 196612
  131.8 3.7 %collective-permute-start.1 = (f32[4,4,22,128]{3,1,0,2:T(4,128)S(1)}, f32[4,4,22,128]{3,1,0,2:T(4,128)S(1)}, u32[]{:S(2)}, u32[]{:S(2)}) collective-permute-start(f32[4,4,22,128]{3,1,0,2:T(4,128)S(1)} %copy.260), channel_id=1, source_target_pairs={{0,16},{16,0},{1,17},{17,1},{2,18},{18,2},{3,19},{19,3},{4,20},{20... | collective-permute-start | bytes 540680 | tf_op jit(solution)/shard_map/ppermute | solution.py:199
  134.0 7.0 %copy-start.10 = (pred[20,4]{0,1:T(4,128)(4,1)S(1)}, pred[20,4]{0,1:T(4,128)(4,1)}, u32[]{:S(2)}) copy-start(pred[20,4]{0,1:T(4,128)(4,1)} %iota_compare_fusion) | copy-start | bytes 244
  136.8 17.2 %all-to-all-start.3 = ((f32[16,22,128]{2,1,0:T(8,128)}), f32[16,22,128]{2,1,0:T(8,128)S(1)}, u32[]{:S(2)}, u32[]{:S(2)}) async-start(f32[16,22,128]{2,1,0:T(8,128)} %copy.263), calls=%async_computation.3 | async-start | bytes 393216 | tf_op jit(solution)/shard_map/all_to_all | solution.py:224
  141.3 48.2 %copy-start.2 = (bf16[5120,160]{0,1:T(8,128)(2,1)S(1)}, bf16[5120,160]{0,1:T(8,128)(2,1)}, u32[]{:S(2)}) copy-start(bf16[5120,160]{0,1:T(8,128)(2,1)} %reshape.377) | copy-start | bytes 4915204
Sparse Core Ops, SparseCore 0:
  11.0 64.4 all-gather.3

commit v5 on v4

--- a/solution.py
+++ b/solution.py
@@ -121,7 +121,6 @@
         .transpose(1, 2, 0, 3, 4)
         .reshape(requests, KEY_HEADS, query_rows, HEAD_SIZE)
     )
-    w_out_cols, query_by_group = lax.optimization_barrier((w_out_cols, query_by_group))
 
     prefix_key_block = prefix_key_cache[0].reshape(prefix_count, KEY_HEADS, HEAD_SIZE)
     prefix_value_block = prefix_value_cache[0].reshape(prefix_count, KEY_HEADS, HEAD_SIZE)
@@ -222,6 +221,7 @@
         axis=2,
     ).reshape(seq_count // 2, query_rows + 2, HEAD_SIZE)
     arrived = lax.all_to_all(pair_packed, "z", 0, 0, tiled=True)
+    w_out_cols, arrived = lax.optimization_barrier((w_out_cols, arrived))
     part_acc = arrived[:, :query_rows, :]
     part_max = arrived[:, query_rows, :query_rows]
     part_weight = arrived[:, query_rows + 1, :query_rows]

time: 198 us -> 194 us (0.980)
  waiting for transfers between devices: 41.6 us -> 37.4 us
    all_to_all x1, waiting for transfers between devices: 12.2 us -> 6.15 us  [body(): arrived = lax.all_to_all(pair_packed, 'z', 0, 0, tiled=True)]
    unnamed x37 -> x51, local copies, waits for them, and re-layouts: 5 us -> 4.78 us
  transfers between devices with their start and end apart: 7 -> 7, of which waited for: 4 -> 5; matrix products, arithmetic and copies ran while one was open for 9% -> 15% of each run, Pallas kernels for 0% -> 0%
where the time goes in v5:
time: 194 us; the launch traced here: 193 us
  blocking collectives  72.9 us (38%)
  waiting for transfers between devices  37.4 us (19%)
  starting transfers between devices  36.6 us (19%)
  local copies, waits for them, and re-layouts  16.7 us (9%)
  between operations  15.4 us (8%)
  other arithmetic  8.05 us (4%)
  matrix products  5.98 us (3%)
    all_gather x1, blocking collectives, body(): gathered = lax.all_gather(owned_rows, SEQ, axis=0, tiled=False)  38.1 us
    all_gather x1, blocking collectives, body(): attention_all = lax.all_gather(attention_slice, SEQ, axis=0, tiled=False)  34.7 us
    all_to_all x1, starting transfers between devices, body(): lax.all_to_all(jnp.broadcast_to(local_squares[None], (seq_count,) + local...  16.7 us
    all_to_all x1, waiting for transfers between devices, body(): reduced = jnp.sum(lax.all_to_all(chunks, 'z', 0, 0, tiled=True), axis=0)  14.2 us
    all_to_all x1, waiting for transfers between devices, body(): lax.all_to_all(jnp.broadcast_to(local_squares[None], (seq_count,) + local...  11.4 us
    all_to_all x1, starting transfers between devices, body(): owned_rows = lax.all_to_all(reduced, 'tensor', 0, 0, tiled=True)  6.77 us
    all_to_all x1, waiting for transfers between devices, body(): arrived = lax.all_to_all(pair_packed, 'z', 0, 0, tiled=True)  6.15 us
    unnamed x51, local copies, waits for them, and re-layouts  4.78 us
  transfers between devices with their start and end apart: 7, of which 5 were waited for; matrix products, arithmetic and copies ran while one was open for 15% of the time, Pallas kernels for 0%

profile of v5, /device:TPU:1, one launch (start us, length us, event | category | flops | bytes accessed | tf_op | source)
XLA Modules:
  0.0 193.0 jit_solution(13204047993512027415)
XLA Ops:
  7.2 0.7 all-gather.4.cloned.1.call-update
  7.9 1.0 fusion.20
  9.0 0.7 reshape.382
  9.7 16.7 %all-to-all-start = ((f32[32,1,256]{2,1,0:T(1,128)}), f32[32,1,256]{2,1,0:T(1,128)S(1)}, u32[]{:S(2)}, u32[]{:S(2)}) async-start(f32[32,1,256]{2,1,0:T(1,128)} %reshape.382), calls=%async_computation | async-start | bytes 65536 | tf_op jit(solution)/shard_map/all_to_all | solution.py:64
  26.5 0.7 convert_element_type.56
  27.1 11.4 %all-to-all-done = f32[32,1,256]{2,1,0:T(1,128)S(1)} async-done(((f32[32,1,256]{2,1,0:T(1,128)}), f32[32,1,256]{2,1,0:T(1,128)S(1)}, u32[]{:S(2)}, u32[]{:S(2)}) %all-to-all-start) | async-done | bytes 32800 | tf_op jit(solution)/shard_map/all_to_all | solution.py:64
  38.5 0.5 broadcast.207
  39.1 0.7 reduce.1
  39.9 1.3 fusion.28
  41.2 0.4 reshape.362
  41.7 0.5 constant_dynamic-slice_fusion.4
  42.2 3.2 %collective-permute-start = (f32[4,16,4,224]{3,1,2,0:T(8,128)S(1)}, f32[4,16,4,224]{3,1,2,0:T(8,128)S(1)}, u32[]{:S(2)}, u32[]{:S(2)}) collective-permute-start(f32[4,16,4,224]{3,1,2,0:T(8,128)S(1)} %bitcast.152), channel_id=1, source_target_pairs={{0,16},{16,0},{1,17},{17,1},{2,18},{18,2},{3,19},{19,3},{4,20},{20... | collective-permute-start | bytes 688136 | tf_op jit(solution)/shard_map/ppermute | solution.py:83
  46.2 0.5 iota_compare_fusion
  46.7 0.8 bitcast_add_fusion
  47.5 3.5 %all-to-all-start.1 = ((f32[16,16,224]{2,1,0:T(8,128)}), f32[16,16,224]{2,1,0:T(8,128)S(1)}, u32[]{:S(2)}, u32[]{:S(2)}) async-start(f32[16,16,224]{2,1,0:T(8,128)} %bitcast.6), calls=%async_computation.1 | async-start | bytes 524288 | tf_op jit(solution)/shard_map/all_to_all | solution.py:85
  51.3 14.2 %all-to-all-done.1 = f32[16,16,224]{2,1,0:T(8,128)S(1)} async-done(((f32[16,16,224]{2,1,0:T(8,128)}), f32[16,16,224]{2,1,0:T(8,128)S(1)}, u32[]{:S(2)}, u32[]{:S(2)}) %all-to-all-start.1) | async-done | bytes 229408 | tf_op jit(solution)/shard_map/all_to_all | solution.py:85
  65.5 0.6 reshape_add_fusion
  66.1 6.8 %all-to-all-start.2 = ((f32[16,1,224]{2,1,0:T(1,128)}), f32[16,1,224]{2,1,0:T(1,128)S(1)}, u32[]{:S(2)}, u32[]{:S(2)}) async-start(f32[16,1,224]{2,1,0:T(1,128)} %reshape_add_fusion), calls=%async_computation.2 | async-start | bytes 32768 | tf_op jit(solution)/shard_map/all_to_all | solution.py:90
  73.2 2.2 %copy.294 = bf16[48,8,8,128]{3,2,1,0:T(8,128)(2,1)} copy(bf16[48,8,8,128]{3,1,2,0:T(8,128)(2,1)} %bitcast.146) | data formatting | bytes 1572864
  75.4 3.9 %all-to-all-done.2 = f32[16,1,224]{2,1,0:T(1,128)S(1)} async-done(((f32[16,1,224]{2,1,0:T(1,128)}), f32[16,1,224]{2,1,0:T(1,128)S(1)}, u32[]{:S(2)}, u32[]{:S(2)}) %all-to-all-start.2) | async-done | bytes 14368 | tf_op jit(solution)/shard_map/all_to_all | solution.py:90
  79.4 38.1 %all-gather = f32[512,1,224]{2,0,1:T(8,128)S(1)} all-gather(f32[16,1,224]{2,0,1:T(8,128)S(1)} %copy.235), channel_id=2, replica_groups=mesh['z'=16,'core'=2,'tensor'=16] {'z','core'}, dimensions={0}, use_global_device_ids=true | all-gather | bytes 473088 | tf_op jit(solution)/shard_map/all_gather | solution.py:91
  117.5 0.4 copy.236
  117.9 0.8 reshape.365
  118.7 0.7 slice_bitcast_fusion.1
  119.4 0.3 subtract_convert_fusion
  120.0 1.4 fusion.66
  121.4 0.7 fusion.65
  122.1 0.6 pad.14
  122.7 0.6 copy.248
  123.3 0.9 reshape.370
  124.2 1.0 fusion.10
  125.3 0.5 convolution_bitcast_fusion
  125.8 0.5 copy-done.7
  126.3 0.3 fusion.18
  126.6 0.4 convolution_add_fusion
  127.5 2.2 %collective-permute-start.1 = (f32[4,4,22,128]{3,1,0,2:T(4,128)S(1)}, f32[4,4,22,128]{3,1,0,2:T(4,128)S(1)}, u32[]{:S(2)}, u32[]{:S(2)}) collective-permute-start(f32[4,4,22,128]{3,1,0,2:T(4,128)S(1)} %copy.259), channel_id=1, source_target_pairs={{0,16},{16,0},{1,17},{17,1},{2,18},{18,2},{3,19},{19,3},{4,20},{20... | collective-permute-start | bytes 540680 | tf_op jit(solution)/shard_map/ppermute | solution.py:198
  129.9 1.0 collective-permute-done.1
  131.5 0.7 copy.262
  132.2 4.2 %all-to-all-start.3 = ((f32[16,22,128]{2,1,0:T(8,128)}), f32[16,22,128]{2,1,0:T(8,128)S(1)}, u32[]{:S(2)}, u32[]{:S(2)}) async-start(f32[16,22,128]{2,1,0:T(8,128)} %copy.262), calls=%async_computation.3 | async-start | bytes 393216 | tf_op jit(solution)/shard_map/all_to_all | solution.py:223
  136.4 0.3 fusion.64
  136.8 0.7 copy.271
  137.5 0.3 fusion.35
  137.8 0.7 fusion.44
  138.6 2.2 %copy.231 = bf16[16,320,160]{1,0,2:T(8,128)(2,1)S(1)} copy(bf16[16,320,160]{1,2,0:T(8,128)(2,1)} %all-gather.4.cloned.1.call-done) | data formatting | bytes 3276800 | tf_op jit(solution)/shard_map/all_gather | solution.py:59
  140.9 2.6 %reshape.377 = bf16[5120,160]{0,1:T(8,128)(2,1)} reshape(bf16[16,320,160]{1,0,2:T(8,128)(2,1)S(1)} %copy.231) | data formatting | bytes 3276800 | tf_op jit(solution)/shard_map/optimization_barrier | solution.py:224
  143.4 6.1 %all-to-all-done.3 = f32[16,22,128]{2,1,0:T(8,128)S(1)} async-done(((f32[16,22,128]{2,1,0:T(8,128)}), f32[16,22,128]{2,1,0:T(8,128)S(1)}, u32[]{:S(2)}, u32[]{:S(2)}) %all-to-all-start.3) | async-done | bytes 180256 | tf_op jit(solution)/shard_map/all_to_all | solution.py:223
  150.0 34.7 %all_gather.16 = bf16[32,20,128]{2,1,0:T(8,128)(2,1)S(1)} all-gather(bf16[1,20,128]{2,1,0:T(8,128)(2,1)S(1)} %copy.268), channel_id=1, replica_groups=mesh['z'=16,'core'=2,'tensor'=16] {'z','core'}, dimensions={0}, use_global_device_ids=true | all-gather | bytes 168960 | tf_op jit(solution)/shard_map/all_gather | solution.py:245
  185.0 1.2 fusion
  (100 shorter events, 3.1 us)
Async XLA Ops:
  7.2 112.8 %copy-start = (bf16[4,128,1024]{2,1,0:T(8,128)(2,1)S(1)}, bf16[4,128,1024]{2,1,0:T(8,128)(2,1)}, u32[]{:S(2)}) copy-start(bf16[4,128,1024]{2,1,0:T(8,128)(2,1)} %param.18) | copy-start | bytes 3145732
  7.2 131.4 %all-gather.4.cloned.1.call-start = ((), (), s32[]{:S(2)}) async-start(), calls=%async_computation.4 | async-start | bytes 2088960 | tf_op jit(solution)/shard_map/all_gather | solution.py:59
  9.7 28.9 %all-to-all-start = ((f32[32,1,256]{2,1,0:T(1,128)}), f32[32,1,256]{2,1,0:T(1,128)S(1)}, u32[]{:S(2)}, u32[]{:S(2)}) async-start(f32[32,1,256]{2,1,0:T(1,128)} %reshape.382), calls=%async_computation | async-start | bytes 65536 | tf_op jit(solution)/shard_map/all_to_all | solution.py:64
  41.2 4.9 %copy-start.18 = (bf16[448]{0:T(512)(128)(2,1)S(1)}, bf16[448]{0:T(512)(128)(2,1)}, u32[]{:S(2)}) copy-start(bf16[448]{0:T(512)(128)(2,1)} %param.14) | copy-start | bytes 2692
  42.1 8.9 %copy-start.21 = (s32[4]{0:T(128)S(1)}, s32[4]{0:T(128)}, u32[]{:S(2)}) copy-start(s32[4]{0:T(128)} %param.21) | copy-start | bytes 52
  42.2 30.8 %copy-start.5 = (bf16[1,384,1024]{2,1,0:T(8,128)(2,1)S(1)}, bf16[1,384,1024]{2,1,0:T(8,128)(2,1)}, u32[]{:S(2)}) copy-start(bf16[1,384,1024]{2,1,0:T(8,128)(2,1)} %param.16) | copy-start | bytes 2359300
  42.2 4.4 %collective-permute-start = (f32[4,16,4,224]{3,1,2,0:T(8,128)S(1)}, f32[4,16,4,224]{3,1,2,0:T(8,128)S(1)}, u32[]{:S(2)}, u32[]{:S(2)}) collective-permute-start(f32[4,16,4,224]{3,1,2,0:T(8,128)S(1)} %bitcast.152), channel_id=1, source_target_pairs={{0,16},{16,0},{1,17},{17,1},{2,18},{18,2},{3,19},{19,3},{4,20},{20... | collective-permute-start | bytes 688136 | tf_op jit(solution)/shard_map/ppermute | solution.py:83
  47.5 18.0 %all-to-all-start.1 = ((f32[16,16,224]{2,1,0:T(8,128)}), f32[16,16,224]{2,1,0:T(8,128)S(1)}, u32[]{:S(2)}, u32[]{:S(2)}) async-start(f32[16,16,224]{2,1,0:T(8,128)} %bitcast.6), calls=%async_computation.1 | async-start | bytes 524288 | tf_op jit(solution)/shard_map/all_to_all | solution.py:85
  51.1 68.9 %copy-start.19 = (pred[4,128]{1,0:T(4,128)(4,1)}, pred[4,128]{1,0:T(4,128)(4,1)S(1)}, u32[]{:S(2)}) copy-start(pred[4,128]{1,0:T(4,128)(4,1)S(1)} %broadcast_compare_fusion) | copy-start | bytes 1540
  51.3 24.1 %copy-start.9 = (f32[4,4,64]{2,0,1:T(4,128)}, f32[4,4,64]{2,0,1:T(4,128)S(1)}, u32[]{:S(2)}) copy-start(f32[4,4,64]{2,0,1:T(4,128)S(1)} %get-tuple-element.48) | copy-start | bytes 12292
  51.3 24.1 %copy-start.11 = (f32[4,4,64]{2,0,1:T(4,128)}, f32[4,4,64]{2,0,1:T(4,128)S(1)}, u32[]{:S(2)}) copy-start(f32[4,4,64]{2,0,1:T(4,128)S(1)} %get-tuple-element.49) | copy-start | bytes 12292
  66.1 13.2 %all-to-all-start.2 = ((f32[16,1,224]{2,1,0:T(1,128)}), f32[16,1,224]{2,1,0:T(1,128)S(1)}, u32[]{:S(2)}, u32[]{:S(2)}) async-start(f32[16,1,224]{2,1,0:T(1,128)} %reshape_add_fusion), calls=%async_computation.2 | async-start | bytes 32768 | tf_op jit(solution)/shard_map/all_to_all | solution.py:90
  72.9 48.5 %copy-start.16 = (pred[384]{0:T(512)(128)(4,1)}, pred[384]{0:T(512)(128)(4,1)S(1)}, u32[]{:S(2)}) copy-start(pred[384]{0:T(512)(128)(4,1)S(1)} %add_compare_fusion) | copy-start | bytes 1156
  120.0 2.1 %copy-start.3 = (bf16[4,8,4,5,128]{4,1,3,2,0:T(8,128)(2,1)}, bf16[4,8,4,5,128]{4,1,3,2,0:T(8,128)(2,1)S(1)}, u32[]{:S(2)}) copy-start(bf16[4,8,4,5,128]{4,1,3,2,0:T(8,128)(2,1)S(1)} %copy.241) | copy-start | bytes 491524
  122.1 3.1 %copy-start.6 = (bf16[48,8,8,128]{3,2,1,0:T(8,128)(2,1)S(1)}, bf16[48,8,8,128]{3,2,1,0:T(8,128)(2,1)}, u32[]{:S(2)}) copy-start(bf16[48,8,8,128]{3,2,1,0:T(8,128)(2,1)} %copy.294) | copy-start | bytes 2359300
  124.2 1.0 copy-start.17
  125.3 1.0 copy-start.7
  125.3 1.0 copy-start.13
  125.3 1.0 copy-start.20
  125.3 1.3 copy-start.2
  126.6 0.7 copy-start.14
  127.0 2.7 %copy-start.10 = (f32[4,4,64]{2,0,1:T(4,128)S(1)}, f32[4,4,64]{2,0,1:T(4,128)}, u32[]{:S(2)}) copy-start(f32[4,4,64]{2,0,1:T(4,128)} %copy-done.9) | copy-start | bytes 12292
  127.0 2.7 %copy-start.12 = (f32[4,4,64]{2,0,1:T(4,128)S(1)}, f32[4,4,64]{2,0,1:T(4,128)}, u32[]{:S(2)}) copy-start(f32[4,4,64]{2,0,1:T(4,128)} %copy-done.11) | copy-start | bytes 12292
  127.5 9.0 %copy-start.4 = (bf16[4,8,4,5,128]{4,1,3,2,0:T(8,128)(2,1)S(1)}, bf16[4,8,4,5,128]{4,1,3,2,0:T(8,128)(2,1)}, u32[]{:S(2)}) copy-start(bf16[4,8,4,5,128]{4,1,3,2,0:T(8,128)(2,1)} %copy-done.3) | copy-start | bytes 491524
  127.5 9.0 %copy-start.15 = (pred[20,4]{0,1:T(4,128)(4,1)S(1)}, pred[20,4]{0,1:T(4,128)(4,1)}, u32[]{:S(2)}) copy-start(pred[20,4]{0,1:T(4,128)(4,1)} %iota_compare_fusion) | copy-start | bytes 244
  127.5 3.4 %collective-permute-start.1 = (f32[4,4,22,128]{3,1,0,2:T(4,128)S(1)}, f32[4,4,22,128]{3,1,0,2:T(4,128)S(1)}, u32[]{:S(2)}, u32[]{:S(2)}) collective-permute-start(f32[4,4,22,128]{3,1,0,2:T(4,128)S(1)} %copy.259), channel_id=1, source_target_pairs={{0,16},{16,0},{1,17},{17,1},{2,18},{18,2},{3,19},{19,3},{4,20},{20... | collective-permute-start | bytes 540680 | tf_op jit(solution)/shard_map/ppermute | solution.py:198
  131.2 5.6 %copy-start.8 = (f32[4,4,1024]{2,0,1:T(4,128)S(1)}, f32[4,4,1024]{2,0,1:T(4,128)}, u32[]{:S(2)}) copy-start(f32[4,4,1024]{2,0,1:T(4,128)} %get-tuple-element.36) | copy-start | bytes 196612
  132.2 17.4 %all-to-all-start.3 = ((f32[16,22,128]{2,1,0:T(8,128)}), f32[16,22,128]{2,1,0:T(8,128)S(1)}, u32[]{:S(2)}, u32[]{:S(2)}) async-start(f32[16,22,128]{2,1,0:T(8,128)} %copy.262), calls=%async_computation.3 | async-start | bytes 393216 | tf_op jit(solution)/shard_map/all_to_all | solution.py:223
  143.4 41.5 %copy-start.1 = (bf16[5120,160]{0,1:T(8,128)(2,1)S(1)}, bf16[5120,160]{0,1:T(8,128)(2,1)}, u32[]{:S(2)}) copy-start(bf16[5120,160]{0,1:T(8,128)(2,1)} %reshape.377) | copy-start | bytes 4915204
Sparse Core Ops, SparseCore 0:
  11.0 64.4 all-gather.3

commit v6 on v5

--- a/solution.py
+++ b/solution.py
@@ -242,7 +242,10 @@
     summed = global_acc * factor_old[..., None] + own_new_acc * factor_new[..., None]
     attention_slice = (summed / total[..., None]).astype(jnp.bfloat16)
 
-    attention_all = lax.all_gather(attention_slice, SEQ, axis=0, tiled=False)
+    attention_all = lax.all_to_all(
+        jnp.broadcast_to(attention_slice[None], (seq_count,) + attention_slice.shape),
+        SEQ, 0, 0, tiled=True,
+    )
     heads_local = (
         attention_all.reshape(requests, KEY_HEADS, steps, query_group_width, HEAD_SIZE)
         .transpose(2, 0, 1, 3, 4)

time: 194 us -> 183 us (0.943)
  blocking collectives: 72.9 us -> 38.2 us
  waiting for transfers between devices: 37.4 us -> 54.9 us
  starting transfers between devices: 36.6 us -> 45.7 us
  local copies, waits for them, and re-layouts: 16.7 us -> 14.3 us
    all_gather x1 -> x0, blocking collectives: 34.7 us -> none  [body(): attention_all = lax.all_gather(attention_slice, SEQ, axis=0, tiled=False)]
    all_to_all x0 -> x1, waiting for transfers between devices: none -> 17.2 us  [body(): lax.all_to_all(jnp.broadcast_to(attention_slice[None], (seq_count,) + att...]
    all_to_all x0 -> x1, starting transfers between devices: none -> 9.18 us  [body(): lax.all_to_all(jnp.broadcast_to(attention_slice[None], (seq_count,) + att...]
    unnamed x51 -> x21, local copies, waits for them, and re-layouts: 4.78 us -> 4.5 us
  transfers between devices with their start and end apart: 7 -> 8, of which waited for: 5 -> 7; matrix products, arithmetic and copies ran while one was open for 15% -> 12% of each run, Pallas kernels for 0% -> 0%
where the time goes in v6:
time: 183 us; the launch traced here: 182 us
  waiting for transfers between devices  54.9 us (30%)
  starting transfers between devices  45.7 us (25%)
  blocking collectives  38.2 us (21%)
  between operations  15.2 us (8%)
  local copies, waits for them, and re-layouts  14.3 us (8%)
  other arithmetic  7.77 us (4%)
  matrix products  6.08 us (3%)
    all_gather x1, blocking collectives, body(): gathered = lax.all_gather(owned_rows, SEQ, axis=0, tiled=False)  38.2 us
    all_to_all x1, waiting for transfers between devices, body(): lax.all_to_all(jnp.broadcast_to(attention_slice[None], (seq_count,) + att...  17.2 us
    all_to_all x1, starting transfers between devices, body(): lax.all_to_all(jnp.broadcast_to(local_squares[None], (seq_count,) + local...  16.7 us
    all_to_all x1, waiting for transfers between devices, body(): reduced = jnp.sum(lax.all_to_all(chunks, 'z', 0, 0, tiled=True), axis=0)  14.1 us
    all_to_all x1, waiting for transfers between devices, body(): lax.all_to_all(jnp.broadcast_to(local_squares[None], (seq_count,) + local...  10.7 us
    all_to_all x1, starting transfers between devices, body(): lax.all_to_all(jnp.broadcast_to(attention_slice[None], (seq_count,) + att...  9.18 us
    all_to_all x1, waiting for transfers between devices, body(): arrived = lax.all_to_all(pair_packed, 'z', 0, 0, tiled=True)  6.78 us
    all_to_all x1, starting transfers between devices, body(): owned_rows = lax.all_to_all(reduced, 'tensor', 0, 0, tiled=True)  6.76 us
  transfers between devices with their start and end apart: 8, of which 7 were waited for; matrix products, arithmetic and copies ran while one was open for 12% of the time, Pallas kernels for 0%

profile of v6, /device:TPU:1, one launch (start us, length us, event | category | flops | bytes accessed | tf_op | source)
XLA Modules:
  0.0 182.2 jit_solution(754688764741654744)
XLA Ops:
  7.2 1.1 fusion.20
  8.3 0.7 reshape.346
  9.0 16.7 %all-to-all-start = ((f32[32,1,256]{2,1,0:T(1,128)}), f32[32,1,256]{2,1,0:T(1,128)S(1)}, u32[]{:S(2)}, u32[]{:S(2)}) async-start(f32[32,1,256]{2,1,0:T(1,128)} %reshape.346), calls=%async_computation | async-start | bytes 65536 | tf_op jit(solution)/shard_map/all_to_all | solution.py:64
  25.8 0.7 all-gather.4.cloned.1.call-update
  26.5 0.7 convert_element_type.53
  27.2 10.7 %all-to-all-done = f32[32,1,256]{2,1,0:T(1,128)S(1)} async-done(((f32[32,1,256]{2,1,0:T(1,128)}), f32[32,1,256]{2,1,0:T(1,128)S(1)}, u32[]{:S(2)}, u32[]{:S(2)}) %all-to-all-start) | async-done | bytes 32800 | tf_op jit(solution)/shard_map/all_to_all | solution.py:64
  37.9 0.5 broadcast.183
  38.4 0.7 reduce.1
  39.3 1.2 fusion.28
  40.6 0.4 reshape.326
  41.0 0.5 constant_dynamic-slice_fusion.3
  41.6 3.2 %collective-permute-start = (f32[4,16,4,224]{3,1,2,0:T(8,128)S(1)}, f32[4,16,4,224]{3,1,2,0:T(8,128)S(1)}, u32[]{:S(2)}, u32[]{:S(2)}) collective-permute-start(f32[4,16,4,224]{3,1,2,0:T(8,128)S(1)} %bitcast.160), channel_id=1, source_target_pairs={{0,16},{16,0},{1,17},{17,1},{2,18},{18,2},{3,19},{19,3},{4,20},{20... | collective-permute-start | bytes 688136 | tf_op jit(solution)/shard_map/ppermute | solution.py:83
  45.5 0.4 collective-permute-done
  45.9 0.8 bitcast_add_fusion
  46.7 3.5 %all-to-all-start.1 = ((f32[16,16,224]{2,1,0:T(8,128)}), f32[16,16,224]{2,1,0:T(8,128)S(1)}, u32[]{:S(2)}, u32[]{:S(2)}) async-start(f32[16,16,224]{2,1,0:T(8,128)} %bitcast.6), calls=%async_computation.1 | async-start | bytes 524288 | tf_op jit(solution)/shard_map/all_to_all | solution.py:85
  50.5 14.1 %all-to-all-done.1 = f32[16,16,224]{2,1,0:T(8,128)S(1)} async-done(((f32[16,16,224]{2,1,0:T(8,128)}), f32[16,16,224]{2,1,0:T(8,128)S(1)}, u32[]{:S(2)}, u32[]{:S(2)}) %all-to-all-start.1) | async-done | bytes 229408 | tf_op jit(solution)/shard_map/all_to_all | solution.py:85
  64.6 0.6 reshape_add_fusion
  65.2 6.8 %all-to-all-start.2 = ((f32[16,1,224]{2,1,0:T(1,128)}), f32[16,1,224]{2,1,0:T(1,128)S(1)}, u32[]{:S(2)}, u32[]{:S(2)}) async-start(f32[16,1,224]{2,1,0:T(1,128)} %reshape_add_fusion), calls=%async_computation.2 | async-start | bytes 32768 | tf_op jit(solution)/shard_map/all_to_all | solution.py:90
  72.2 2.2 %copy.290 = bf16[48,8,8,128]{3,2,1,0:T(8,128)(2,1)} copy(bf16[48,8,8,128]{3,1,2,0:T(8,128)(2,1)} %bitcast.154) | data formatting | bytes 1572864
  74.4 4.0 %all-to-all-done.2 = f32[16,1,224]{2,1,0:T(1,128)S(1)} async-done(((f32[16,1,224]{2,1,0:T(1,128)}), f32[16,1,224]{2,1,0:T(1,128)S(1)}, u32[]{:S(2)}, u32[]{:S(2)}) %all-to-all-start.2) | async-done | bytes 14368 | tf_op jit(solution)/shard_map/all_to_all | solution.py:90
  78.4 38.2 %all-gather = f32[512,1,224]{2,0,1:T(8,128)S(1)} all-gather(f32[16,1,224]{2,0,1:T(8,128)S(1)} %copy.232), channel_id=2, replica_groups=mesh['z'=16,'core'=2,'tensor'=16] {'z','core'}, dimensions={0}, use_global_device_ids=true | all-gather | bytes 473088 | tf_op jit(solution)/shard_map/all_gather | solution.py:91
  116.7 0.4 copy.233
  117.1 0.8 reshape.329
  117.9 0.3 subtract_convert_fusion
  118.5 0.7 fusion.68
  119.1 0.7 fusion.69
  119.9 0.4 fusion.10
  120.4 0.5 convolution_bitcast_fusion
  120.9 0.3 fusion.18
  121.2 0.4 copy-done.2
  121.6 0.4 convolution_add_fusion
  122.3 2.1 %collective-permute-start.1 = (f32[4,4,22,128]{3,1,0,2:T(4,128)S(1)}, f32[4,4,22,128]{3,1,0,2:T(4,128)S(1)}, u32[]{:S(2)}, u32[]{:S(2)}) collective-permute-start(f32[4,4,22,128]{3,1,0,2:T(4,128)S(1)} %copy.256), channel_id=1, source_target_pairs={{0,16},{16,0},{1,17},{17,1},{2,18},{18,2},{3,19},{19,3},{4,20},{20... | collective-permute-start | bytes 540680 | tf_op jit(solution)/shard_map/ppermute | solution.py:198
  124.5 1.1 collective-permute-done.1
  125.9 0.2 fusion.27
  126.2 0.7 copy.259
  126.9 4.2 %all-to-all-start.3 = ((f32[16,22,128]{2,1,0:T(8,128)}), f32[16,22,128]{2,1,0:T(8,128)S(1)}, u32[]{:S(2)}, u32[]{:S(2)}) async-start(f32[16,22,128]{2,1,0:T(8,128)} %copy.259), calls=%async_computation.3 | async-start | bytes 393216 | tf_op jit(solution)/shard_map/all_to_all | solution.py:223
  131.3 0.3 fusion.67
  131.6 1.1 fusion.35
  132.8 2.2 %copy.228 = bf16[16,320,160]{1,0,2:T(8,128)(2,1)S(1)} copy(bf16[16,320,160]{1,2,0:T(8,128)(2,1)} %all-gather.4.cloned.1.call-done) | data formatting | bytes 3276800 | tf_op jit(solution)/shard_map/all_gather | solution.py:59
  135.0 2.5 %reshape.341 = bf16[5120,160]{0,1:T(8,128)(2,1)} reshape(bf16[16,320,160]{1,0,2:T(8,128)(2,1)S(1)} %copy.228) | data formatting | bytes 3276800 | tf_op jit(solution)/shard_map/optimization_barrier | solution.py:224
  137.5 6.8 %all-to-all-done.3 = f32[16,22,128]{2,1,0:T(8,128)S(1)} async-done(((f32[16,22,128]{2,1,0:T(8,128)}), f32[16,22,128]{2,1,0:T(8,128)S(1)}, u32[]{:S(2)}, u32[]{:S(2)}) %all-to-all-start.3) | async-done | bytes 180256 | tf_op jit(solution)/shard_map/all_to_all | solution.py:223
  144.6 0.9 fusion.46
  145.4 0.7 broadcast_in_dim.111
  146.2 9.2 %all-to-all-start.4 = ((bf16[32,20,128]{2,1,0:T(8,128)(2,1)}), bf16[32,20,128]{2,1,0:T(8,128)(2,1)S(1)}, u32[]{:S(2)}, u32[]{:S(2)}) async-start(bf16[32,20,128]{2,1,0:T(8,128)(2,1)} %broadcast_in_dim.111), calls=%async_computation.4 | async-start | bytes 393216 | tf_op jit(solution)/shard_map/all_to_all | solution.py:245
  155.3 0.7 copy.267
  156.0 0.7 fusion.47
  156.7 17.2 %all-to-all-done.4 = bf16[32,20,128]{2,1,0:T(8,128)(2,1)S(1)} async-done(((bf16[32,20,128]{2,1,0:T(8,128)(2,1)}), bf16[32,20,128]{2,1,0:T(8,128)(2,1)S(1)}, u32[]{:S(2)}, u32[]{:S(2)}) %all-to-all-start.4) | async-done | bytes 163872 | tf_op jit(solution)/shard_map/all_to_all | solution.py:245
  174.2 1.2 fusion
  (70 shorter events, 2.6 us)
Async XLA Ops:
  7.2 112.0 %copy-start = (bf16[4,128,1024]{2,1,0:T(8,128)(2,1)S(1)}, bf16[4,128,1024]{2,1,0:T(8,128)(2,1)}, u32[]{:S(2)}) copy-start(bf16[4,128,1024]{2,1,0:T(8,128)(2,1)} %param.18) | copy-start | bytes 3145732
  9.0 28.9 %all-to-all-start = ((f32[32,1,256]{2,1,0:T(1,128)}), f32[32,1,256]{2,1,0:T(1,128)S(1)}, u32[]{:S(2)}, u32[]{:S(2)}) async-start(f32[32,1,256]{2,1,0:T(1,128)} %reshape.346), calls=%async_computation | async-start | bytes 65536 | tf_op jit(solution)/shard_map/all_to_all | solution.py:64
  25.8 107.0 %all-gather.4.cloned.1.call-start = ((), (), s32[]{:S(2)}) async-start(), calls=%async_computation.5 | async-start | bytes 2088960 | tf_op jit(solution)/shard_map/all_gather | solution.py:59
  40.5 4.9 %copy-start.5 = (bf16[448]{0:T(512)(128)(2,1)S(1)}, bf16[448]{0:T(512)(128)(2,1)}, u32[]{:S(2)}) copy-start(bf16[448]{0:T(512)(128)(2,1)} %param.14) | copy-start | bytes 2692
  41.5 8.7 %copy-start.6 = (s32[4]{0:T(128)S(1)}, s32[4]{0:T(128)}, u32[]{:S(2)}) copy-start(s32[4]{0:T(128)} %param.21) | copy-start | bytes 52
  41.5 30.5 %copy-start.3 = (bf16[1,384,1024]{2,1,0:T(8,128)(2,1)S(1)}, bf16[1,384,1024]{2,1,0:T(8,128)(2,1)}, u32[]{:S(2)}) copy-start(bf16[1,384,1024]{2,1,0:T(8,128)(2,1)} %param.16) | copy-start | bytes 2359300
  41.6 4.3 %collective-permute-start = (f32[4,16,4,224]{3,1,2,0:T(8,128)S(1)}, f32[4,16,4,224]{3,1,2,0:T(8,128)S(1)}, u32[]{:S(2)}, u32[]{:S(2)}) collective-permute-start(f32[4,16,4,224]{3,1,2,0:T(8,128)S(1)} %bitcast.160), channel_id=1, source_target_pairs={{0,16},{16,0},{1,17},{17,1},{2,18},{18,2},{3,19},{19,3},{4,20},{20... | collective-permute-start | bytes 688136 | tf_op jit(solution)/shard_map/ppermute | solution.py:83
  46.7 17.9 %all-to-all-start.1 = ((f32[16,16,224]{2,1,0:T(8,128)}), f32[16,16,224]{2,1,0:T(8,128)S(1)}, u32[]{:S(2)}, u32[]{:S(2)}) async-start(f32[16,16,224]{2,1,0:T(8,128)} %bitcast.6), calls=%async_computation.1 | async-start | bytes 524288 | tf_op jit(solution)/shard_map/all_to_all | solution.py:85
  65.2 13.2 %all-to-all-start.2 = ((f32[16,1,224]{2,1,0:T(1,128)}), f32[16,1,224]{2,1,0:T(1,128)S(1)}, u32[]{:S(2)}, u32[]{:S(2)}) async-start(f32[16,1,224]{2,1,0:T(1,128)} %reshape_add_fusion), calls=%async_computation.2 | async-start | bytes 32768 | tf_op jit(solution)/shard_map/all_to_all | solution.py:90
  119.1 1.2 copy-start.4
  120.4 1.2 copy-start.2
  122.3 3.3 %collective-permute-start.1 = (f32[4,4,22,128]{3,1,0,2:T(4,128)S(1)}, f32[4,4,22,128]{3,1,0,2:T(4,128)S(1)}, u32[]{:S(2)}, u32[]{:S(2)}) collective-permute-start(f32[4,4,22,128]{3,1,0,2:T(4,128)S(1)} %copy.256), channel_id=1, source_target_pairs={{0,16},{16,0},{1,17},{17,1},{2,18},{18,2},{3,19},{19,3},{4,20},{20... | collective-permute-start | bytes 540680 | tf_op jit(solution)/shard_map/ppermute | solution.py:198
  126.9 17.4 %all-to-all-start.3 = ((f32[16,22,128]{2,1,0:T(8,128)}), f32[16,22,128]{2,1,0:T(8,128)S(1)}, u32[]{:S(2)}, u32[]{:S(2)}) async-start(f32[16,22,128]{2,1,0:T(8,128)} %copy.259), calls=%async_computation.3 | async-start | bytes 393216 | tf_op jit(solution)/shard_map/all_to_all | solution.py:223
  144.4 29.8 %copy-start.1 = (bf16[5120,160]{0,1:T(8,128)(2,1)S(1)}, bf16[5120,160]{0,1:T(8,128)(2,1)}, u32[]{:S(2)}) copy-start(bf16[5120,160]{0,1:T(8,128)(2,1)} %reshape.341) | copy-start | bytes 4915204
  146.2 27.8 %all-to-all-start.4 = ((bf16[32,20,128]{2,1,0:T(8,128)(2,1)}), bf16[32,20,128]{2,1,0:T(8,128)(2,1)S(1)}, u32[]{:S(2)}, u32[]{:S(2)}) async-start(bf16[32,20,128]{2,1,0:T(8,128)(2,1)} %broadcast_in_dim.111), calls=%async_computation.4 | async-start | bytes 393216 | tf_op jit(solution)/shard_map/all_to_all | solution.py:245
Sparse Core Ops, SparseCore 0:
  29.6 59.8 all-gather.3

commit v7 on v6

--- a/solution.py
+++ b/solution.py
@@ -88,7 +88,9 @@
     )
     reduced = reduced + bias[None, :]
     owned_rows = lax.all_to_all(reduced, "tensor", 0, 0, tiled=True)
-    gathered = lax.all_gather(owned_rows, SEQ, axis=0, tiled=False)
+    gathered = lax.all_to_all(
+        jnp.broadcast_to(owned_rows[None], (seq_count,) + owned_rows.shape), SEQ, 0, 0, tiled=True
+    )
     combined_output = (
         gathered.reshape(steps, requests, halves, tensor_count, half_width)
         .transpose(0, 1, 3, 2, 4)

time: 183 us -> 199 us (1.087)
  waiting for transfers between devices: 54.9 us -> 85.9 us
  blocking collectives: 38.2 us -> 13 us
  starting transfers between devices: 45.7 us -> 55.2 us
    all_gather x1 -> x0, blocking collectives: 38.2 us -> none  [body(): gathered = lax.all_gather(owned_rows, SEQ, axis=0, tiled=False)]
    all_to_all x1, waiting for transfers between devices: 3.98 us -> 29.3 us  [body(): lax.all_to_all(jnp.broadcast_to(owned_rows[None], (seq_count,) + owned_ro...]
    all_to_all x0 -> x1, blocking collectives: none -> 13 us  [body(): owned_rows = lax.all_to_all(reduced, 'tensor', 0, 0, tiled=True)]
    all_gather x1, waiting for transfers between devices: 0.01 us -> 10.9 us  [body(): w_out_cols = lax.all_gather(w_out, 'tensor', axis=0, tiled=True)]
    all_to_all x1, waiting for transfers between devices: 6.78 us -> 0.01 us  [body(): arrived = lax.all_to_all(pair_packed, 'z', 0, 0, tiled=True)]
    all_to_all x1, starting transfers between devices: 6.76 us -> 12.1 us  [body(): lax.all_to_all(jnp.broadcast_to(owned_rows[None], (seq_count,) + owned_ro...]
    all_to_all x1, starting transfers between devices: 9.18 us -> 13.8 us  [body(): lax.all_to_all(jnp.broadcast_to(attention_slice[None], (seq_count,) + att...]
    unnamed x21 -> x22, local copies, waits for them, and re-layouts: 4.5 us -> 4.5 us
  transfers between devices with their start and end apart: 8 -> 8, of which waited for: 7 -> 7; matrix products, arithmetic and copies ran while one was open for 12% -> 9% of each run, Pallas kernels for 0% -> 0%
where the time goes in v7:
time: 199 us; the launch traced here: 198 us
  waiting for transfers between devices  85.9 us (43%)
  starting transfers between devices  55.2 us (28%)
  local copies, waits for them, and re-layouts  15.2 us (8%)
  between operations  15.2 us (8%)
  blocking collectives  13 us (7%)
  other arithmetic  7.16 us (4%)
  matrix products  6.08 us (3%)
    all_to_all x1, waiting for transfers between devices, body(): lax.all_to_all(jnp.broadcast_to(owned_rows[None], (seq_count,) + owned_ro...  29.3 us
    all_to_all x1, waiting for transfers between devices, body(): lax.all_to_all(jnp.broadcast_to(attention_slice[None], (seq_count,) + att...  17.2 us
    all_to_all x1, starting transfers between devices, body(): lax.all_to_all(jnp.broadcast_to(local_squares[None], (seq_count,) + local...  16.7 us
    all_to_all x1, waiting for transfers between devices, body(): reduced = jnp.sum(lax.all_to_all(chunks, 'z', 0, 0, tiled=True), axis=0)  14.2 us
    all_to_all x1, starting transfers between devices, body(): lax.all_to_all(jnp.broadcast_to(attention_slice[None], (seq_count,) + att...  13.8 us
    all_to_all x1, blocking collectives, body(): owned_rows = lax.all_to_all(reduced, 'tensor', 0, 0, tiled=True)  13 us
    all_to_all x1, starting transfers between devices, body(): lax.all_to_all(jnp.broadcast_to(owned_rows[None], (seq_count,) + owned_ro...  12.1 us
    all_to_all x1, waiting for transfers between devices, body(): lax.all_to_all(jnp.broadcast_to(local_squares[None], (seq_count,) + local...  11.4 us
  transfers between devices with their start and end apart: 8, of which 7 were waited for; matrix products, arithmetic and copies ran while one was open for 9% of the time, Pallas kernels for 0%

profile of v7, /device:TPU:1, one launch (start us, length us, event | category | flops | bytes accessed | tf_op | source)
XLA Modules:
  0.0 197.7 jit_solution(9587950657682747550)
XLA Ops:
  7.2 1.1 fusion.20
  8.3 0.7 reshape.345
  9.0 16.7 %all-to-all-start = ((f32[32,1,256]{2,1,0:T(1,128)}), f32[32,1,256]{2,1,0:T(1,128)S(1)}, u32[]{:S(2)}, u32[]{:S(2)}) async-start(f32[32,1,256]{2,1,0:T(1,128)} %reshape.345), calls=%async_computation | async-start | bytes 65536 | tf_op jit(solution)/shard_map/all_to_all | solution.py:64
  25.8 0.7 convert_element_type.53
  26.5 11.4 %all-to-all-done = f32[32,1,256]{2,1,0:T(1,128)S(1)} async-done(((f32[32,1,256]{2,1,0:T(1,128)}), f32[32,1,256]{2,1,0:T(1,128)S(1)}, u32[]{:S(2)}, u32[]{:S(2)}) %all-to-all-start) | async-done | bytes 32800 | tf_op jit(solution)/shard_map/all_to_all | solution.py:64
  37.9 0.5 broadcast.183
  38.4 0.7 reduce.1
  39.3 1.2 fusion.28
  40.5 0.5 reshape.327
  41.0 0.5 constant_dynamic-slice_fusion.3
  41.6 3.0 %collective-permute-start = (f32[4,16,4,224]{3,1,2,0:T(8,128)S(1)}, f32[4,16,4,224]{3,1,2,0:T(8,128)S(1)}, u32[]{:S(2)}, u32[]{:S(2)}) collective-permute-start(f32[4,16,4,224]{3,1,2,0:T(8,128)S(1)} %bitcast.163), channel_id=1, source_target_pairs={{0,16},{16,0},{1,17},{17,1},{2,18},{18,2},{3,19},{19,3},{4,20},{20... | collective-permute-start | bytes 688136 | tf_op jit(solution)/shard_map/ppermute | solution.py:83
  44.6 1.1 collective-permute-done
  45.7 0.8 bitcast_add_fusion
  46.5 3.5 %all-to-all-start.1 = ((f32[16,16,224]{2,1,0:T(8,128)}), f32[16,16,224]{2,1,0:T(8,128)S(1)}, u32[]{:S(2)}, u32[]{:S(2)}) async-start(f32[16,16,224]{2,1,0:T(8,128)} %bitcast.6), calls=%async_computation.1 | async-start | bytes 524288 | tf_op jit(solution)/shard_map/all_to_all | solution.py:85
  50.2 14.2 %all-to-all-done.1 = f32[16,16,224]{2,1,0:T(8,128)S(1)} async-done(((f32[16,16,224]{2,1,0:T(8,128)}), f32[16,16,224]{2,1,0:T(8,128)S(1)}, u32[]{:S(2)}, u32[]{:S(2)}) %all-to-all-start.1) | async-done | bytes 229408 | tf_op jit(solution)/shard_map/all_to_all | solution.py:85
  64.5 13.0 %all_to_all.31 = f32[16,1,224]{2,1,0:T(1,128)S(1)} all-to-all(f32[16,1,224]{2,1,0:T(1,128)S(1)} %reshape_add_fusion), channel_id=1, replica_groups=mesh['z'=16,'core'=2,'tensor'=16] {'tensor'}, dimensions={0} | all-to-all | bytes 28672 | tf_op jit(solution)/shard_map/all_to_all | solution.py:90
  77.5 0.9 broadcast_in_dim.112
  78.3 12.1 %all-to-all-start.3 = ((f32[32,16,224]{2,1,0:T(8,128)}), f32[32,16,224]{2,1,0:T(8,128)S(1)}, u32[]{:S(2)}, u32[]{:S(2)}) async-start(f32[32,16,224]{2,1,0:T(8,128)} %broadcast_in_dim.112), calls=%async_computation.3 | async-start | bytes 1048576 | tf_op jit(solution)/shard_map/all_to_all | solution.py:91
  90.5 0.7 all-gather.3.cloned.1.call-update
  92.3 2.2 %copy.287 = bf16[48,8,8,128]{3,2,1,0:T(8,128)(2,1)} copy(bf16[48,8,8,128]{3,1,2,0:T(8,128)(2,1)} %bitcast.157) | data formatting | bytes 1572864
  94.7 29.3 %all-to-all-done.3 = f32[32,16,224]{2,1,0:T(8,128)S(1)} async-done(((f32[32,16,224]{2,1,0:T(8,128)}), f32[32,16,224]{2,1,0:T(8,128)S(1)}, u32[]{:S(2)}, u32[]{:S(2)}) %all-to-all-start.3) | async-done | bytes 458784 | tf_op jit(solution)/shard_map/all_to_all | solution.py:91
  124.0 0.4 copy.229
  124.4 0.8 reshape.330
  125.2 0.3 subtract_convert_fusion
  125.8 0.7 fusion.68
  126.5 0.7 fusion.69
  127.3 0.4 fusion.10
  127.7 0.5 convolution_bitcast_fusion
  128.2 0.3 fusion.18
  128.6 0.4 copy-done.2
  128.9 0.4 convolution_add_fusion
  129.7 2.4 %collective-permute-start.1 = (f32[4,4,22,128]{3,1,0,2:T(4,128)S(1)}, f32[4,4,22,128]{3,1,0,2:T(4,128)S(1)}, u32[]{:S(2)}, u32[]{:S(2)}) collective-permute-start(f32[4,4,22,128]{3,1,0,2:T(4,128)S(1)} %copy.252), channel_id=1, source_target_pairs={{0,16},{16,0},{1,17},{17,1},{2,18},{18,2},{3,19},{19,3},{4,20},{20... | collective-permute-start | bytes 540680 | tf_op jit(solution)/shard_map/ppermute | solution.py:200
  132.2 0.9 collective-permute-done.1
  133.4 0.2 fusion.27
  133.6 0.7 copy.255
  134.3 3.5 %all-to-all-start.4 = ((f32[16,22,128]{2,1,0:T(8,128)}), f32[16,22,128]{2,1,0:T(8,128)S(1)}, u32[]{:S(2)}, u32[]{:S(2)}) async-start(f32[16,22,128]{2,1,0:T(8,128)} %copy.255), calls=%async_computation.4 | async-start | bytes 393216 | tf_op jit(solution)/shard_map/all_to_all | solution.py:225
  138.0 0.3 fusion.67
  138.4 1.1 fusion.35
  139.5 10.9 %all-gather.3.cloned.1.call-done = bf16[16,320,160]{1,2,0:T(8,128)(2,1)} async-done(((bf16[1,320,160]{1,2,0:T(8,128)(2,1)}), bf16[16,320,160]{1,2,0:T(8,128)(2,1)}) %all-gather.3.cloned.1.call-update) | async-done | bytes 1638416 | tf_op jit(solution)/shard_map/all_gather | solution.py:59
  150.4 2.2 %copy.225 = bf16[16,320,160]{1,0,2:T(8,128)(2,1)S(1)} copy(bf16[16,320,160]{1,2,0:T(8,128)(2,1)} %all-gather.3.cloned.1.call-done) | data formatting | bytes 3276800 | tf_op jit(solution)/shard_map/all_gather | solution.py:59
  152.6 2.5 %reshape.340 = bf16[5120,160]{0,1:T(8,128)(2,1)} reshape(bf16[16,320,160]{1,0,2:T(8,128)(2,1)S(1)} %copy.225) | data formatting | bytes 3276800 | tf_op jit(solution)/shard_map/optimization_barrier | solution.py:226
  155.4 0.9 fusion.46
  156.3 0.7 broadcast_in_dim.121
  157.0 13.8 %all-to-all-start.5 = ((bf16[32,20,128]{2,1,0:T(8,128)(2,1)}), bf16[32,20,128]{2,1,0:T(8,128)(2,1)S(1)}, u32[]{:S(2)}, u32[]{:S(2)}) async-start(bf16[32,20,128]{2,1,0:T(8,128)(2,1)} %broadcast_in_dim.121), calls=%async_computation.5 | async-start | bytes 393216 | tf_op jit(solution)/shard_map/all_to_all | solution.py:247
  170.8 0.7 copy.263
  171.5 0.7 fusion.47
  172.2 17.2 %all-to-all-done.5 = bf16[32,20,128]{2,1,0:T(8,128)(2,1)S(1)} async-done(((bf16[32,20,128]{2,1,0:T(8,128)(2,1)}), bf16[32,20,128]{2,1,0:T(8,128)(2,1)S(1)}, u32[]{:S(2)}, u32[]{:S(2)}) %all-to-all-start.5) | async-done | bytes 163872 | tf_op jit(solution)/shard_map/all_to_all | solution.py:247
  189.7 1.2 fusion
  (71 shorter events, 2.6 us)
Async XLA Ops:
  7.2 119.3 %copy-start = (bf16[4,128,1024]{2,1,0:T(8,128)(2,1)S(1)}, bf16[4,128,1024]{2,1,0:T(8,128)(2,1)}, u32[]{:S(2)}) copy-start(bf16[4,128,1024]{2,1,0:T(8,128)(2,1)} %param.18) | copy-start | bytes 3145732
  9.0 28.9 %all-to-all-start = ((f32[32,1,256]{2,1,0:T(1,128)}), f32[32,1,256]{2,1,0:T(1,128)S(1)}, u32[]{:S(2)}, u32[]{:S(2)}) async-start(f32[32,1,256]{2,1,0:T(1,128)} %reshape.345), calls=%async_computation | async-start | bytes 65536 | tf_op jit(solution)/shard_map/all_to_all | solution.py:64
  41.5 8.6 %copy-start.5 = (bf16[448]{0:T(512)(128)(2,1)S(1)}, bf16[448]{0:T(512)(128)(2,1)}, u32[]{:S(2)}) copy-start(bf16[448]{0:T(512)(128)(2,1)} %param.14) | copy-start | bytes 2692
  41.6 4.2 %collective-permute-start = (f32[4,16,4,224]{3,1,2,0:T(8,128)S(1)}, f32[4,16,4,224]{3,1,2,0:T(8,128)S(1)}, u32[]{:S(2)}, u32[]{:S(2)}) collective-permute-start(f32[4,16,4,224]{3,1,2,0:T(8,128)S(1)} %bitcast.163), channel_id=1, source_target_pairs={{0,16},{16,0},{1,17},{17,1},{2,18},{18,2},{3,19},{19,3},{4,20},{20... | collective-permute-start | bytes 688136 | tf_op jit(solution)/shard_map/ppermute | solution.py:83
  46.5 17.9 %all-to-all-start.1 = ((f32[16,16,224]{2,1,0:T(8,128)}), f32[16,16,224]{2,1,0:T(8,128)S(1)}, u32[]{:S(2)}, u32[]{:S(2)}) async-start(f32[16,16,224]{2,1,0:T(8,128)} %bitcast.6), calls=%async_computation.1 | async-start | bytes 524288 | tf_op jit(solution)/shard_map/all_to_all | solution.py:85
  50.0 41.9 %copy-start.6 = (s32[4]{0:T(128)S(1)}, s32[4]{0:T(128)}, u32[]{:S(2)}) copy-start(s32[4]{0:T(128)} %param.21) | copy-start | bytes 52
  50.0 42.1 %copy-start.3 = (bf16[1,384,1024]{2,1,0:T(8,128)(2,1)S(1)}, bf16[1,384,1024]{2,1,0:T(8,128)(2,1)}, u32[]{:S(2)}) copy-start(bf16[1,384,1024]{2,1,0:T(8,128)(2,1)} %param.16) | copy-start | bytes 2359300
  78.3 45.7 %all-to-all-start.3 = ((f32[32,16,224]{2,1,0:T(8,128)}), f32[32,16,224]{2,1,0:T(8,128)S(1)}, u32[]{:S(2)}, u32[]{:S(2)}) async-start(f32[32,16,224]{2,1,0:T(8,128)} %broadcast_in_dim.112), calls=%async_computation.3 | async-start | bytes 1048576 | tf_op jit(solution)/shard_map/all_to_all | solution.py:91
  90.5 59.9 %all-gather.3.cloned.1.call-start = ((), (), s32[]{:S(2)}) async-start(), calls=%async_computation.6 | async-start | bytes 2088960 | tf_op jit(solution)/shard_map/all_gather | solution.py:59
  126.5 1.2 copy-start.4
  127.7 1.2 copy-start.2
  129.7 3.4 %collective-permute-start.1 = (f32[4,4,22,128]{3,1,0,2:T(4,128)S(1)}, f32[4,4,22,128]{3,1,0,2:T(4,128)S(1)}, u32[]{:S(2)}, u32[]{:S(2)}) collective-permute-start(f32[4,4,22,128]{3,1,0,2:T(4,128)S(1)} %copy.252), channel_id=1, source_target_pairs={{0,16},{16,0},{1,17},{17,1},{2,18},{18,2},{3,19},{19,3},{4,20},{20... | collective-permute-start | bytes 540680 | tf_op jit(solution)/shard_map/ppermute | solution.py:200
  134.3 20.8 %all-to-all-start.4 = ((f32[16,22,128]{2,1,0:T(8,128)}), f32[16,22,128]{2,1,0:T(8,128)S(1)}, u32[]{:S(2)}, u32[]{:S(2)}) async-start(f32[16,22,128]{2,1,0:T(8,128)} %copy.255), calls=%async_computation.4 | async-start | bytes 393216 | tf_op jit(solution)/shard_map/all_to_all | solution.py:225
  155.3 34.4 %copy-start.1 = (bf16[5120,160]{0,1:T(8,128)(2,1)S(1)}, bf16[5120,160]{0,1:T(8,128)(2,1)}, u32[]{:S(2)}) copy-start(bf16[5120,160]{0,1:T(8,128)(2,1)} %reshape.340) | copy-start | bytes 4915204
  157.0 32.4 %all-to-all-start.5 = ((bf16[32,20,128]{2,1,0:T(8,128)(2,1)}), bf16[32,20,128]{2,1,0:T(8,128)(2,1)S(1)}, u32[]{:S(2)}, u32[]{:S(2)}) async-start(bf16[32,20,128]{2,1,0:T(8,128)(2,1)} %broadcast_in_dim.121), calls=%async_computation.5 | async-start | bytes 393216 | tf_op jit(solution)/shard_map/all_to_all | solution.py:247
Sparse Core Ops, SparseCore 0:
  94.3 56.0 all-gather.2

commit v8 on v6

--- a/solution.py
+++ b/solution.py
@@ -56,7 +56,9 @@
     scale = float(HEAD_SIZE) ** (-0.5)
     seq_index = lax.axis_index(SEQ)
 
-    w_out_cols = lax.all_gather(w_out, "tensor", axis=0, tiled=True)
+    w_out_cols = lax.all_to_all(
+        jnp.broadcast_to(w_out[None], (tensor_count,) + w_out.shape), "tensor", 0, 0, tiled=True
+    ).reshape(-1, w_out.shape[1])
 
     xf = hidden.astype(jnp.float32)
     local_squares = jnp.sum(xf * xf, axis=2)

time: 183 us -> 191 us (1.044)
  between operations: 15.2 us -> 1.83 us
  local copies, waits for them, and re-layouts: 14.3 us -> 24.6 us
  other arithmetic: 7.77 us -> 14.7 us
  waiting for transfers between devices: 54.9 us -> 48.2 us
  starting transfers between devices: 45.7 us -> 51.2 us
  matrix products: 6.08 us -> 10.3 us
    all_to_all x1, waiting for transfers between devices: 6.78 us -> 1.65 us  [body(): arrived = lax.all_to_all(pair_packed, 'z', 0, 0, tiled=True)]
    all_to_all x0 -> x1, starting transfers between devices: none -> 3.72 us  [body(): lax.all_to_all(jnp.broadcast_to(w_out[None], (tensor_count,) + w_out.shap...]
    reshape x0 -> x1, local copies, waits for them, and re-layouts: none -> 2.56 us  [body(): w_out_cols = lax.all_to_all(jnp.broadcast_to(w_out[None], (tensor_count,)...]
    optimization_barrier x2 -> x1, local copies, waits for them, and re-layouts: 2.57 us -> 0.04 us  [body(): w_out_cols, arrived = lax.optimization_barrier((w_out_cols, arrived))]
    reduce_sum x2, other arithmetic: 0.75 us -> 3.07 us  [body(): local_weight = jnp.sum(prob_pre, axis=3) + jnp.sum(prob_suf, axis=3)]
    all_gather x1 -> x0, local copies, waits for them, and re-layouts: 2.24 us -> none  [body(): w_out_cols = lax.all_gather(w_out, 'tensor', axis=0, tiled=True)]
    all_to_all x0 -> x1, local copies, waits for them, and re-layouts: none -> 2.23 us  [body(): lax.all_to_all(jnp.broadcast_to(w_out[None], (tensor_count,) + w_out.shap...]
    unnamed x21 -> x41, local copies, waits for them, and re-layouts: 4.5 us -> 3.96 us
  transfers between devices with their start and end apart: 8 -> 8, of which waited for: 7 -> 6; matrix products, arithmetic and copies ran while one was open for 12% -> 20% of each run, Pallas kernels for 0% -> 0%
where the time goes in v8:
time: 191 us; the launch traced here: 189 us
  starting transfers between devices  51.2 us (27%)
  waiting for transfers between devices  48.2 us (25%)
  blocking collectives  38.2 us (20%)
  local copies, waits for them, and re-layouts  24.6 us (13%)
  other arithmetic  14.7 us (8%)
  matrix products  10.3 us (5%)
    all_gather x1, blocking collectives, body(): gathered = lax.all_gather(owned_rows, SEQ, axis=0, tiled=False)  38.2 us
    all_to_all x1, waiting for transfers between devices, body(): lax.all_to_all(jnp.broadcast_to(attention_slice[None], (seq_count,) + att...  17.2 us
    all_to_all x1, starting transfers between devices, body(): lax.all_to_all(jnp.broadcast_to(local_squares[None], (seq_count,) + local...  16.8 us
    all_to_all x1, waiting for transfers between devices, body(): reduced = jnp.sum(lax.all_to_all(chunks, 'z', 0, 0, tiled=True), axis=0)  13.7 us
    all_to_all x1, waiting for transfers between devices, body(): lax.all_to_all(jnp.broadcast_to(local_squares[None], (seq_count,) + local...  11.4 us
    all_to_all x1, starting transfers between devices, body(): lax.all_to_all(jnp.broadcast_to(attention_slice[None], (seq_count,) + att...  10.9 us
    all_to_all x1, starting transfers between devices, body(): owned_rows = lax.all_to_all(reduced, 'tensor', 0, 0, tiled=True)  6.75 us
    all_to_all x1, starting transfers between devices, body(): arrived = lax.all_to_all(pair_packed, 'z', 0, 0, tiled=True)  4.17 us
  transfers between devices with their start and end apart: 8, of which 6 were waited for; matrix products, arithmetic and copies ran while one was open for 20% of the time, Pallas kernels for 0%

profile of v8, /device:TPU:1, one launch (start us, length us, event | category | flops | bytes accessed | tf_op | source)
XLA Modules:
  0.0 188.9 jit_solution(1427831801556109272)
XLA Ops:
  0.6 1.1 fusion.20
  1.8 0.7 reshape.349
  2.5 16.8 %all-to-all-start.1 = ((f32[32,1,256]{2,1,0:T(1,128)}), f32[32,1,256]{2,1,0:T(1,128)S(1)}, u32[]{:S(2)}, u32[]{:S(2)}) async-start(f32[32,1,256]{2,1,0:T(1,128)} %reshape.349), calls=%async_computation.1 | async-start | bytes 65536 | tf_op jit(solution)/shard_map/all_to_all | solution.py:66
  19.9 11.4 %all-to-all-done.1 = f32[32,1,256]{2,1,0:T(1,128)S(1)} async-done(((f32[32,1,256]{2,1,0:T(1,128)}), f32[32,1,256]{2,1,0:T(1,128)S(1)}, u32[]{:S(2)}, u32[]{:S(2)}) %all-to-all-start.1) | async-done | bytes 32800 | tf_op jit(solution)/shard_map/all_to_all | solution.py:66
  31.9 0.7 reduce.1
  32.8 1.2 fusion.28
  35.0 3.2 %collective-permute-start = (f32[4,16,4,224]{3,1,2,0:T(8,128)S(1)}, f32[4,16,4,224]{3,1,2,0:T(8,128)S(1)}, u32[]{:S(2)}, u32[]{:S(2)}) collective-permute-start(f32[4,16,4,224]{3,1,2,0:T(8,128)S(1)} %bitcast.159), channel_id=1, source_target_pairs={{0,16},{16,0},{1,17},{17,1},{2,18},{18,2},{3,19},{19,3},{4,20},{20... | collective-permute-start | bytes 688136 | tf_op jit(solution)/shard_map/ppermute | solution.py:85
  39.6 0.8 bitcast_add_fusion
  40.4 3.7 %all-to-all-start.2 = ((f32[16,16,224]{2,1,0:T(8,128)}), f32[16,16,224]{2,1,0:T(8,128)S(1)}, u32[]{:S(2)}, u32[]{:S(2)}) async-start(f32[16,16,224]{2,1,0:T(8,128)} %bitcast.5), calls=%async_computation.2 | async-start | bytes 524288 | tf_op jit(solution)/shard_map/all_to_all | solution.py:87
  44.9 13.7 %all-to-all-done.2 = f32[16,16,224]{2,1,0:T(8,128)S(1)} async-done(((f32[16,16,224]{2,1,0:T(8,128)}), f32[16,16,224]{2,1,0:T(8,128)S(1)}, u32[]{:S(2)}, u32[]{:S(2)}) %all-to-all-start.2) | async-done | bytes 229408 | tf_op jit(solution)/shard_map/all_to_all | solution.py:87
  59.2 6.8 %all-to-all-start.3 = ((f32[16,1,224]{2,1,0:T(1,128)}), f32[16,1,224]{2,1,0:T(1,128)S(1)}, u32[]{:S(2)}, u32[]{:S(2)}) async-start(f32[16,1,224]{2,1,0:T(1,128)} %reshape_add_fusion), calls=%async_computation.3 | async-start | bytes 32768 | tf_op jit(solution)/shard_map/all_to_all | solution.py:92
  66.5 1.1 copy.322
  67.6 1.1 copy.323
  68.6 3.7 %all-to-all-done.3 = f32[16,1,224]{2,1,0:T(1,128)S(1)} async-done(((f32[16,1,224]{2,1,0:T(1,128)}), f32[16,1,224]{2,1,0:T(1,128)S(1)}, u32[]{:S(2)}, u32[]{:S(2)}) %all-to-all-start.3) | async-done | bytes 14368 | tf_op jit(solution)/shard_map/all_to_all | solution.py:92
  72.4 1.5 broadcast_in_dim.64
  73.9 3.7 %all-to-all-start = ((bf16[16,320,160]{1,2,0:T(8,128)(2,1)}), bf16[16,320,160]{1,2,0:T(8,128)(2,1)S(1)}, u32[]{:S(2)}, u32[]{:S(2)}) async-start(bf16[16,320,160]{1,2,0:T(8,128)(2,1)} %broadcast_in_dim.64), calls=%async_computation | async-start | bytes 3932160 | tf_op jit(solution)/shard_map/all_to_all | solution.py:59
  77.6 38.2 %all-gather = f32[512,1,224]{2,0,1:T(8,128)S(1)} all-gather(f32[16,1,224]{2,0,1:T(8,128)S(1)} %copy.265), channel_id=2, replica_groups=mesh['z'=16,'core'=2,'tensor'=16] {'z','core'}, dimensions={0}, use_global_device_ids=true | all-gather | bytes 473088 | tf_op jit(solution)/shard_map/all_gather | solution.py:93
  116.2 1.6 reshape.334
  117.8 1.5 slice_bitcast_fusion.1
  119.3 1.0 slice_bitcast_fusion
  120.9 1.4 fusion.69
  122.3 1.6 fusion.68
  124.6 1.8 fusion.10
  126.4 1.3 fusion.18
  127.8 1.7 convolution_bitcast_fusion
  130.2 2.1 %collective-permute-start.1 = (f32[4,4,22,128]{3,1,0,2:T(4,128)S(1)}, f32[4,4,22,128]{3,1,0,2:T(4,128)S(1)}, u32[]{:S(2)}, u32[]{:S(2)}) collective-permute-start(f32[4,4,22,128]{3,1,0,2:T(4,128)S(1)} %copy.289), channel_id=1, source_target_pairs={{0,16},{16,0},{1,17},{17,1},{2,18},{18,2},{3,19},{19,3},{4,20},{20... | collective-permute-start | bytes 540680 | tf_op jit(solution)/shard_map/ppermute | solution.py:200
  132.3 0.7 fusion.66
  134.2 1.4 copy.290
  135.6 1.4 copy.291
  137.0 1.0 fusion.27
  138.1 0.7 copy.292
  138.8 4.2 %all-to-all-start.4 = ((f32[16,22,128]{2,1,0:T(8,128)}), f32[16,22,128]{2,1,0:T(8,128)S(1)}, u32[]{:S(2)}, u32[]{:S(2)}) async-start(f32[16,22,128]{2,1,0:T(8,128)} %copy.292), calls=%async_computation.4 | async-start | bytes 393216 | tf_op jit(solution)/shard_map/all_to_all | solution.py:225
  143.0 1.0 multiply_subtract_fusion
  144.0 1.5 slice.111
  145.4 0.8 convert_element_type.62
  146.2 1.0 fusion.67
  147.2 0.8 fusion.33
  147.9 1.8 fusion.35
  149.7 2.2 %copy.261 = bf16[16,320,160]{1,0,2:T(8,128)(2,1)S(1)} copy(bf16[16,320,160]{1,2,0:T(8,128)(2,1)} %copy-done.1) | data formatting | bytes 3276800 | tf_op jit(solution)/shard_map/all_to_all | solution.py:59
  152.0 2.6 %reshape.330 = bf16[5120,160]{0,1:T(8,128)(2,1)} reshape(bf16[16,320,160]{1,0,2:T(8,128)(2,1)S(1)} %copy.261) | data formatting | bytes 3276800 | tf_op jit(solution)/shard_map/reshape | solution.py:61
  154.5 1.6 all-to-all-done.4
  156.4 0.9 fusion.46
  157.3 0.7 broadcast_in_dim.118
  158.0 10.9 %all-to-all-start.5 = ((bf16[32,20,128]{2,1,0:T(8,128)(2,1)}), bf16[32,20,128]{2,1,0:T(8,128)(2,1)S(1)}, u32[]{:S(2)}, u32[]{:S(2)}) async-start(bf16[32,20,128]{2,1,0:T(8,128)(2,1)} %broadcast_in_dim.118), calls=%async_computation.5 | async-start | bytes 393216 | tf_op jit(solution)/shard_map/all_to_all | solution.py:247
  168.9 0.7 copy.300
  169.6 0.7 fusion.47
  170.3 17.2 %all-to-all-done.5 = bf16[32,20,128]{2,1,0:T(8,128)(2,1)S(1)} async-done(((bf16[32,20,128]{2,1,0:T(8,128)(2,1)}), bf16[32,20,128]{2,1,0:T(8,128)(2,1)S(1)}, u32[]{:S(2)}, u32[]{:S(2)}) %all-to-all-start.5) | async-done | bytes 163872 | tf_op jit(solution)/shard_map/all_to_all | solution.py:247
  187.8 1.2 fusion
  (90 shorter events, 9.0 us)
Async XLA Ops:
  0.6 120.2 %copy-start = (bf16[4,128,1024]{2,1,0:T(8,128)(2,1)S(1)}, bf16[4,128,1024]{2,1,0:T(8,128)(2,1)}, u32[]{:S(2)}) copy-start(bf16[4,128,1024]{2,1,0:T(8,128)(2,1)} %param.18) | copy-start | bytes 3145732
  2.5 28.9 %all-to-all-start.1 = ((f32[32,1,256]{2,1,0:T(1,128)}), f32[32,1,256]{2,1,0:T(1,128)S(1)}, u32[]{:S(2)}, u32[]{:S(2)}) async-start(f32[32,1,256]{2,1,0:T(1,128)} %reshape.349), calls=%async_computation.1 | async-start | bytes 65536 | tf_op jit(solution)/shard_map/all_to_all | solution.py:66
  34.0 4.9 %copy-start.14 = (bf16[448]{0:T(512)(128)(2,1)S(1)}, bf16[448]{0:T(512)(128)(2,1)}, u32[]{:S(2)}) copy-start(bf16[448]{0:T(512)(128)(2,1)} %param.14) | copy-start | bytes 2692
  35.0 9.1 %copy-start.16 = (s32[4]{0:T(128)S(1)}, s32[4]{0:T(128)}, u32[]{:S(2)}) copy-start(s32[4]{0:T(128)} %param.21) | copy-start | bytes 52
  35.0 31.5 %copy-start.6 = (bf16[1,384,1024]{2,1,0:T(8,128)(2,1)S(1)}, bf16[1,384,1024]{2,1,0:T(8,128)(2,1)}, u32[]{:S(2)}) copy-start(bf16[1,384,1024]{2,1,0:T(8,128)(2,1)} %param.16) | copy-start | bytes 2359300
  35.0 4.5 %collective-permute-start = (f32[4,16,4,224]{3,1,2,0:T(8,128)S(1)}, f32[4,16,4,224]{3,1,2,0:T(8,128)S(1)}, u32[]{:S(2)}, u32[]{:S(2)}) collective-permute-start(f32[4,16,4,224]{3,1,2,0:T(8,128)S(1)} %bitcast.159), channel_id=1, source_target_pairs={{0,16},{16,0},{1,17},{17,1},{2,18},{18,2},{3,19},{19,3},{4,20},{20... | collective-permute-start | bytes 688136 | tf_op jit(solution)/shard_map/ppermute | solution.py:85
  40.4 27.2 %copy-start.7 = (bf16[1,384,1024]{2,1,0:T(8,128)(2,1)S(1)}, bf16[1,384,1024]{2,1,0:T(8,128)(2,1)}, u32[]{:S(2)}) copy-start(bf16[1,384,1024]{2,1,0:T(8,128)(2,1)} %param.17) | copy-start | bytes 2359300
  40.4 18.2 %all-to-all-start.2 = ((f32[16,16,224]{2,1,0:T(8,128)}), f32[16,16,224]{2,1,0:T(8,128)S(1)}, u32[]{:S(2)}, u32[]{:S(2)}) async-start(f32[16,16,224]{2,1,0:T(8,128)} %bitcast.5), calls=%async_computation.2 | async-start | bytes 524288 | tf_op jit(solution)/shard_map/all_to_all | solution.py:87
  44.9 23.8 %copy-start.11 = (f32[4,4,64]{2,0,1:T(4,128)}, f32[4,4,64]{2,0,1:T(4,128)S(1)}, u32[]{:S(2)}) copy-start(f32[4,4,64]{2,0,1:T(4,128)S(1)} %get-tuple-element.51) | copy-start | bytes 12292
  44.9 23.8 %copy-start.12 = (f32[4,4,64]{2,0,1:T(4,128)}, f32[4,4,64]{2,0,1:T(4,128)S(1)}, u32[]{:S(2)}) copy-start(f32[4,4,64]{2,0,1:T(4,128)S(1)} %get-tuple-element.52) | copy-start | bytes 12292
  59.2 13.2 %all-to-all-start.3 = ((f32[16,1,224]{2,1,0:T(1,128)}), f32[16,1,224]{2,1,0:T(1,128)S(1)}, u32[]{:S(2)}, u32[]{:S(2)}) async-start(f32[16,1,224]{2,1,0:T(1,128)} %reshape_add_fusion), calls=%async_computation.3 | async-start | bytes 32768 | tf_op jit(solution)/shard_map/all_to_all | solution.py:92
  67.6 4.8 %copy-start.10 = (bf16[320,160]{0,1:T(8,128)(2,1)S(1)}, bf16[320,160]{0,1:T(8,128)(2,1)}, u32[]{:S(2)}) copy-start(bf16[320,160]{0,1:T(8,128)(2,1)} %param.15) | copy-start | bytes 307204
  73.9 65.0 %all-to-all-start = ((bf16[16,320,160]{1,2,0:T(8,128)(2,1)}), bf16[16,320,160]{1,2,0:T(8,128)(2,1)S(1)}, u32[]{:S(2)}, u32[]{:S(2)}) async-start(bf16[16,320,160]{1,2,0:T(8,128)(2,1)} %broadcast_in_dim.64), calls=%async_computation | async-start | bytes 3932160 | tf_op jit(solution)/shard_map/all_to_all | solution.py:59
  119.3 1.6 copy-start.15
  120.6 1.7 copy-start.3
  120.6 1.7 copy-start.13
  124.6 3.1 %copy-start.2 = (f32[4,8,20,384]{3,2,0,1:T(8,128)S(1)}, f32[4,8,20,384]{3,2,0,1:T(8,128)}, u32[]{:S(2)}) copy-start(f32[4,8,20,384]{3,2,0,1:T(8,128)} %get-tuple-element.56) | copy-start | bytes 2949124
  127.8 1.7 copy-start.5
  129.9 2.4 %copy-start.8 = (f32[4,4,8,128]{3,2,1,0:T(8,128)S(1)}, f32[4,4,8,128]{3,2,1,0:T(8,128)}, u32[]{:S(2)}) copy-start(f32[4,4,8,128]{3,2,1,0:T(8,128)} %reshape.339) | copy-start | bytes 196612
  130.2 3.3 %collective-permute-start.1 = (f32[4,4,22,128]{3,1,0,2:T(4,128)S(1)}, f32[4,4,22,128]{3,1,0,2:T(4,128)S(1)}, u32[]{:S(2)}, u32[]{:S(2)}) collective-permute-start(f32[4,4,22,128]{3,1,0,2:T(4,128)S(1)} %copy.289), channel_id=1, source_target_pairs={{0,16},{16,0},{1,17},{17,1},{2,18},{18,2},{3,19},{19,3},{4,20},{20... | collective-permute-start | bytes 540680 | tf_op jit(solution)/shard_map/ppermute | solution.py:200
  138.8 9.1 %copy-start.1 = (bf16[16,320,160]{1,2,0:T(8,128)(2,1)}, bf16[16,320,160]{1,2,0:T(8,128)(2,1)S(1)}, u32[]{:S(2)}) copy-start(bf16[16,320,160]{1,2,0:T(8,128)(2,1)S(1)} %all-to-all-done) | copy-start | bytes 4915204
  138.8 17.4 %all-to-all-start.4 = ((f32[16,22,128]{2,1,0:T(8,128)}), f32[16,22,128]{2,1,0:T(8,128)S(1)}, u32[]{:S(2)}, u32[]{:S(2)}) async-start(f32[16,22,128]{2,1,0:T(8,128)} %copy.292), calls=%async_computation.4 | async-start | bytes 393216 | tf_op jit(solution)/shard_map/all_to_all | solution.py:225
  154.5 14.4 %copy-start.9 = (f32[4,4,1024]{2,0,1:T(4,128)S(1)}, f32[4,4,1024]{2,0,1:T(4,128)}, u32[]{:S(2)}) copy-start(f32[4,4,1024]{2,0,1:T(4,128)} %get-tuple-element.39) | copy-start | bytes 196612
  156.3 31.5 %copy-start.4 = (bf16[5120,160]{0,1:T(8,128)(2,1)S(1)}, bf16[5120,160]{0,1:T(8,128)(2,1)}, u32[]{:S(2)}) copy-start(bf16[5120,160]{0,1:T(8,128)(2,1)} %reshape.330) | copy-start | bytes 4915204
  158.0 29.5 %all-to-all-start.5 = ((bf16[32,20,128]{2,1,0:T(8,128)(2,1)}), bf16[32,20,128]{2,1,0:T(8,128)(2,1)S(1)}, u32[]{:S(2)}, u32[]{:S(2)}) async-start(bf16[32,20,128]{2,1,0:T(8,128)(2,1)} %broadcast_in_dim.118), calls=%async_computation.5 | async-start | bytes 393216 | tf_op jit(solution)/shard_map/all_to_all | solution.py:247

commit v9 on v8

--- a/solution.py
+++ b/solution.py
@@ -56,9 +56,9 @@
     scale = float(HEAD_SIZE) ** (-0.5)
     seq_index = lax.axis_index(SEQ)
 
-    w_out_cols = lax.all_to_all(
+    w_out_rows = lax.all_to_all(
         jnp.broadcast_to(w_out[None], (tensor_count,) + w_out.shape), "tensor", 0, 0, tiled=True
-    ).reshape(-1, w_out.shape[1])
+    )
 
     xf = hidden.astype(jnp.float32)
     local_squares = jnp.sum(xf * xf, axis=2)
@@ -123,6 +123,8 @@
         .transpose(1, 2, 0, 3, 4)
         .reshape(requests, KEY_HEADS, query_rows, HEAD_SIZE)
     )
+    w_out_rows, query_by_group = lax.optimization_barrier((w_out_rows, query_by_group))
+    w_out_cols = w_out_rows.reshape(-1, w_out.shape[1])
 
     prefix_key_block = prefix_key_cache[0].reshape(prefix_count, KEY_HEADS, HEAD_SIZE)
     prefix_value_block = prefix_value_cache[0].reshape(prefix_count, KEY_HEADS, HEAD_SIZE)

time: 191 us -> 188 us (0.984)
  waiting for transfers between devices: 48.2 us -> 56.7 us
  other arithmetic: 14.7 us -> 10.1 us
  matrix products: 10.3 us -> 7.79 us
    all_to_all x1, waiting for transfers between devices: 1.65 us -> 5.96 us  [body(): arrived = lax.all_to_all(pair_packed, 'z', 0, 0, tiled=True)]
    all_to_all x1, waiting for transfers between devices: 3.73 us -> 6.42 us  [body(): owned_rows = lax.all_to_all(reduced, 'tensor', 0, 0, tiled=True)]
    reduce_sum x2, other arithmetic: 3.07 us -> 0.75 us  [body(): local_weight = jnp.sum(prob_pre, axis=3) + jnp.sum(prob_suf, axis=3)]
    optimization_barrier x0 -> x1, local copies, waits for them, and re-layouts: none -> 2.24 us  [body(): lax.optimization_barrier((w_out_rows, query_by_group))]
    all_to_all x1 -> x0, local copies, waits for them, and re-layouts: 2.23 us -> none  [body(): lax.all_to_all(jnp.broadcast_to(w_out[None], (tensor_count,) + w_out.shap...]
    unnamed x41 -> x33, local copies, waits for them, and re-layouts: 3.96 us -> 6.09 us
  transfers between devices with their start and end apart: 8 -> 8, of which waited for: 6 -> 7; matrix products, arithmetic and copies ran while one was open for 20% -> 12% of each run, Pallas kernels for 0% -> 0%
where the time goes in v9:
time: 188 us; the launch traced here: 187 us
  waiting for transfers between devices  56.7 us (30%)
  starting transfers between devices  49.3 us (26%)
  blocking collectives  38.2 us (20%)
  local copies, waits for them, and re-layouts  22.7 us (12%)
  other arithmetic  10.1 us (5%)
  matrix products  7.79 us (4%)
    all_gather x1, blocking collectives, body(): gathered = lax.all_gather(owned_rows, SEQ, axis=0, tiled=False)  38.2 us
    all_to_all x1, waiting for transfers between devices, body(): lax.all_to_all(jnp.broadcast_to(attention_slice[None], (seq_count,) + att...  17.2 us
    all_to_all x1, starting transfers between devices, body(): lax.all_to_all(jnp.broadcast_to(local_squares[None], (seq_count,) + local...  16.8 us
    all_to_all x1, waiting for transfers between devices, body(): reduced = jnp.sum(lax.all_to_all(chunks, 'z', 0, 0, tiled=True), axis=0)  14.1 us
    all_to_all x1, waiting for transfers between devices, body(): lax.all_to_all(jnp.broadcast_to(local_squares[None], (seq_count,) + local...  11.4 us
    all_to_all x1, starting transfers between devices, body(): lax.all_to_all(jnp.broadcast_to(attention_slice[None], (seq_count,) + att...  9.16 us
    all_to_all x1, starting transfers between devices, body(): owned_rows = lax.all_to_all(reduced, 'tensor', 0, 0, tiled=True)  6.75 us
    all_to_all x1, waiting for transfers between devices, body(): owned_rows = lax.all_to_all(reduced, 'tensor', 0, 0, tiled=True)  6.42 us
  transfers between devices with their start and end apart: 8, of which 7 were waited for; matrix products, arithmetic and copies ran while one was open for 12% of the time, Pallas kernels for 0%

profile of v9, /device:TPU:1, one launch (start us, length us, event | category | flops | bytes accessed | tf_op | source)
XLA Modules:
  0.0 186.6 jit_solution(2538530101375201763)
XLA Ops:
  0.6 1.1 fusion.20
  1.8 0.7 reshape.349
  2.5 16.8 %all-to-all-start.1 = ((f32[32,1,256]{2,1,0:T(1,128)}), f32[32,1,256]{2,1,0:T(1,128)S(1)}, u32[]{:S(2)}, u32[]{:S(2)}) async-start(f32[32,1,256]{2,1,0:T(1,128)} %reshape.349), calls=%async_computation.1 | async-start | bytes 65536 | tf_op jit(solution)/shard_map/all_to_all | solution.py:66
  19.3 0.7 convert_element_type.53
  19.9 11.4 %all-to-all-done.1 = f32[32,1,256]{2,1,0:T(1,128)S(1)} async-done(((f32[32,1,256]{2,1,0:T(1,128)}), f32[32,1,256]{2,1,0:T(1,128)S(1)}, u32[]{:S(2)}, u32[]{:S(2)}) %all-to-all-start.1) | async-done | bytes 32800 | tf_op jit(solution)/shard_map/all_to_all | solution.py:66
  31.4 0.5 broadcast.184
  31.9 0.7 reduce.1
  32.8 1.2 fusion.28
  35.0 3.0 %collective-permute-start = (f32[4,16,4,224]{3,1,2,0:T(8,128)S(1)}, f32[4,16,4,224]{3,1,2,0:T(8,128)S(1)}, u32[]{:S(2)}, u32[]{:S(2)}) collective-permute-start(f32[4,16,4,224]{3,1,2,0:T(8,128)S(1)} %bitcast.159), channel_id=1, source_target_pairs={{0,16},{16,0},{1,17},{17,1},{2,18},{18,2},{3,19},{19,3},{4,20},{20... | collective-permute-start | bytes 688136 | tf_op jit(solution)/shard_map/ppermute | solution.py:85
  39.2 0.8 bitcast_add_fusion
  40.0 3.5 %all-to-all-start.2 = ((f32[16,16,224]{2,1,0:T(8,128)}), f32[16,16,224]{2,1,0:T(8,128)S(1)}, u32[]{:S(2)}, u32[]{:S(2)}) async-start(f32[16,16,224]{2,1,0:T(8,128)} %bitcast.4), calls=%async_computation.2 | async-start | bytes 524288 | tf_op jit(solution)/shard_map/all_to_all | solution.py:87
  43.8 14.1 %all-to-all-done.2 = f32[16,16,224]{2,1,0:T(8,128)S(1)} async-done(((f32[16,16,224]{2,1,0:T(8,128)}), f32[16,16,224]{2,1,0:T(8,128)S(1)}, u32[]{:S(2)}, u32[]{:S(2)}) %all-to-all-start.2) | async-done | bytes 229408 | tf_op jit(solution)/shard_map/all_to_all | solution.py:87
  57.9 0.6 reshape_add_fusion
  58.5 6.8 %all-to-all-start.3 = ((f32[16,1,224]{2,1,0:T(1,128)}), f32[16,1,224]{2,1,0:T(1,128)S(1)}, u32[]{:S(2)}, u32[]{:S(2)}) async-start(f32[16,1,224]{2,1,0:T(1,128)} %reshape_add_fusion), calls=%async_computation.3 | async-start | bytes 32768 | tf_op jit(solution)/shard_map/all_to_all | solution.py:92
  65.3 6.4 %all-to-all-done.3 = f32[16,1,224]{2,1,0:T(1,128)S(1)} async-done(((f32[16,1,224]{2,1,0:T(1,128)}), f32[16,1,224]{2,1,0:T(1,128)S(1)}, u32[]{:S(2)}, u32[]{:S(2)}) %all-to-all-start.3) | async-done | bytes 14368 | tf_op jit(solution)/shard_map/all_to_all | solution.py:92
  71.7 1.5 broadcast_in_dim.64
  73.2 3.7 %all-to-all-start = ((bf16[16,320,160]{1,2,0:T(8,128)(2,1)}), bf16[16,320,160]{1,2,0:T(8,128)(2,1)S(1)}, u32[]{:S(2)}, u32[]{:S(2)}) async-start(bf16[16,320,160]{1,2,0:T(8,128)(2,1)} %broadcast_in_dim.64), calls=%async_computation | async-start | bytes 3932160 | tf_op jit(solution)/shard_map/all_to_all | solution.py:59
  76.9 0.6 add_compare_fusion
  77.5 0.6 copy.268
  78.1 0.6 copy.270
  78.7 2.2 %copy.323 = bf16[48,8,8,128]{3,2,1,0:T(8,128)(2,1)} copy(bf16[48,8,8,128]{3,1,2,0:T(8,128)(2,1)} %bitcast.152) | data formatting | bytes 1572864
  80.9 1.1 copy.324
  82.0 0.5 iota_compare_fusion
  82.5 0.6 broadcast_compare_fusion
  83.2 38.2 %all-gather = f32[512,1,224]{2,0,1:T(8,128)S(1)} all-gather(f32[16,1,224]{2,0,1:T(8,128)S(1)} %copy.265), channel_id=2, replica_groups=mesh['z'=16,'core'=2,'tensor'=16] {'z','core'}, dimensions={0}, use_global_device_ids=true | all-gather | bytes 473088 | tf_op jit(solution)/shard_map/all_gather | solution.py:93
  121.8 1.6 reshape.333
  123.4 1.0 slice_bitcast_fusion
  124.4 1.0 subtract_convert_fusion
  125.6 1.5 slice_bitcast_fusion.1
  127.2 2.4 %fusion.68 = (f32[4,8,20]{2,0,1:T(4,128)S(1)}, f32[4,8,20,384]{3,2,0,1:T(8,128)S(1)}) fusion(bf16[384,8,128,1]{2,1,0,3:T(8,128)(2,1)} %bitcast.146, bf16[4,8,20,128]{3,1,2,0:T(8,128)(2,1)S(1)} %bitcast.149, pred[384]{0:T(512)(128)(4,1)S(1)} %copy-done.9), kind=kOutput, calls=%fused_computation.124 | convolution fusion | flops 63651200 | bytes 1936256 | tf_op jit(solution)/shard_map/rhqd,phd->rhqp/dot_general | solution.py:134
  129.6 0.7 fusion.69
  132.0 0.7 copy-done.3
  133.5 2.1 %collective-permute-start.1 = (f32[4,4,22,128]{3,1,0,2:T(4,128)S(1)}, f32[4,4,22,128]{3,1,0,2:T(4,128)S(1)}, u32[]{:S(2)}, u32[]{:S(2)}) collective-permute-start(f32[4,4,22,128]{3,1,0,2:T(4,128)S(1)} %copy.290), channel_id=1, source_target_pairs={{0,16},{16,0},{1,17},{17,1},{2,18},{18,2},{3,19},{19,3},{4,20},{20... | collective-permute-start | bytes 540680 | tf_op jit(solution)/shard_map/ppermute | solution.py:202
  135.6 1.2 collective-permute-done.1
  137.3 0.8 copy.293
  138.1 4.2 %all-to-all-start.4 = ((f32[16,22,128]{2,1,0:T(8,128)}), f32[16,22,128]{2,1,0:T(8,128)S(1)}, u32[]{:S(2)}, u32[]{:S(2)}) async-start(f32[16,22,128]{2,1,0:T(8,128)} %copy.293), calls=%async_computation.4 | async-start | bytes 393216 | tf_op jit(solution)/shard_map/all_to_all | solution.py:227
  142.4 0.9 slice.111
  143.3 2.2 %copy.272 = bf16[16,320,160]{1,0,2:T(8,128)(2,1)S(1)} copy(bf16[16,320,160]{1,2,0:T(8,128)(2,1)} %copy-done.1) | data formatting | bytes 3276800 | tf_op jit(solution)/shard_map/optimization_barrier | solution.py:126
  145.6 2.5 %reshape.336 = bf16[5120,160]{0,1:T(8,128)(2,1)} reshape(bf16[16,320,160]{1,0,2:T(8,128)(2,1)S(1)} %copy.272) | data formatting | bytes 3276800 | tf_op jit(solution)/shard_map/reshape | solution.py:127
  148.5 1.1 fusion.35
  149.5 6.0 %all-to-all-done.4 = f32[16,22,128]{2,1,0:T(8,128)S(1)} async-done(((f32[16,22,128]{2,1,0:T(8,128)}), f32[16,22,128]{2,1,0:T(8,128)S(1)}, u32[]{:S(2)}, u32[]{:S(2)}) %all-to-all-start.4) | async-done | bytes 180256 | tf_op jit(solution)/shard_map/all_to_all | solution.py:227
  155.8 0.9 fusion.46
  156.6 0.7 broadcast_in_dim.118
  157.4 9.2 %all-to-all-start.5 = ((bf16[32,20,128]{2,1,0:T(8,128)(2,1)}), bf16[32,20,128]{2,1,0:T(8,128)(2,1)S(1)}, u32[]{:S(2)}, u32[]{:S(2)}) async-start(bf16[32,20,128]{2,1,0:T(8,128)(2,1)} %broadcast_in_dim.118), calls=%async_computation.5 | async-start | bytes 393216 | tf_op jit(solution)/shard_map/all_to_all | solution.py:249
  166.5 0.7 copy.301
  167.2 0.7 fusion.47
  168.0 17.2 %all-to-all-done.5 = bf16[32,20,128]{2,1,0:T(8,128)(2,1)S(1)} async-done(((bf16[32,20,128]{2,1,0:T(8,128)(2,1)}), bf16[32,20,128]{2,1,0:T(8,128)(2,1)S(1)}, u32[]{:S(2)}, u32[]{:S(2)}) %all-to-all-start.5) | async-done | bytes 163872 | tf_op jit(solution)/shard_map/all_to_all | solution.py:249
  185.4 1.2 fusion
  (82 shorter events, 6.4 us)
Async XLA Ops:
  0.6 129.0 %copy-start = (bf16[4,128,1024]{2,1,0:T(8,128)(2,1)S(1)}, bf16[4,128,1024]{2,1,0:T(8,128)(2,1)}, u32[]{:S(2)}) copy-start(bf16[4,128,1024]{2,1,0:T(8,128)(2,1)} %param.18) | copy-start | bytes 3145732
  2.5 28.9 %all-to-all-start.1 = ((f32[32,1,256]{2,1,0:T(1,128)}), f32[32,1,256]{2,1,0:T(1,128)S(1)}, u32[]{:S(2)}, u32[]{:S(2)}) async-start(f32[32,1,256]{2,1,0:T(1,128)} %reshape.349), calls=%async_computation.1 | async-start | bytes 65536 | tf_op jit(solution)/shard_map/all_to_all | solution.py:66
  34.0 4.7 %copy-start.10 = (bf16[448]{0:T(512)(128)(2,1)S(1)}, bf16[448]{0:T(512)(128)(2,1)}, u32[]{:S(2)}) copy-start(bf16[448]{0:T(512)(128)(2,1)} %param.14) | copy-start | bytes 2692
  35.0 8.6 %copy-start.12 = (s32[4]{0:T(128)S(1)}, s32[4]{0:T(128)}, u32[]{:S(2)}) copy-start(s32[4]{0:T(128)} %param.21) | copy-start | bytes 52
  35.0 36.8 %copy-start.7 = (bf16[320,160]{0,1:T(8,128)(2,1)S(1)}, bf16[320,160]{0,1:T(8,128)(2,1)}, u32[]{:S(2)}) copy-start(bf16[320,160]{0,1:T(8,128)(2,1)} %param.15) | copy-start | bytes 307204
  35.0 4.2 %collective-permute-start = (f32[4,16,4,224]{3,1,2,0:T(8,128)S(1)}, f32[4,16,4,224]{3,1,2,0:T(8,128)S(1)}, u32[]{:S(2)}, u32[]{:S(2)}) collective-permute-start(f32[4,16,4,224]{3,1,2,0:T(8,128)S(1)} %bitcast.159), channel_id=1, source_target_pairs={{0,16},{16,0},{1,17},{17,1},{2,18},{18,2},{3,19},{19,3},{4,20},{20... | collective-permute-start | bytes 688136 | tf_op jit(solution)/shard_map/ppermute | solution.py:85
  40.0 17.9 %all-to-all-start.2 = ((f32[16,16,224]{2,1,0:T(8,128)}), f32[16,16,224]{2,1,0:T(8,128)S(1)}, u32[]{:S(2)}, u32[]{:S(2)}) async-start(f32[16,16,224]{2,1,0:T(8,128)} %bitcast.4), calls=%async_computation.2 | async-start | bytes 524288 | tf_op jit(solution)/shard_map/all_to_all | solution.py:87
  58.5 13.2 %all-to-all-start.3 = ((f32[16,1,224]{2,1,0:T(1,128)}), f32[16,1,224]{2,1,0:T(1,128)S(1)}, u32[]{:S(2)}, u32[]{:S(2)}) async-start(f32[16,1,224]{2,1,0:T(1,128)} %reshape_add_fusion), calls=%async_computation.3 | async-start | bytes 32768 | tf_op jit(solution)/shard_map/all_to_all | solution.py:92
  73.2 54.0 %all-to-all-start = ((bf16[16,320,160]{1,2,0:T(8,128)(2,1)}), bf16[16,320,160]{1,2,0:T(8,128)(2,1)S(1)}, u32[]{:S(2)}, u32[]{:S(2)}) async-start(bf16[16,320,160]{1,2,0:T(8,128)(2,1)} %broadcast_in_dim.64), calls=%async_computation | async-start | bytes 3932160 | tf_op jit(solution)/shard_map/all_to_all | solution.py:59
  77.5 3.4 %copy-start.4 = (bf16[1,384,1024]{2,1,0:T(8,128)(2,1)S(1)}, bf16[1,384,1024]{2,1,0:T(8,128)(2,1)}, u32[]{:S(2)}) copy-start(bf16[1,384,1024]{2,1,0:T(8,128)(2,1)} %param.17) | copy-start | bytes 2359300
  124.4 2.8 %copy-start.9 = (pred[384]{0:T(512)(128)(4,1)S(1)}, pred[384]{0:T(512)(128)(4,1)}, u32[]{:S(2)}) copy-start(pred[384]{0:T(512)(128)(4,1)} %add_compare_fusion) | copy-start | bytes 1156
  127.2 2.5 %copy-start.11 = (pred[4,128]{1,0:T(4,128)(4,1)S(1)}, pred[4,128]{1,0:T(4,128)(4,1)}, u32[]{:S(2)}) copy-start(pred[4,128]{1,0:T(4,128)(4,1)} %broadcast_compare_fusion) | copy-start | bytes 1540
  127.2 3.2 %copy-start.1 = (bf16[16,320,160]{1,2,0:T(8,128)(2,1)}, bf16[16,320,160]{1,2,0:T(8,128)(2,1)S(1)}, u32[]{:S(2)}) copy-start(bf16[16,320,160]{1,2,0:T(8,128)(2,1)S(1)} %all-to-all-done) | copy-start | bytes 4915204
  130.4 1.1 copy-start.5
  131.5 1.2 copy-start.3
  133.5 3.3 %collective-permute-start.1 = (f32[4,4,22,128]{3,1,0,2:T(4,128)S(1)}, f32[4,4,22,128]{3,1,0,2:T(4,128)S(1)}, u32[]{:S(2)}, u32[]{:S(2)}) collective-permute-start(f32[4,4,22,128]{3,1,0,2:T(4,128)S(1)} %copy.290), channel_id=1, source_target_pairs={{0,16},{16,0},{1,17},{17,1},{2,18},{18,2},{3,19},{19,3},{4,20},{20... | collective-permute-start | bytes 540680 | tf_op jit(solution)/shard_map/ppermute | solution.py:202
  138.1 17.4 %all-to-all-start.4 = ((f32[16,22,128]{2,1,0:T(8,128)}), f32[16,22,128]{2,1,0:T(8,128)S(1)}, u32[]{:S(2)}, u32[]{:S(2)}) async-start(f32[16,22,128]{2,1,0:T(8,128)} %copy.293), calls=%async_computation.4 | async-start | bytes 393216 | tf_op jit(solution)/shard_map/all_to_all | solution.py:227
  145.5 2.5 %copy-start.8 = (pred[20,4]{0,1:T(4,128)(4,1)S(1)}, pred[20,4]{0,1:T(4,128)(4,1)}, u32[]{:S(2)}) copy-start(pred[20,4]{0,1:T(4,128)(4,1)} %iota_compare_fusion) | copy-start | bytes 244
  148.1 18.4 %copy-start.6 = (f32[4,4,1024]{2,0,1:T(4,128)S(1)}, f32[4,4,1024]{2,0,1:T(4,128)}, u32[]{:S(2)}) copy-start(f32[4,4,1024]{2,0,1:T(4,128)} %get-tuple-element.43) | copy-start | bytes 196612
  155.6 29.8 %copy-start.2 = (bf16[5120,160]{0,1:T(8,128)(2,1)S(1)}, bf16[5120,160]{0,1:T(8,128)(2,1)}, u32[]{:S(2)}) copy-start(bf16[5120,160]{0,1:T(8,128)(2,1)} %reshape.336) | copy-start | bytes 4915204
  157.4 27.8 %all-to-all-start.5 = ((bf16[32,20,128]{2,1,0:T(8,128)(2,1)}), bf16[32,20,128]{2,1,0:T(8,128)(2,1)S(1)}, u32[]{:S(2)}, u32[]{:S(2)}) async-start(bf16[32,20,128]{2,1,0:T(8,128)(2,1)} %broadcast_in_dim.118), calls=%async_computation.5 | async-start | bytes 393216 | tf_op jit(solution)/shard_map/all_to_all | solution.py:249

commit v10 on v6

--- a/solution.py
+++ b/solution.py
@@ -77,17 +77,18 @@
     groups = request_total // requests
     core = lax.axis_index("core")
     plane_count = seq_count // halves
-    by_half = partial_value.reshape(steps, groups, requests, halves, half_width)
-    keep = lax.dynamic_index_in_dim(by_half, core, axis=3, keepdims=False)
-    send = lax.dynamic_index_in_dim(by_half, 1 - core, axis=3, keepdims=False)
-    pair_sum = keep + lax.ppermute(send, "core", [(0, 1), (1, 0)])
-    chunks = pair_sum.transpose(0, 2, 1, 3).reshape(plane_count, groups, half_width)
-    reduced = jnp.sum(lax.all_to_all(chunks, "z", 0, 0, tiled=True), axis=0)
-    bias = lax.dynamic_slice_in_dim(
-        b_qkv.astype(jnp.float32), (seq_index % halves) * half_width, half_width
-    )
-    reduced = reduced + bias[None, :]
-    owned_rows = lax.all_to_all(reduced, "tensor", 0, 0, tiled=True)
+    partial_value = partial_value + jnp.where(seq_index == 0, b_qkv.astype(jnp.float32), 0.0)
+    by_dest = (
+        partial_value.reshape(steps, groups, requests, halves, half_width)
+        .transpose(3, 1, 0, 2, 4)
+        .reshape(halves * groups, steps, requests, half_width)
+    )
+    came = lax.all_to_all(by_dest, ("core", "tensor"), 0, 0, tiled=True).reshape(
+        halves, tensor_count, steps, requests, half_width
+    )
+    pair_sum = jnp.sum(came, axis=0)
+    chunks = pair_sum.transpose(1, 2, 0, 3).reshape(plane_count, tensor_count, half_width)
+    owned_rows = jnp.sum(lax.all_to_all(chunks, "z", 0, 0, tiled=True), axis=0)
     gathered = lax.all_gather(owned_rows, SEQ, axis=0, tiled=False)
     combined_output = (
         gathered.reshape(steps, requests, halves, tensor_count, half_width)

time: 183 us -> 185 us (1.011)
  waiting for transfers between devices: 54.9 us -> 57.4 us
    all_to_all x2, waiting for transfers between devices: 18 us -> 22.3 us  [the longest x1 12 us: body(): lax.all_to_all(by_dest, ('core', 'tensor'), 0, 0, tiled=True)]
    ppermute x1 -> x0, starting transfers between devices: 3.16 us -> none  [body(): pair_sum = keep + lax.ppermute(send, 'core', [(0, 1), (1, 0)])]
    unnamed x21 -> x20, local copies, waits for them, and re-layouts: 4.5 us -> 5.36 us
  transfers between devices with their start and end apart: 8 -> 7, of which waited for: 7 -> 6; matrix products, arithmetic and copies ran while one was open for 12% -> 13% of each run, Pallas kernels for 0% -> 0%
where the time goes in v10:
time: 185 us; the launch traced here: 184 us
  waiting for transfers between devices  57.4 us (31%)
  starting transfers between devices  45.3 us (24%)
  blocking collectives  37 us (20%)
  local copies, waits for them, and re-layouts  15.9 us (9%)
  between operations  15.2 us (8%)
  other arithmetic  7.27 us (4%)
  matrix products  6.08 us (3%)
    all_gather x1, blocking collectives, body(): gathered = lax.all_gather(owned_rows, SEQ, axis=0, tiled=False)  37 us
    all_to_all x1, waiting for transfers between devices, body(): lax.all_to_all(jnp.broadcast_to(attention_slice[None], (seq_count,) + att...  17.2 us
    all_to_all x1, starting transfers between devices, body(): lax.all_to_all(jnp.broadcast_to(local_squares[None], (seq_count,) + local...  16.7 us
    all_to_all x1, waiting for transfers between devices, body(): lax.all_to_all(by_dest, ('core', 'tensor'), 0, 0, tiled=True)  12 us
    all_to_all x1, waiting for transfers between devices, body(): owned_rows = jnp.sum(lax.all_to_all(chunks, 'z', 0, 0, tiled=True), axis=0)  10.2 us
    all_to_all x1, waiting for transfers between devices, body(): lax.all_to_all(jnp.broadcast_to(local_squares[None], (seq_count,) + local...  9.36 us
    all_to_all x1, starting transfers between devices, body(): lax.all_to_all(jnp.broadcast_to(attention_slice[None], (seq_count,) + att...  9.16 us
    all_to_all x1, starting transfers between devices, body(): lax.all_to_all(by_dest, ('core', 'tensor'), 0, 0, tiled=True)  8.22 us
  transfers between devices with their start and end apart: 7, of which 6 were waited for; matrix products, arithmetic and copies ran while one was open for 13% of the time, Pallas kernels for 0%

profile of v10, /device:TPU:1, one launch (start us, length us, event | category | flops | bytes accessed | tf_op | source)
XLA Modules:
  0.0 184.1 jit_solution(15912692584347907204)
XLA Ops:
  7.2 1.1 fusion.20
  8.3 0.7 reshape.327
  9.0 16.7 %all-to-all-start = ((f32[32,1,256]{2,1,0:T(1,128)}), f32[32,1,256]{2,1,0:T(1,128)S(1)}, u32[]{:S(2)}, u32[]{:S(2)}) async-start(f32[32,1,256]{2,1,0:T(1,128)} %reshape.327), calls=%async_computation | async-start | bytes 65536 | tf_op jit(solution)/shard_map/all_to_all | solution.py:64
  25.8 0.7 all-gather.4.cloned.1.call-update
  26.5 0.7 convert_select_fusion
  27.2 0.7 convert_element_type.53
  28.5 9.4 %all-to-all-done = f32[32,1,256]{2,1,0:T(1,128)S(1)} async-done(((f32[32,1,256]{2,1,0:T(1,128)}), f32[32,1,256]{2,1,0:T(1,128)S(1)}, u32[]{:S(2)}, u32[]{:S(2)}) %all-to-all-start) | async-done | bytes 32800 | tf_op jit(solution)/shard_map/all_to_all | solution.py:64
  37.9 0.5 broadcast.168
  38.4 0.7 reduce.1
  39.3 1.3 convolution_add_fusion
  40.5 0.4 reshape.305
  41.2 1.1 copy.228
  42.3 8.2 %all-to-all-start.1 = ((f32[32,4,4,224]{3,2,1,0:T(4,128)}), f32[32,4,4,224]{3,2,1,0:T(4,128)S(1)}, u32[]{:S(2)}, u32[]{:S(2)}) async-start(f32[32,4,4,224]{3,2,1,0:T(4,128)} %copy.228), calls=%async_computation.1 | async-start | bytes 1048576 | tf_op jit(solution)/shard_map/all_to_all | solution.py:86
  50.7 12.0 %all-to-all-done.1 = f32[32,4,4,224]{3,2,1,0:T(4,128)S(1)} async-done(((f32[32,4,4,224]{3,2,1,0:T(4,128)}), f32[32,4,4,224]{3,2,1,0:T(4,128)S(1)}, u32[]{:S(2)}, u32[]{:S(2)}) %all-to-all-start.1) | async-done | bytes 458784 | tf_op jit(solution)/shard_map/all_to_all | solution.py:86
  62.9 0.9 copy.280
  63.8 3.5 %all-to-all-start.2 = ((f32[16,16,224]{2,1,0:T(8,128)}), f32[16,16,224]{2,1,0:T(8,128)S(1)}, u32[]{:S(2)}, u32[]{:S(2)}) async-start(f32[16,16,224]{2,1,0:T(8,128)} %bitcast.7), calls=%async_computation.2 | async-start | bytes 524288 | tf_op jit(solution)/shard_map/all_to_all | solution.py:91
  67.7 2.2 %copy.288 = bf16[48,8,8,128]{3,2,1,0:T(8,128)(2,1)} copy(bf16[48,8,8,128]{3,1,2,0:T(8,128)(2,1)} %bitcast.155) | data formatting | bytes 1572864
  70.0 10.2 %all-to-all-done.2 = f32[16,16,224]{2,1,0:T(8,128)S(1)} async-done(((f32[16,16,224]{2,1,0:T(8,128)}), f32[16,16,224]{2,1,0:T(8,128)S(1)}, u32[]{:S(2)}, u32[]{:S(2)}) %all-to-all-start.2) | async-done | bytes 229408 | tf_op jit(solution)/shard_map/all_to_all | solution.py:91
  80.3 37.0 %all-gather = f32[512,224]{1,0:T(8,128)S(1)} all-gather(f32[16,224]{1,0:T(8,128)S(1)} %reduce_sum.84), channel_id=2, replica_groups=mesh['z'=16,'core'=2,'tensor'=16] {'z','core'}, dimensions={0}, use_global_device_ids=true | all-gather | bytes 473088 | tf_op jit(solution)/shard_map/all_gather | solution.py:92
  117.3 0.4 copy.230
  117.7 0.8 reshape.310
  118.6 0.3 subtract_convert_fusion
  118.8 0.2 maximum_bitcast_fusion
  119.1 0.7 fusion.67
  119.8 0.7 fusion.68
  120.6 0.4 fusion.10
  121.0 0.5 convolution_bitcast_fusion
  121.5 0.3 fusion.18
  121.9 0.4 copy-done.2
  122.2 0.4 convolution_add_fusion.1
  122.6 0.2 copy_dynamic-update-slice_fusion
  123.0 2.1 %collective-permute-start = (f32[4,4,22,128]{3,1,0,2:T(4,128)S(1)}, f32[4,4,22,128]{3,1,0,2:T(4,128)S(1)}, u32[]{:S(2)}, u32[]{:S(2)}) collective-permute-start(f32[4,4,22,128]{3,1,0,2:T(4,128)S(1)} %copy.253), channel_id=1, source_target_pairs={{0,16},{16,0},{1,17},{17,1},{2,18},{18,2},{3,19},{19,3},{4,20},{20... | collective-permute-start | bytes 540680 | tf_op jit(solution)/shard_map/ppermute | solution.py:199
  125.2 1.1 collective-permute-done
  126.6 0.2 fusion.27
  126.8 0.7 copy.256
  127.5 5.5 %all-to-all-start.3 = ((f32[16,22,128]{2,1,0:T(8,128)}), f32[16,22,128]{2,1,0:T(8,128)S(1)}, u32[]{:S(2)}, u32[]{:S(2)}) async-start(f32[16,22,128]{2,1,0:T(8,128)} %copy.256), calls=%async_computation.3 | async-start | bytes 393216 | tf_op jit(solution)/shard_map/all_to_all | solution.py:224
  133.2 0.3 fusion.66
  133.5 1.1 fusion.34
  134.6 2.2 %copy.225 = bf16[16,320,160]{1,0,2:T(8,128)(2,1)S(1)} copy(bf16[16,320,160]{1,2,0:T(8,128)(2,1)} %all-gather.4.cloned.1.call-done) | data formatting | bytes 3276800 | tf_op jit(solution)/shard_map/all_gather | solution.py:59
  136.9 2.5 %reshape.322 = bf16[5120,160]{0,1:T(8,128)(2,1)} reshape(bf16[16,320,160]{1,0,2:T(8,128)(2,1)S(1)} %copy.225) | data formatting | bytes 3276800 | tf_op jit(solution)/shard_map/optimization_barrier | solution.py:225
  139.4 6.8 %all-to-all-done.3 = f32[16,22,128]{2,1,0:T(8,128)S(1)} async-done(((f32[16,22,128]{2,1,0:T(8,128)}), f32[16,22,128]{2,1,0:T(8,128)S(1)}, u32[]{:S(2)}, u32[]{:S(2)}) %all-to-all-start.3) | async-done | bytes 180256 | tf_op jit(solution)/shard_map/all_to_all | solution.py:224
  146.5 0.9 fusion.45
  147.4 0.7 broadcast_in_dim.116
  148.1 9.2 %all-to-all-start.4 = ((bf16[32,20,128]{2,1,0:T(8,128)(2,1)}), bf16[32,20,128]{2,1,0:T(8,128)(2,1)S(1)}, u32[]{:S(2)}, u32[]{:S(2)}) async-start(bf16[32,20,128]{2,1,0:T(8,128)(2,1)} %broadcast_in_dim.116), calls=%async_computation.4 | async-start | bytes 393216 | tf_op jit(solution)/shard_map/all_to_all | solution.py:246
  157.2 0.7 copy.264
  157.9 0.7 fusion.46
  158.6 17.2 %all-to-all-done.4 = bf16[32,20,128]{2,1,0:T(8,128)(2,1)S(1)} async-done(((bf16[32,20,128]{2,1,0:T(8,128)(2,1)}), bf16[32,20,128]{2,1,0:T(8,128)(2,1)S(1)}, u32[]{:S(2)}, u32[]{:S(2)}) %all-to-all-start.4) | async-done | bytes 163872 | tf_op jit(solution)/shard_map/all_to_all | solution.py:246
  176.1 1.2 fusion
  (65 shorter events, 2.3 us)
Async XLA Ops:
  7.2 112.6 %copy-start = (bf16[4,128,1024]{2,1,0:T(8,128)(2,1)S(1)}, bf16[4,128,1024]{2,1,0:T(8,128)(2,1)}, u32[]{:S(2)}) copy-start(bf16[4,128,1024]{2,1,0:T(8,128)(2,1)} %param.18) | copy-start | bytes 3145732
  9.0 28.9 %all-to-all-start = ((f32[32,1,256]{2,1,0:T(1,128)}), f32[32,1,256]{2,1,0:T(1,128)S(1)}, u32[]{:S(2)}, u32[]{:S(2)}) async-start(f32[32,1,256]{2,1,0:T(1,128)} %reshape.327), calls=%async_computation | async-start | bytes 65536 | tf_op jit(solution)/shard_map/all_to_all | solution.py:64
  25.8 108.9 %all-gather.4.cloned.1.call-start = ((), (), s32[]{:S(2)}) async-start(), calls=%async_computation.5 | async-start | bytes 2088960 | tf_op jit(solution)/shard_map/all_gather | solution.py:59
  41.2 9.4 %copy-start.5 = (s32[4]{0:T(128)S(1)}, s32[4]{0:T(128)}, u32[]{:S(2)}) copy-start(s32[4]{0:T(128)} %param.21) | copy-start | bytes 52
  42.3 20.4 %all-to-all-start.1 = ((f32[32,4,4,224]{3,2,1,0:T(4,128)}), f32[32,4,4,224]{3,2,1,0:T(4,128)S(1)}, u32[]{:S(2)}, u32[]{:S(2)}) async-start(f32[32,4,4,224]{3,2,1,0:T(4,128)} %copy.228), calls=%async_computation.1 | async-start | bytes 1048576 | tf_op jit(solution)/shard_map/all_to_all | solution.py:86
  50.6 16.9 %copy-start.3 = (bf16[1,384,1024]{2,1,0:T(8,128)(2,1)S(1)}, bf16[1,384,1024]{2,1,0:T(8,128)(2,1)}, u32[]{:S(2)}) copy-start(bf16[1,384,1024]{2,1,0:T(8,128)(2,1)} %param.16) | copy-start | bytes 2359300
  63.8 16.5 %all-to-all-start.2 = ((f32[16,16,224]{2,1,0:T(8,128)}), f32[16,16,224]{2,1,0:T(8,128)S(1)}, u32[]{:S(2)}, u32[]{:S(2)}) async-start(f32[16,16,224]{2,1,0:T(8,128)} %bitcast.7), calls=%async_computation.2 | async-start | bytes 524288 | tf_op jit(solution)/shard_map/all_to_all | solution.py:91
  119.8 1.2 copy-start.4
  121.0 1.2 copy-start.2
  123.0 3.3 %collective-permute-start = (f32[4,4,22,128]{3,1,0,2:T(4,128)S(1)}, f32[4,4,22,128]{3,1,0,2:T(4,128)S(1)}, u32[]{:S(2)}, u32[]{:S(2)}) collective-permute-start(f32[4,4,22,128]{3,1,0,2:T(4,128)S(1)} %copy.253), channel_id=1, source_target_pairs={{0,16},{16,0},{1,17},{17,1},{2,18},{18,2},{3,19},{19,3},{4,20},{20... | collective-permute-start | bytes 540680 | tf_op jit(solution)/shard_map/ppermute | solution.py:199
  127.5 18.7 %all-to-all-start.3 = ((f32[16,22,128]{2,1,0:T(8,128)}), f32[16,22,128]{2,1,0:T(8,128)S(1)}, u32[]{:S(2)}, u32[]{:S(2)}) async-start(f32[16,22,128]{2,1,0:T(8,128)} %copy.256), calls=%async_computation.3 | async-start | bytes 393216 | tf_op jit(solution)/shard_map/all_to_all | solution.py:224
  146.3 29.8 %copy-start.1 = (bf16[5120,160]{0,1:T(8,128)(2,1)S(1)}, bf16[5120,160]{0,1:T(8,128)(2,1)}, u32[]{:S(2)}) copy-start(bf16[5120,160]{0,1:T(8,128)(2,1)} %reshape.322) | copy-start | bytes 4915204
  148.1 27.8 %all-to-all-start.4 = ((bf16[32,20,128]{2,1,0:T(8,128)(2,1)}), bf16[32,20,128]{2,1,0:T(8,128)(2,1)S(1)}, u32[]{:S(2)}, u32[]{:S(2)}) async-start(bf16[32,20,128]{2,1,0:T(8,128)(2,1)} %broadcast_in_dim.116), calls=%async_computation.4 | async-start | bytes 393216 | tf_op jit(solution)/shard_map/all_to_all | solution.py:246
Sparse Core Ops, SparseCore 0:
  29.6 59.8 all-gather.3

commit v11 on v7

--- a/solution.py
+++ b/solution.py
@@ -88,8 +88,10 @@
     )
     reduced = reduced + bias[None, :]
     owned_rows = lax.all_to_all(reduced, "tensor", 0, 0, tiled=True)
-    gathered = lax.all_to_all(
-        jnp.broadcast_to(owned_rows[None], (seq_count,) + owned_rows.shape), SEQ, 0, 0, tiled=True
+    gathered = (
+        lax.all_gather(owned_rows, ("core", "z"), axis=0, tiled=False)
+        .reshape((2, seq_count // 2) + owned_rows.shape)
+        .transpose(1, 0, 2, 3)
     )
     combined_output = (
         gathered.reshape(steps, requests, halves, tensor_count, half_width)

time: 199 us -> 209 us (1.050)
  blocking collectives: 13 us -> 60.7 us
  waiting for transfers between devices: 85.9 us -> 54.7 us
  starting transfers between devices: 55.2 us -> 49.3 us
    all_gather x0 -> x1, blocking collectives: none -> 60.7 us  [body(): lax.all_gather(owned_rows, ('core', 'z'), axis=0, tiled=False)]
    all_to_all x1, waiting for transfers between devices: 29.3 us -> 3.98 us  [body(): owned_rows = lax.all_to_all(reduced, 'tensor', 0, 0, tiled=True)]
    all_to_all x1 -> x0, blocking collectives: 13 us -> none  [body(): owned_rows = lax.all_to_all(reduced, 'tensor', 0, 0, tiled=True)]
    all_gather x1, waiting for transfers between devices: 10.9 us -> 0.01 us  [body(): w_out_cols = lax.all_gather(w_out, 'tensor', axis=0, tiled=True)]
    all_to_all x1, waiting for transfers between devices: 0.01 us -> 6.52 us  [body(): arrived = lax.all_to_all(pair_packed, 'z', 0, 0, tiled=True)]
    all_to_all x1, starting transfers between devices: 12.1 us -> 6.76 us  [body(): owned_rows = lax.all_to_all(reduced, 'tensor', 0, 0, tiled=True)]
    all_to_all x1, starting transfers between devices: 13.8 us -> 9.44 us  [body(): lax.all_to_all(jnp.broadcast_to(attention_slice[None], (seq_count,) + att...]
    all_to_all x1, starting transfers between devices: 3.53 us -> 7.65 us  [body(): arrived = lax.all_to_all(pair_packed, 'z', 0, 0, tiled=True)]
  transfers between devices with their start and end apart: 8 -> 8, of which waited for: 7 -> 7; matrix products, arithmetic and copies ran while one was open for 9% -> 11% of each run, Pallas kernels for 0% -> 0%
where the time goes in v11:
time: 209 us; the launch traced here: 208 us
  blocking collectives  60.7 us (29%)
  waiting for transfers between devices  54.7 us (26%)
  starting transfers between devices  49.3 us (24%)
  between operations  15.2 us (7%)
  local copies, waits for them, and re-layouts  14.3 us (7%)
  other arithmetic  7.77 us (4%)
  matrix products  6.08 us (3%)
    all_gather x1, blocking collectives, body(): lax.all_gather(owned_rows, ('core', 'z'), axis=0, tiled=False)  60.7 us
    all_to_all x1, waiting for transfers between devices, body(): lax.all_to_all(jnp.broadcast_to(attention_slice[None], (seq_count,) + att...  17.2 us
    all_to_all x1, starting transfers between devices, body(): lax.all_to_all(jnp.broadcast_to(local_squares[None], (seq_count,) + local...  16.7 us
    all_to_all x1, waiting for transfers between devices, body(): reduced = jnp.sum(lax.all_to_all(chunks, 'z', 0, 0, tiled=True), axis=0)  14.1 us
    all_to_all x1, waiting for transfers between devices, body(): lax.all_to_all(jnp.broadcast_to(local_squares[None], (seq_count,) + local...  10.7 us
    all_to_all x1, starting transfers between devices, body(): lax.all_to_all(jnp.broadcast_to(attention_slice[None], (seq_count,) + att...  9.44 us
    all_to_all x1, starting transfers between devices, body(): arrived = lax.all_to_all(pair_packed, 'z', 0, 0, tiled=True)  7.65 us
    all_to_all x1, starting transfers between devices, body(): owned_rows = lax.all_to_all(reduced, 'tensor', 0, 0, tiled=True)  6.76 us
  transfers between devices with their start and end apart: 8, of which 7 were waited for; matrix products, arithmetic and copies ran while one was open for 11% of the time, Pallas kernels for 0%

profile of v11, /device:TPU:1, one launch (start us, length us, event | category | flops | bytes accessed | tf_op | source)
XLA Modules:
  0.0 208.1 jit_solution(5835194069553013088)
XLA Ops:
  7.2 1.1 fusion.20
  8.3 0.7 reshape.350
  9.0 16.7 %all-to-all-start = ((f32[32,1,256]{2,1,0:T(1,128)}), f32[32,1,256]{2,1,0:T(1,128)S(1)}, u32[]{:S(2)}, u32[]{:S(2)}) async-start(f32[32,1,256]{2,1,0:T(1,128)} %reshape.350), calls=%async_computation | async-start | bytes 65536 | tf_op jit(solution)/shard_map/all_to_all | solution.py:64
  25.8 0.7 all-gather.4.cloned.1.call-update
  26.5 0.7 convert_element_type.53
  27.2 10.7 %all-to-all-done = f32[32,1,256]{2,1,0:T(1,128)S(1)} async-done(((f32[32,1,256]{2,1,0:T(1,128)}), f32[32,1,256]{2,1,0:T(1,128)S(1)}, u32[]{:S(2)}, u32[]{:S(2)}) %all-to-all-start) | async-done | bytes 32800 | tf_op jit(solution)/shard_map/all_to_all | solution.py:64
  37.9 0.5 broadcast.183
  38.4 0.7 reduce.1
  39.3 1.2 fusion.28
  40.6 0.4 reshape.329
  41.0 0.5 constant_dynamic-slice_fusion.3
  41.6 3.2 %collective-permute-start = (f32[4,16,4,224]{3,1,2,0:T(8,128)S(1)}, f32[4,16,4,224]{3,1,2,0:T(8,128)S(1)}, u32[]{:S(2)}, u32[]{:S(2)}) collective-permute-start(f32[4,16,4,224]{3,1,2,0:T(8,128)S(1)} %bitcast.164), channel_id=1, source_target_pairs={{0,16},{16,0},{1,17},{17,1},{2,18},{18,2},{3,19},{19,3},{4,20},{20... | collective-permute-start | bytes 688136 | tf_op jit(solution)/shard_map/ppermute | solution.py:83
  45.5 0.4 collective-permute-done
  45.9 0.8 bitcast_add_fusion
  46.7 3.5 %all-to-all-start.1 = ((f32[16,16,224]{2,1,0:T(8,128)}), f32[16,16,224]{2,1,0:T(8,128)S(1)}, u32[]{:S(2)}, u32[]{:S(2)}) async-start(f32[16,16,224]{2,1,0:T(8,128)} %bitcast.6), calls=%async_computation.1 | async-start | bytes 524288 | tf_op jit(solution)/shard_map/all_to_all | solution.py:85
  50.5 14.1 %all-to-all-done.1 = f32[16,16,224]{2,1,0:T(8,128)S(1)} async-done(((f32[16,16,224]{2,1,0:T(8,128)}), f32[16,16,224]{2,1,0:T(8,128)S(1)}, u32[]{:S(2)}, u32[]{:S(2)}) %all-to-all-start.1) | async-done | bytes 229408 | tf_op jit(solution)/shard_map/all_to_all | solution.py:85
  64.6 0.6 reshape_add_fusion
  65.2 6.8 %all-to-all-start.2 = ((f32[16,1,224]{2,1,0:T(1,128)}), f32[16,1,224]{2,1,0:T(1,128)S(1)}, u32[]{:S(2)}, u32[]{:S(2)}) async-start(f32[16,1,224]{2,1,0:T(1,128)} %reshape_add_fusion), calls=%async_computation.2 | async-start | bytes 32768 | tf_op jit(solution)/shard_map/all_to_all | solution.py:90
  72.2 2.2 %copy.297 = bf16[48,8,8,128]{3,2,1,0:T(8,128)(2,1)} copy(bf16[48,8,8,128]{3,1,2,0:T(8,128)(2,1)} %bitcast.158) | data formatting | bytes 1572864
  74.4 4.0 %all-to-all-done.2 = f32[16,1,224]{2,1,0:T(1,128)S(1)} async-done(((f32[16,1,224]{2,1,0:T(1,128)}), f32[16,1,224]{2,1,0:T(1,128)S(1)}, u32[]{:S(2)}, u32[]{:S(2)}) %all-to-all-start.2) | async-done | bytes 14368 | tf_op jit(solution)/shard_map/all_to_all | solution.py:90
  78.4 60.7 %all-gather = f32[512,1,224]{2,0,1:T(8,128)S(1)} all-gather(f32[16,1,224]{2,0,1:T(8,128)S(1)} %copy.237), channel_id=2, replica_groups=mesh['z'=16,'core'=2,'tensor'=16] {'core','z'}, dimensions={0}, use_global_device_ids=true | all-gather | bytes 473088 | tf_op jit(solution)/shard_map/all_gather | solution.py:92
  139.1 0.4 copy.239
  139.5 0.8 reshape.333
  140.3 0.3 subtract_convert_fusion
  140.9 0.7 fusion.68
  141.6 0.7 fusion.69
  142.4 0.4 fusion.10
  142.8 0.5 convolution_bitcast_fusion
  143.3 0.3 fusion.18
  143.7 0.4 copy-done.2
  144.0 0.4 convolution_add_fusion
  144.8 2.0 collective-permute-start.1
  146.9 1.2 collective-permute-done.1
  148.3 0.2 fusion.27
  148.6 0.7 copy.265
  149.3 7.6 %all-to-all-start.3 = ((f32[16,22,128]{2,1,0:T(8,128)}), f32[16,22,128]{2,1,0:T(8,128)S(1)}, u32[]{:S(2)}, u32[]{:S(2)}) async-start(f32[16,22,128]{2,1,0:T(8,128)} %copy.265), calls=%async_computation.3 | async-start | bytes 393216 | tf_op jit(solution)/shard_map/all_to_all | solution.py:227
  157.1 0.3 fusion.67
  157.5 1.1 fusion.35
  158.6 2.2 %copy.233 = bf16[16,320,160]{1,0,2:T(8,128)(2,1)S(1)} copy(bf16[16,320,160]{1,2,0:T(8,128)(2,1)} %all-gather.4.cloned.1.call-done) | data formatting | bytes 3276800 | tf_op jit(solution)/shard_map/all_gather | solution.py:59
  160.8 2.5 %reshape.345 = bf16[5120,160]{0,1:T(8,128)(2,1)} reshape(bf16[16,320,160]{1,0,2:T(8,128)(2,1)S(1)} %copy.233) | data formatting | bytes 3276800 | tf_op jit(solution)/shard_map/optimization_barrier | solution.py:228
  163.4 6.5 %all-to-all-done.3 = f32[16,22,128]{2,1,0:T(8,128)S(1)} async-done(((f32[16,22,128]{2,1,0:T(8,128)}), f32[16,22,128]{2,1,0:T(8,128)S(1)}, u32[]{:S(2)}, u32[]{:S(2)}) %all-to-all-start.3) | async-done | bytes 180256 | tf_op jit(solution)/shard_map/all_to_all | solution.py:227
  170.1 0.9 fusion.46
  171.0 0.7 broadcast_in_dim.111
  171.7 9.4 %all-to-all-start.4 = ((bf16[32,20,128]{2,1,0:T(8,128)(2,1)}), bf16[32,20,128]{2,1,0:T(8,128)(2,1)S(1)}, u32[]{:S(2)}, u32[]{:S(2)}) async-start(bf16[32,20,128]{2,1,0:T(8,128)(2,1)} %broadcast_in_dim.111), calls=%async_computation.4 | async-start | bytes 393216 | tf_op jit(solution)/shard_map/all_to_all | solution.py:249
  181.2 0.7 copy.273
  181.9 0.7 fusion.47
  182.6 17.2 %all-to-all-done.4 = bf16[32,20,128]{2,1,0:T(8,128)(2,1)S(1)} async-done(((bf16[32,20,128]{2,1,0:T(8,128)(2,1)}), bf16[32,20,128]{2,1,0:T(8,128)(2,1)S(1)}, u32[]{:S(2)}, u32[]{:S(2)}) %all-to-all-start.4) | async-done | bytes 163872 | tf_op jit(solution)/shard_map/all_to_all | solution.py:249
  200.1 1.2 fusion
  (70 shorter events, 2.6 us)
Async XLA Ops:
  7.2 134.4 %copy-start = (bf16[4,128,1024]{2,1,0:T(8,128)(2,1)S(1)}, bf16[4,128,1024]{2,1,0:T(8,128)(2,1)}, u32[]{:S(2)}) copy-start(bf16[4,128,1024]{2,1,0:T(8,128)(2,1)} %param.18) | copy-start | bytes 3145732
  9.0 28.9 %all-to-all-start = ((f32[32,1,256]{2,1,0:T(1,128)}), f32[32,1,256]{2,1,0:T(1,128)S(1)}, u32[]{:S(2)}, u32[]{:S(2)}) async-start(f32[32,1,256]{2,1,0:T(1,128)} %reshape.350), calls=%async_computation | async-start | bytes 65536 | tf_op jit(solution)/shard_map/all_to_all | solution.py:64
  25.8 132.8 %all-gather.4.cloned.1.call-start = ((), (), s32[]{:S(2)}) async-start(), calls=%async_computation.5 | async-start | bytes 2088960 | tf_op jit(solution)/shard_map/all_gather | solution.py:59
  40.5 4.9 %copy-start.5 = (bf16[448]{0:T(512)(128)(2,1)S(1)}, bf16[448]{0:T(512)(128)(2,1)}, u32[]{:S(2)}) copy-start(bf16[448]{0:T(512)(128)(2,1)} %param.14) | copy-start | bytes 2692
  41.5 8.7 %copy-start.6 = (s32[4]{0:T(128)S(1)}, s32[4]{0:T(128)}, u32[]{:S(2)}) copy-start(s32[4]{0:T(128)} %param.21) | copy-start | bytes 52
  41.5 30.5 %copy-start.3 = (bf16[1,384,1024]{2,1,0:T(8,128)(2,1)S(1)}, bf16[1,384,1024]{2,1,0:T(8,128)(2,1)}, u32[]{:S(2)}) copy-start(bf16[1,384,1024]{2,1,0:T(8,128)(2,1)} %param.16) | copy-start | bytes 2359300
  41.6 4.3 %collective-permute-start = (f32[4,16,4,224]{3,1,2,0:T(8,128)S(1)}, f32[4,16,4,224]{3,1,2,0:T(8,128)S(1)}, u32[]{:S(2)}, u32[]{:S(2)}) collective-permute-start(f32[4,16,4,224]{3,1,2,0:T(8,128)S(1)} %bitcast.164), channel_id=1, source_target_pairs={{0,16},{16,0},{1,17},{17,1},{2,18},{18,2},{3,19},{19,3},{4,20},{20... | collective-permute-start | bytes 688136 | tf_op jit(solution)/shard_map/ppermute | solution.py:83
  46.7 17.9 %all-to-all-start.1 = ((f32[16,16,224]{2,1,0:T(8,128)}), f32[16,16,224]{2,1,0:T(8,128)S(1)}, u32[]{:S(2)}, u32[]{:S(2)}) async-start(f32[16,16,224]{2,1,0:T(8,128)} %bitcast.6), calls=%async_computation.1 | async-start | bytes 524288 | tf_op jit(solution)/shard_map/all_to_all | solution.py:85
  65.2 13.2 %all-to-all-start.2 = ((f32[16,1,224]{2,1,0:T(1,128)}), f32[16,1,224]{2,1,0:T(1,128)S(1)}, u32[]{:S(2)}, u32[]{:S(2)}) async-start(f32[16,1,224]{2,1,0:T(1,128)} %reshape_add_fusion), calls=%async_computation.2 | async-start | bytes 32768 | tf_op jit(solution)/shard_map/all_to_all | solution.py:90
  141.6 1.2 copy-start.4
  142.8 1.2 copy-start.2
  144.8 3.3 %collective-permute-start.1 = (f32[4,4,22,128]{3,1,0,2:T(4,128)S(1)}, f32[4,4,22,128]{3,1,0,2:T(4,128)S(1)}, u32[]{:S(2)}, u32[]{:S(2)}) collective-permute-start(f32[4,4,22,128]{3,1,0,2:T(4,128)S(1)} %copy.262), channel_id=1, source_target_pairs={{0,16},{16,0},{1,17},{17,1},{2,18},{18,2},{3,19},{19,3},{4,20},{20... | collective-permute-start | bytes 540680 | tf_op jit(solution)/shard_map/ppermute | solution.py:202
  149.3 20.6 %all-to-all-start.3 = ((f32[16,22,128]{2,1,0:T(8,128)}), f32[16,22,128]{2,1,0:T(8,128)S(1)}, u32[]{:S(2)}, u32[]{:S(2)}) async-start(f32[16,22,128]{2,1,0:T(8,128)} %copy.265), calls=%async_computation.3 | async-start | bytes 393216 | tf_op jit(solution)/shard_map/all_to_all | solution.py:227
  170.0 30.1 %copy-start.1 = (bf16[5120,160]{0,1:T(8,128)(2,1)S(1)}, bf16[5120,160]{0,1:T(8,128)(2,1)}, u32[]{:S(2)}) copy-start(bf16[5120,160]{0,1:T(8,128)(2,1)} %reshape.345) | copy-start | bytes 4915204
  171.7 28.1 %all-to-all-start.4 = ((bf16[32,20,128]{2,1,0:T(8,128)(2,1)}), bf16[32,20,128]{2,1,0:T(8,128)(2,1)S(1)}, u32[]{:S(2)}, u32[]{:S(2)}) async-start(bf16[32,20,128]{2,1,0:T(8,128)(2,1)} %broadcast_in_dim.111), calls=%async_computation.4 | async-start | bytes 393216 | tf_op jit(solution)/shard_map/all_to_all | solution.py:249
Sparse Core Ops, SparseCore 0:
  29.6 59.8 all-gather.3

commit v12 on v6

--- a/solution.py
+++ b/solution.py
@@ -88,7 +88,7 @@
     )
     reduced = reduced + bias[None, :]
     owned_rows = lax.all_to_all(reduced, "tensor", 0, 0, tiled=True)
-    gathered = lax.all_gather(owned_rows, SEQ, axis=0, tiled=False)
+    gathered = lax.all_gather(owned_rows.reshape(1, -1), SEQ, axis=0, tiled=True)
     combined_output = (
         gathered.reshape(steps, requests, halves, tensor_count, half_width)
         .transpose(0, 1, 3, 2, 4)

time: 183 us -> 184 us (level)
    unnamed x21 -> x22, local copies, waits for them, and re-layouts: 4.5 us -> 4.59 us
  transfers between devices with their start and end apart: 8 -> 8, of which waited for: 7 -> 7; matrix products, arithmetic and copies ran while one was open for 12% -> 13% of each run, Pallas kernels for 0% -> 0%
where the time goes in v12:
time: 184 us
  waiting for transfers between devices  54.9 us (30%)
  starting transfers between devices  45.7 us (25%)
  blocking collectives  38.1 us (21%)
  between operations  15.2 us (8%)
  local copies, waits for them, and re-layouts  14.7 us (8%)
  other arithmetic  8.9 us (5%)
  matrix products  6.08 us (3%)
    all_gather x1, blocking collectives, body(): lax.all_gather(owned_rows.reshape(1, -1), SEQ, axis=0, tiled=True)  38.1 us
    all_to_all x1, waiting for transfers between devices, body(): lax.all_to_all(jnp.broadcast_to(attention_slice[None], (seq_count,) + att...  17.2 us
    all_to_all x1, starting transfers between devices, body(): lax.all_to_all(jnp.broadcast_to(local_squares[None], (seq_count,) + local...  16.7 us
    all_to_all x1, waiting for transfers between devices, body(): reduced = jnp.sum(lax.all_to_all(chunks, 'z', 0, 0, tiled=True), axis=0)  14.1 us
    all_to_all x1, waiting for transfers between devices, body(): lax.all_to_all(jnp.broadcast_to(local_squares[None], (seq_count,) + local...  10.7 us
    all_to_all x1, starting transfers between devices, body(): lax.all_to_all(jnp.broadcast_to(attention_slice[None], (seq_count,) + att...  9.16 us
    all_to_all x1, waiting for transfers between devices, body(): arrived = lax.all_to_all(pair_packed, 'z', 0, 0, tiled=True)  6.79 us
    all_to_all x1, starting transfers between devices, body(): owned_rows = lax.all_to_all(reduced, 'tensor', 0, 0, tiled=True)  6.76 us
  transfers between devices with their start and end apart: 8, of which 7 were waited for; matrix products, arithmetic and copies ran while one was open for 13% of the time, Pallas kernels for 0%

profile of v12, /device:TPU:1, one launch (start us, length us, event | category | flops | bytes accessed | tf_op | source)
XLA Modules:
  0.0 183.6 jit_solution(14849080154780183464)
XLA Ops:
  7.2 1.1 fusion.20
  8.3 0.7 reshape.354
  9.0 16.7 %all-to-all-start = ((f32[32,1,256]{2,1,0:T(1,128)}), f32[32,1,256]{2,1,0:T(1,128)S(1)}, u32[]{:S(2)}, u32[]{:S(2)}) async-start(f32[32,1,256]{2,1,0:T(1,128)} %reshape.354), calls=%async_computation | async-start | bytes 65536 | tf_op jit(solution)/shard_map/all_to_all | solution.py:64
  25.8 0.7 all-gather.4.cloned.1.call-update
  26.5 0.7 convert_element_type.53
  27.2 10.7 %all-to-all-done = f32[32,1,256]{2,1,0:T(1,128)S(1)} async-done(((f32[32,1,256]{2,1,0:T(1,128)}), f32[32,1,256]{2,1,0:T(1,128)S(1)}, u32[]{:S(2)}, u32[]{:S(2)}) %all-to-all-start) | async-done | bytes 32800 | tf_op jit(solution)/shard_map/all_to_all | solution.py:64
  37.9 0.5 broadcast.185
  38.4 0.7 reduce.3
  39.3 1.2 fusion.28
  40.6 0.4 reshape.329
  41.0 0.5 constant_dynamic-slice_fusion.3
  41.6 3.2 %collective-permute-start = (f32[4,16,4,224]{3,1,2,0:T(8,128)S(1)}, f32[4,16,4,224]{3,1,2,0:T(8,128)S(1)}, u32[]{:S(2)}, u32[]{:S(2)}) collective-permute-start(f32[4,16,4,224]{3,1,2,0:T(8,128)S(1)} %bitcast.158), channel_id=1, source_target_pairs={{0,16},{16,0},{1,17},{17,1},{2,18},{18,2},{3,19},{19,3},{4,20},{20... | collective-permute-start | bytes 688136 | tf_op jit(solution)/shard_map/ppermute | solution.py:83
  45.5 0.4 collective-permute-done
  45.9 0.8 bitcast_add_fusion
  46.7 3.5 %all-to-all-start.1 = ((f32[16,16,224]{2,1,0:T(8,128)}), f32[16,16,224]{2,1,0:T(8,128)S(1)}, u32[]{:S(2)}, u32[]{:S(2)}) async-start(f32[16,16,224]{2,1,0:T(8,128)} %bitcast.6), calls=%async_computation.1 | async-start | bytes 524288 | tf_op jit(solution)/shard_map/all_to_all | solution.py:85
  50.5 14.1 %all-to-all-done.1 = f32[16,16,224]{2,1,0:T(8,128)S(1)} async-done(((f32[16,16,224]{2,1,0:T(8,128)}), f32[16,16,224]{2,1,0:T(8,128)S(1)}, u32[]{:S(2)}, u32[]{:S(2)}) %all-to-all-start.1) | async-done | bytes 229408 | tf_op jit(solution)/shard_map/all_to_all | solution.py:85
  64.6 0.6 reshape_add_fusion
  65.2 6.8 %all-to-all-start.2 = ((f32[16,1,224]{2,1,0:T(1,128)}), f32[16,1,224]{2,1,0:T(1,128)S(1)}, u32[]{:S(2)}, u32[]{:S(2)}) async-start(f32[16,1,224]{2,1,0:T(1,128)} %reshape_add_fusion), calls=%async_computation.2 | async-start | bytes 32768 | tf_op jit(solution)/shard_map/all_to_all | solution.py:90
  72.2 2.2 %copy.286 = bf16[48,8,8,128]{3,2,1,0:T(8,128)(2,1)} copy(bf16[48,8,8,128]{3,1,2,0:T(8,128)(2,1)} %bitcast.152) | data formatting | bytes 1572864
  74.4 4.0 %all-to-all-done.2 = f32[16,1,224]{2,1,0:T(1,128)S(1)} async-done(((f32[16,1,224]{2,1,0:T(1,128)}), f32[16,1,224]{2,1,0:T(1,128)S(1)}, u32[]{:S(2)}, u32[]{:S(2)}) %all-to-all-start.2) | async-done | bytes 14368 | tf_op jit(solution)/shard_map/all_to_all | solution.py:90
  78.6 38.1 %all-gather.1 = f32[32,1,3584]{2,1,0:T(1,128)S(1)} all-gather(f32[1,1,3584]{2,1,0:T(1,128)S(1)} %reshape.344), channel_id=1, replica_groups=mesh['z'=16,'core'=2,'tensor'=16] {'z','core'}, dimensions={0}, use_global_device_ids=true | all-gather | bytes 473088 | tf_op jit(solution)/shard_map/all_gather | solution.py:91
  116.6 1.1 reduce.2
  117.7 0.3 reshape.332
  118.1 0.4 copy.229
  118.5 0.8 reshape.333
  119.9 0.7 fusion.68
  120.6 0.7 fusion.69
  121.3 0.4 fusion.10
  121.8 0.5 convolution_bitcast_fusion
  122.3 0.3 fusion.18
  122.6 0.4 copy-done.2
  123.0 0.4 convolution_add_fusion
  123.7 2.1 %collective-permute-start.1 = (f32[4,4,22,128]{3,1,0,2:T(4,128)S(1)}, f32[4,4,22,128]{3,1,0,2:T(4,128)S(1)}, u32[]{:S(2)}, u32[]{:S(2)}) collective-permute-start(f32[4,4,22,128]{3,1,0,2:T(4,128)S(1)} %copy.252), channel_id=1, source_target_pairs={{0,16},{16,0},{1,17},{17,1},{2,18},{18,2},{3,19},{19,3},{4,20},{20... | collective-permute-start | bytes 540680 | tf_op jit(solution)/shard_map/ppermute | solution.py:198
  126.0 1.1 collective-permute-done.1
  127.6 0.7 copy.255
  128.3 4.2 %all-to-all-start.3 = ((f32[16,22,128]{2,1,0:T(8,128)}), f32[16,22,128]{2,1,0:T(8,128)S(1)}, u32[]{:S(2)}, u32[]{:S(2)}) async-start(f32[16,22,128]{2,1,0:T(8,128)} %copy.255), calls=%async_computation.3 | async-start | bytes 393216 | tf_op jit(solution)/shard_map/all_to_all | solution.py:223
  132.7 0.3 fusion.67
  133.1 1.1 fusion.35
  134.2 2.2 %copy.225 = bf16[16,320,160]{1,0,2:T(8,128)(2,1)S(1)} copy(bf16[16,320,160]{1,2,0:T(8,128)(2,1)} %all-gather.4.cloned.1.call-done) | data formatting | bytes 3276800 | tf_op jit(solution)/shard_map/all_gather | solution.py:59
  136.4 2.5 %reshape.343 = bf16[5120,160]{0,1:T(8,128)(2,1)} reshape(bf16[16,320,160]{1,0,2:T(8,128)(2,1)S(1)} %copy.225) | data formatting | bytes 3276800 | tf_op jit(solution)/shard_map/optimization_barrier | solution.py:224
  138.9 6.8 %all-to-all-done.3 = f32[16,22,128]{2,1,0:T(8,128)S(1)} async-done(((f32[16,22,128]{2,1,0:T(8,128)}), f32[16,22,128]{2,1,0:T(8,128)S(1)}, u32[]{:S(2)}, u32[]{:S(2)}) %all-to-all-start.3) | async-done | bytes 180256 | tf_op jit(solution)/shard_map/all_to_all | solution.py:223
  146.0 0.9 fusion.46
  146.9 0.7 broadcast_in_dim.111
  147.6 9.2 %all-to-all-start.4 = ((bf16[32,20,128]{2,1,0:T(8,128)(2,1)}), bf16[32,20,128]{2,1,0:T(8,128)(2,1)S(1)}, u32[]{:S(2)}, u32[]{:S(2)}) async-start(bf16[32,20,128]{2,1,0:T(8,128)(2,1)} %broadcast_in_dim.111), calls=%async_computation.4 | async-start | bytes 393216 | tf_op jit(solution)/shard_map/all_to_all | solution.py:245
  156.8 0.7 copy.263
  157.4 0.7 fusion.47
  158.2 17.2 %all-to-all-done.4 = bf16[32,20,128]{2,1,0:T(8,128)(2,1)S(1)} async-done(((bf16[32,20,128]{2,1,0:T(8,128)(2,1)}), bf16[32,20,128]{2,1,0:T(8,128)(2,1)S(1)}, u32[]{:S(2)}, u32[]{:S(2)}) %all-to-all-start.4) | async-done | bytes 163872 | tf_op jit(solution)/shard_map/all_to_all | solution.py:245
  175.6 1.2 fusion
  (73 shorter events, 3.2 us)
Async XLA Ops:
  7.2 113.4 %copy-start = (bf16[4,128,1024]{2,1,0:T(8,128)(2,1)S(1)}, bf16[4,128,1024]{2,1,0:T(8,128)(2,1)}, u32[]{:S(2)}) copy-start(bf16[4,128,1024]{2,1,0:T(8,128)(2,1)} %param.18) | copy-start | bytes 3145732
  9.0 28.9 %all-to-all-start = ((f32[32,1,256]{2,1,0:T(1,128)}), f32[32,1,256]{2,1,0:T(1,128)S(1)}, u32[]{:S(2)}, u32[]{:S(2)}) async-start(f32[32,1,256]{2,1,0:T(1,128)} %reshape.354), calls=%async_computation | async-start | bytes 65536 | tf_op jit(solution)/shard_map/all_to_all | solution.py:64
  25.8 108.4 %all-gather.4.cloned.1.call-start = ((), (), s32[]{:S(2)}) async-start(), calls=%async_computation.5 | async-start | bytes 2088960 | tf_op jit(solution)/shard_map/all_gather | solution.py:59
  40.5 4.9 %copy-start.5 = (bf16[448]{0:T(512)(128)(2,1)S(1)}, bf16[448]{0:T(512)(128)(2,1)}, u32[]{:S(2)}) copy-start(bf16[448]{0:T(512)(128)(2,1)} %param.14) | copy-start | bytes 2692
  41.5 8.7 %copy-start.6 = (s32[4]{0:T(128)S(1)}, s32[4]{0:T(128)}, u32[]{:S(2)}) copy-start(s32[4]{0:T(128)} %param.21) | copy-start | bytes 52
  41.5 30.5 %copy-start.3 = (bf16[1,384,1024]{2,1,0:T(8,128)(2,1)S(1)}, bf16[1,384,1024]{2,1,0:T(8,128)(2,1)}, u32[]{:S(2)}) copy-start(bf16[1,384,1024]{2,1,0:T(8,128)(2,1)} %param.16) | copy-start | bytes 2359300
  41.6 4.3 %collective-permute-start = (f32[4,16,4,224]{3,1,2,0:T(8,128)S(1)}, f32[4,16,4,224]{3,1,2,0:T(8,128)S(1)}, u32[]{:S(2)}, u32[]{:S(2)}) collective-permute-start(f32[4,16,4,224]{3,1,2,0:T(8,128)S(1)} %bitcast.158), channel_id=1, source_target_pairs={{0,16},{16,0},{1,17},{17,1},{2,18},{18,2},{3,19},{19,3},{4,20},{20... | collective-permute-start | bytes 688136 | tf_op jit(solution)/shard_map/ppermute | solution.py:83
  46.7 17.9 %all-to-all-start.1 = ((f32[16,16,224]{2,1,0:T(8,128)}), f32[16,16,224]{2,1,0:T(8,128)S(1)}, u32[]{:S(2)}, u32[]{:S(2)}) async-start(f32[16,16,224]{2,1,0:T(8,128)} %bitcast.6), calls=%async_computation.1 | async-start | bytes 524288 | tf_op jit(solution)/shard_map/all_to_all | solution.py:85
  65.2 13.2 %all-to-all-start.2 = ((f32[16,1,224]{2,1,0:T(1,128)}), f32[16,1,224]{2,1,0:T(1,128)S(1)}, u32[]{:S(2)}, u32[]{:S(2)}) async-start(f32[16,1,224]{2,1,0:T(1,128)} %reshape_add_fusion), calls=%async_computation.2 | async-start | bytes 32768 | tf_op jit(solution)/shard_map/all_to_all | solution.py:90
  120.5 1.2 copy-start.4
  121.8 1.2 copy-start.2
  123.7 3.3 %collective-permute-start.1 = (f32[4,4,22,128]{3,1,0,2:T(4,128)S(1)}, f32[4,4,22,128]{3,1,0,2:T(4,128)S(1)}, u32[]{:S(2)}, u32[]{:S(2)}) collective-permute-start(f32[4,4,22,128]{3,1,0,2:T(4,128)S(1)} %copy.252), channel_id=1, source_target_pairs={{0,16},{16,0},{1,17},{17,1},{2,18},{18,2},{3,19},{19,3},{4,20},{20... | collective-permute-start | bytes 540680 | tf_op jit(solution)/shard_map/ppermute | solution.py:198
  128.3 17.4 %all-to-all-start.3 = ((f32[16,22,128]{2,1,0:T(8,128)}), f32[16,22,128]{2,1,0:T(8,128)S(1)}, u32[]{:S(2)}, u32[]{:S(2)}) async-start(f32[16,22,128]{2,1,0:T(8,128)} %copy.255), calls=%async_computation.3 | async-start | bytes 393216 | tf_op jit(solution)/shard_map/all_to_all | solution.py:223
  145.8 29.8 %copy-start.1 = (bf16[5120,160]{0,1:T(8,128)(2,1)S(1)}, bf16[5120,160]{0,1:T(8,128)(2,1)}, u32[]{:S(2)}) copy-start(bf16[5120,160]{0,1:T(8,128)(2,1)} %reshape.343) | copy-start | bytes 4915204
  147.6 27.8 %all-to-all-start.4 = ((bf16[32,20,128]{2,1,0:T(8,128)(2,1)}), bf16[32,20,128]{2,1,0:T(8,128)(2,1)S(1)}, u32[]{:S(2)}, u32[]{:S(2)}) async-start(bf16[32,20,128]{2,1,0:T(8,128)(2,1)} %broadcast_in_dim.111), calls=%async_computation.4 | async-start | bytes 393216 | tf_op jit(solution)/shard_map/all_to_all | solution.py:245
Sparse Core Ops, SparseCore 0:
  29.6 59.8 all-gather.3

commit v13 on v5

--- a/solution.py
+++ b/solution.py
@@ -242,7 +242,10 @@
     summed = global_acc * factor_old[..., None] + own_new_acc * factor_new[..., None]
     attention_slice = (summed / total[..., None]).astype(jnp.bfloat16)
 
-    attention_all = lax.all_gather(attention_slice, SEQ, axis=0, tiled=False)
+    flat_slice = attention_slice.reshape(1, -1)
+    attention_all = lax.all_to_all(
+        jnp.broadcast_to(flat_slice[None], (seq_count,) + flat_slice.shape), SEQ, 0, 0, tiled=True
+    ).reshape((seq_count,) + attention_slice.shape)
     heads_local = (
         attention_all.reshape(requests, KEY_HEADS, steps, query_group_width, HEAD_SIZE)
         .transpose(2, 0, 1, 3, 4)

time: 194 us -> 184 us (0.948)
  blocking collectives: 72.9 us -> 38.2 us
  waiting for transfers between devices: 37.4 us -> 53.4 us
  starting transfers between devices: 36.6 us -> 45.9 us
    all_gather x1 -> x0, blocking collectives: 34.7 us -> none  [body(): attention_all = lax.all_gather(attention_slice, SEQ, axis=0, tiled=False)]
    all_to_all x0 -> x1, waiting for transfers between devices: none -> 15.7 us  [body(): lax.all_to_all(jnp.broadcast_to(flat_slice[None], (seq_count,) + flat_sli...]
    all_to_all x0 -> x1, starting transfers between devices: none -> 9.3 us  [body(): lax.all_to_all(jnp.broadcast_to(flat_slice[None], (seq_count,) + flat_sli...]
    unnamed x51 -> x23, local copies, waits for them, and re-layouts: 4.78 us -> 5.33 us
  transfers between devices with their start and end apart: 7 -> 8, of which waited for: 5 -> 7; matrix products, arithmetic and copies ran while one was open for 15% -> 12% of each run, Pallas kernels for 0% -> 0%
where the time goes in v13:
time: 184 us; the launch traced here: 183 us
  waiting for transfers between devices  53.4 us (29%)
  starting transfers between devices  45.9 us (25%)
  blocking collectives  38.2 us (21%)
  between operations  15.3 us (8%)
  local copies, waits for them, and re-layouts  15.1 us (8%)
  other arithmetic  9.27 us (5%)
  matrix products  6.07 us (3%)
    all_gather x1, blocking collectives, body(): gathered = lax.all_gather(owned_rows, SEQ, axis=0, tiled=False)  38.2 us
    all_to_all x1, starting transfers between devices, body(): lax.all_to_all(jnp.broadcast_to(local_squares[None], (seq_count,) + local...  16.7 us
    all_to_all x1, waiting for transfers between devices, body(): lax.all_to_all(jnp.broadcast_to(flat_slice[None], (seq_count,) + flat_sli...  15.7 us
    all_to_all x1, waiting for transfers between devices, body(): reduced = jnp.sum(lax.all_to_all(chunks, 'z', 0, 0, tiled=True), axis=0)  14.1 us
    all_to_all x1, waiting for transfers between devices, body(): lax.all_to_all(jnp.broadcast_to(local_squares[None], (seq_count,) + local...  10.7 us
    all_to_all x1, starting transfers between devices, body(): lax.all_to_all(jnp.broadcast_to(flat_slice[None], (seq_count,) + flat_sli...  9.3 us
    all_to_all x1, waiting for transfers between devices, body(): arrived = lax.all_to_all(pair_packed, 'z', 0, 0, tiled=True)  6.79 us
    all_to_all x1, starting transfers between devices, body(): owned_rows = lax.all_to_all(reduced, 'tensor', 0, 0, tiled=True)  6.76 us
  transfers between devices with their start and end apart: 8, of which 7 were waited for; matrix products, arithmetic and copies ran while one was open for 12% of the time, Pallas kernels for 0%

profile of v13, /device:TPU:1, one launch (start us, length us, event | category | flops | bytes accessed | tf_op | source)
XLA Modules:
  0.0 183.2 jit_solution(3754792900675968017)
XLA Ops:
  7.2 1.1 fusion.20
  8.3 0.7 reshape.329
  9.0 16.7 %all-to-all-start = ((f32[32,1,256]{2,1,0:T(1,128)}), f32[32,1,256]{2,1,0:T(1,128)S(1)}, u32[]{:S(2)}, u32[]{:S(2)}) async-start(f32[32,1,256]{2,1,0:T(1,128)} %reshape.329), calls=%async_computation | async-start | bytes 65536 | tf_op jit(solution)/shard_map/all_to_all | solution.py:64
  25.8 0.7 all-gather.4.cloned.1.call-update
  26.5 0.7 convert_element_type.53
  27.2 10.7 %all-to-all-done = f32[32,1,256]{2,1,0:T(1,128)S(1)} async-done(((f32[32,1,256]{2,1,0:T(1,128)}), f32[32,1,256]{2,1,0:T(1,128)S(1)}, u32[]{:S(2)}, u32[]{:S(2)}) %all-to-all-start) | async-done | bytes 32800 | tf_op jit(solution)/shard_map/all_to_all | solution.py:64
  37.9 0.5 broadcast.169
  38.4 0.7 reduce.1
  39.3 1.2 fusion.28
  40.6 0.4 reshape.310
  41.0 0.5 constant_dynamic-slice_fusion.3
  41.6 3.2 %collective-permute-start = (f32[4,16,4,224]{3,1,2,0:T(8,128)S(1)}, f32[4,16,4,224]{3,1,2,0:T(8,128)S(1)}, u32[]{:S(2)}, u32[]{:S(2)}) collective-permute-start(f32[4,16,4,224]{3,1,2,0:T(8,128)S(1)} %bitcast.166), channel_id=1, source_target_pairs={{0,16},{16,0},{1,17},{17,1},{2,18},{18,2},{3,19},{19,3},{4,20},{20... | collective-permute-start | bytes 688136 | tf_op jit(solution)/shard_map/ppermute | solution.py:83
  45.5 0.4 collective-permute-done
  45.9 0.8 bitcast_add_fusion
  46.7 3.5 %all-to-all-start.1 = ((f32[16,16,224]{2,1,0:T(8,128)}), f32[16,16,224]{2,1,0:T(8,128)S(1)}, u32[]{:S(2)}, u32[]{:S(2)}) async-start(f32[16,16,224]{2,1,0:T(8,128)} %bitcast.6), calls=%async_computation.1 | async-start | bytes 524288 | tf_op jit(solution)/shard_map/all_to_all | solution.py:85
  50.5 14.1 %all-to-all-done.1 = f32[16,16,224]{2,1,0:T(8,128)S(1)} async-done(((f32[16,16,224]{2,1,0:T(8,128)}), f32[16,16,224]{2,1,0:T(8,128)S(1)}, u32[]{:S(2)}, u32[]{:S(2)}) %all-to-all-start.1) | async-done | bytes 229408 | tf_op jit(solution)/shard_map/all_to_all | solution.py:85
  64.6 0.6 reshape_add_fusion
  65.2 6.8 %all-to-all-start.2 = ((f32[16,1,224]{2,1,0:T(1,128)}), f32[16,1,224]{2,1,0:T(1,128)S(1)}, u32[]{:S(2)}, u32[]{:S(2)}) async-start(f32[16,1,224]{2,1,0:T(1,128)} %reshape_add_fusion), calls=%async_computation.2 | async-start | bytes 32768 | tf_op jit(solution)/shard_map/all_to_all | solution.py:90
  72.2 2.2 %copy.290 = bf16[48,8,8,128]{3,2,1,0:T(8,128)(2,1)} copy(bf16[48,8,8,128]{3,1,2,0:T(8,128)(2,1)} %bitcast.160) | data formatting | bytes 1572864
  74.4 4.0 %all-to-all-done.2 = f32[16,1,224]{2,1,0:T(1,128)S(1)} async-done(((f32[16,1,224]{2,1,0:T(1,128)}), f32[16,1,224]{2,1,0:T(1,128)S(1)}, u32[]{:S(2)}, u32[]{:S(2)}) %all-to-all-start.2) | async-done | bytes 14368 | tf_op jit(solution)/shard_map/all_to_all | solution.py:90
  78.4 38.2 %all-gather = f32[512,1,224]{2,0,1:T(8,128)S(1)} all-gather(f32[16,1,224]{2,0,1:T(8,128)S(1)} %copy.232), channel_id=2, replica_groups=mesh['z'=16,'core'=2,'tensor'=16] {'z','core'}, dimensions={0}, use_global_device_ids=true | all-gather | bytes 473088 | tf_op jit(solution)/shard_map/all_gather | solution.py:91
  116.7 0.4 copy.233
  117.1 0.8 reshape.313
  118.5 0.7 fusion.67
  119.1 0.7 fusion.68
  119.9 0.4 fusion.10
  120.4 0.5 convolution_bitcast_fusion
  120.9 0.3 fusion.18
  121.2 0.4 copy-done.2
  121.6 0.4 convolution_add_fusion
  122.3 2.1 %collective-permute-start.1 = (f32[4,4,22,128]{3,1,0,2:T(4,128)S(1)}, f32[4,4,22,128]{3,1,0,2:T(4,128)S(1)}, u32[]{:S(2)}, u32[]{:S(2)}) collective-permute-start(f32[4,4,22,128]{3,1,0,2:T(4,128)S(1)} %copy.256), channel_id=1, source_target_pairs={{0,16},{16,0},{1,17},{17,1},{2,18},{18,2},{3,19},{19,3},{4,20},{20... | collective-permute-start | bytes 540680 | tf_op jit(solution)/shard_map/ppermute | solution.py:198
  124.5 1.1 collective-permute-done.1
  126.2 0.7 copy.259
  126.9 4.2 %all-to-all-start.3 = ((f32[16,22,128]{2,1,0:T(8,128)}), f32[16,22,128]{2,1,0:T(8,128)S(1)}, u32[]{:S(2)}, u32[]{:S(2)}) async-start(f32[16,22,128]{2,1,0:T(8,128)} %copy.259), calls=%async_computation.3 | async-start | bytes 393216 | tf_op jit(solution)/shard_map/all_to_all | solution.py:223
  131.3 0.3 fusion.66
  131.7 1.1 fusion.35
  132.8 2.2 %copy.228 = bf16[16,320,160]{1,0,2:T(8,128)(2,1)S(1)} copy(bf16[16,320,160]{1,2,0:T(8,128)(2,1)} %all-gather.4.cloned.1.call-done) | data formatting | bytes 3276800 | tf_op jit(solution)/shard_map/all_gather | solution.py:59
  135.0 2.5 %reshape.324 = bf16[5120,160]{0,1:T(8,128)(2,1)} reshape(bf16[16,320,160]{1,0,2:T(8,128)(2,1)S(1)} %copy.228) | data formatting | bytes 3276800 | tf_op jit(solution)/shard_map/optimization_barrier | solution.py:224
  137.5 6.8 %all-to-all-done.3 = f32[16,22,128]{2,1,0:T(8,128)S(1)} async-done(((f32[16,22,128]{2,1,0:T(8,128)}), f32[16,22,128]{2,1,0:T(8,128)S(1)}, u32[]{:S(2)}, u32[]{:S(2)}) %all-to-all-start.3) | async-done | bytes 180256 | tf_op jit(solution)/shard_map/all_to_all | solution.py:223
  144.6 0.8 fusion.44
  145.5 0.5 broadcast.170
  146.1 1.6 reduce.2
  147.7 0.7 reshape.331
  148.4 9.3 %all-to-all-start.4 = ((bf16[32,2,1280]{2,1,0:T(2,128)(2,1)}), bf16[32,2,1280]{2,1,0:T(2,128)(2,1)S(1)}, u32[]{:S(2)}, u32[]{:S(2)}) async-start(bf16[32,2,1280]{2,1,0:T(2,128)(2,1)} %reshape.331), calls=%async_computation.4 | async-start | bytes 327680 | tf_op jit(solution)/shard_map/all_to_all | solution.py:246
  157.7 0.7 copy.267
  158.3 0.7 fusion.46
  159.1 15.7 %all-to-all-done.4 = bf16[32,2,1280]{2,1,0:T(2,128)(2,1)S(1)} async-done(((bf16[32,2,1280]{2,1,0:T(2,128)(2,1)}), bf16[32,2,1280]{2,1,0:T(2,128)(2,1)S(1)}, u32[]{:S(2)}, u32[]{:S(2)}) %all-to-all-start.4) | async-done | bytes 163872 | tf_op jit(solution)/shard_map/all_to_all | solution.py:246
  175.2 1.2 fusion
  (74 shorter events, 3.3 us)
Async XLA Ops:
  7.2 112.0 %copy-start = (bf16[4,128,1024]{2,1,0:T(8,128)(2,1)S(1)}, bf16[4,128,1024]{2,1,0:T(8,128)(2,1)}, u32[]{:S(2)}) copy-start(bf16[4,128,1024]{2,1,0:T(8,128)(2,1)} %param.18) | copy-start | bytes 3145732
  9.0 28.9 %all-to-all-start = ((f32[32,1,256]{2,1,0:T(1,128)}), f32[32,1,256]{2,1,0:T(1,128)S(1)}, u32[]{:S(2)}, u32[]{:S(2)}) async-start(f32[32,1,256]{2,1,0:T(1,128)} %reshape.329), calls=%async_computation | async-start | bytes 65536 | tf_op jit(solution)/shard_map/all_to_all | solution.py:64
  25.8 107.0 %all-gather.4.cloned.1.call-start = ((), (), s32[]{:S(2)}) async-start(), calls=%async_computation.5 | async-start | bytes 2088960 | tf_op jit(solution)/shard_map/all_gather | solution.py:59
  40.5 4.9 %copy-start.5 = (bf16[448]{0:T(512)(128)(2,1)S(1)}, bf16[448]{0:T(512)(128)(2,1)}, u32[]{:S(2)}) copy-start(bf16[448]{0:T(512)(128)(2,1)} %param.14) | copy-start | bytes 2692
  41.5 8.7 %copy-start.6 = (s32[4]{0:T(128)S(1)}, s32[4]{0:T(128)}, u32[]{:S(2)}) copy-start(s32[4]{0:T(128)} %param.21) | copy-start | bytes 52
  41.5 30.5 %copy-start.3 = (bf16[1,384,1024]{2,1,0:T(8,128)(2,1)S(1)}, bf16[1,384,1024]{2,1,0:T(8,128)(2,1)}, u32[]{:S(2)}) copy-start(bf16[1,384,1024]{2,1,0:T(8,128)(2,1)} %param.16) | copy-start | bytes 2359300
  41.6 4.3 %collective-permute-start = (f32[4,16,4,224]{3,1,2,0:T(8,128)S(1)}, f32[4,16,4,224]{3,1,2,0:T(8,128)S(1)}, u32[]{:S(2)}, u32[]{:S(2)}) collective-permute-start(f32[4,16,4,224]{3,1,2,0:T(8,128)S(1)} %bitcast.166), channel_id=1, source_target_pairs={{0,16},{16,0},{1,17},{17,1},{2,18},{18,2},{3,19},{19,3},{4,20},{20... | collective-permute-start | bytes 688136 | tf_op jit(solution)/shard_map/ppermute | solution.py:83
  46.7 17.9 %all-to-all-start.1 = ((f32[16,16,224]{2,1,0:T(8,128)}), f32[16,16,224]{2,1,0:T(8,128)S(1)}, u32[]{:S(2)}, u32[]{:S(2)}) async-start(f32[16,16,224]{2,1,0:T(8,128)} %bitcast.6), calls=%async_computation.1 | async-start | bytes 524288 | tf_op jit(solution)/shard_map/all_to_all | solution.py:85
  65.2 13.2 %all-to-all-start.2 = ((f32[16,1,224]{2,1,0:T(1,128)}), f32[16,1,224]{2,1,0:T(1,128)S(1)}, u32[]{:S(2)}, u32[]{:S(2)}) async-start(f32[16,1,224]{2,1,0:T(1,128)} %reshape_add_fusion), calls=%async_computation.2 | async-start | bytes 32768 | tf_op jit(solution)/shard_map/all_to_all | solution.py:90
  119.1 1.2 copy-start.4
  120.4 1.2 copy-start.2
  122.3 3.3 %collective-permute-start.1 = (f32[4,4,22,128]{3,1,0,2:T(4,128)S(1)}, f32[4,4,22,128]{3,1,0,2:T(4,128)S(1)}, u32[]{:S(2)}, u32[]{:S(2)}) collective-permute-start(f32[4,4,22,128]{3,1,0,2:T(4,128)S(1)} %copy.256), channel_id=1, source_target_pairs={{0,16},{16,0},{1,17},{17,1},{2,18},{18,2},{3,19},{19,3},{4,20},{20... | collective-permute-start | bytes 540680 | tf_op jit(solution)/shard_map/ppermute | solution.py:198
  126.9 17.4 %all-to-all-start.3 = ((f32[16,22,128]{2,1,0:T(8,128)}), f32[16,22,128]{2,1,0:T(8,128)S(1)}, u32[]{:S(2)}, u32[]{:S(2)}) async-start(f32[16,22,128]{2,1,0:T(8,128)} %copy.259), calls=%async_computation.3 | async-start | bytes 393216 | tf_op jit(solution)/shard_map/all_to_all | solution.py:223
  148.4 26.8 %copy-start.1 = (bf16[5120,160]{0,1:T(8,128)(2,1)S(1)}, bf16[5120,160]{0,1:T(8,128)(2,1)}, u32[]{:S(2)}) copy-start(bf16[5120,160]{0,1:T(8,128)(2,1)} %reshape.324) | copy-start | bytes 4915204
  148.4 26.4 %all-to-all-start.4 = ((bf16[32,2,1280]{2,1,0:T(2,128)(2,1)}), bf16[32,2,1280]{2,1,0:T(2,128)(2,1)S(1)}, u32[]{:S(2)}, u32[]{:S(2)}) async-start(bf16[32,2,1280]{2,1,0:T(2,128)(2,1)} %reshape.331), calls=%async_computation.4 | async-start | bytes 327680 | tf_op jit(solution)/shard_map/all_to_all | solution.py:246
Sparse Core Ops, SparseCore 0:
  29.6 59.8 all-gather.3
